TPU v7x, 512 devices: a whole 4x8x8 slice. The times are simulated.
512 devices in a mesh: section: 8 (over z), ctx: 64 (over x, y, core).
Axes of the slice: x: 4, y: 8, z: 8, core: 2. Of those that a mesh axis runs over, the one named last changes fastest.
Arguments:
- earlier_span: bfloat16 [8, 8192, 4096], P('section', 'ctx'), may hold values from -6 to 6
- span_inputs: bfloat16 [8, 8192, 4096], P('section', 'ctx'), may hold values from -24 to 24
- next_inputs: bfloat16 [8192, 4096], P('ctx'), may hold values from -24 to 24
- block_list: int32 [64, 4], replicated, may hold values from -1 to 127, as said below
- q_gain: float32 [8, 4096], P('section'), may hold values from 0.5 to 8
- k_gain: float32 [8, 4096], P('section'), may hold values from -8 to 8
- out_gain: float32 [8, 4096], P('section'), may hold values from 0.5 to 2
Outputs:
- second_out: bfloat16 [8, 8192, 4096], P('section', 'ctx')
Inputs may be any that keep to these rules, and one draw needn't show every extreme that they name: `block_list`: row i names key block 64 + i, then 64 + i - 1, then 1 increasing blocks r from 0 to 61, the same in every row, then the blocks 64 + r in the same order, each replaced by -1 unless it is at least 2 blocks before 64 + i. The last row has no -1.
All inputs are finite; a program needn't handle non-finite values.
Results may differ from a plain program's by a relative error of at most 0.0055.
The roundings to bfloat16 on the way count: a program that leaves them out, or rounds other values in their place, can miss the bound.
Values may be sent and summed in bfloat16 or wider, within the bound.
No kernel may reach another device: no remote copies, remote signals or barrier semaphores. Data moves between devices by JAX's collectives and lax.ppermute only.
A program may use at most 64 MiB of HBM per device.

v0:
```python
import jax
import jax.numpy as jnp
from jax import lax
from jax.sharding import PartitionSpec as P

HEADS = 32
HD = 128
BLOCK = 128
LOCAL = 2
NR = 1
WIDTH = 4096
NSEL = 4


def from_behind(value, axis, steps):
    count = lax.axis_size(axis)
    pairs = [(source, (source + steps) % count) for source in range(count)]
    return lax.ppermute(value, axis, pairs)


def broadcast(value, axis, source):
    kept = jnp.where(lax.axis_index(axis) == source, value, 0).astype(value.dtype)
    return lax.psum(kept, axis)


def passed_along(value, axis, steps):
    count = lax.axis_size(axis)
    initial, last = (max(0, -steps), min(count, count - steps))
    return lax.ppermute(value, axis, [(source, source + steps) for source in range(initial, last)])


def normalize(rows):
    widened = rows.astype(jnp.float32).reshape(rows.shape[0], HEADS, HD)
    return widened * lax.rsqrt(jnp.mean(widened * widened, axis=-1, keepdims=True) + 1e-06)


def attend_block(query_rows, key_rows, entries, global_block, gain_query, gain_key, gain_out):
    key_flat = key_rows.reshape(NSEL * BLOCK, WIDTH)
    queries = (normalize(query_rows) * gain_query.reshape(HEADS, HD) * HD ** (-0.5)).astype(
        jnp.bfloat16
    )
    keys = (normalize(key_flat) * gain_key.reshape(HEADS, HD)).astype(jnp.bfloat16)
    values = key_flat.reshape(NSEL * BLOCK, HEADS, HD)
    key_entry = jnp.repeat(entries, BLOCK)
    key_pos = jnp.arange(NSEL * BLOCK, dtype=jnp.int32) % BLOCK
    query_pos = jnp.arange(BLOCK, dtype=jnp.int32)
    allowed = (key_entry >= 0)[None, :] & (
        (key_entry != global_block)[None, :] | (key_pos[None, :] <= query_pos[:, None])
    )
    scores = jnp.einsum("qhd,khd->hqk", queries, keys, preferred_element_type=jnp.float32)
    scores = jnp.where(allowed[None], scores, -jnp.inf)
    maxima = jnp.max(scores, axis=-1, keepdims=True)
    raw = jnp.exp(scores - maxima)
    totals = jnp.sum(raw, axis=-1)
    weights = raw.astype(jnp.bfloat16)
    context = jnp.einsum("hqk,khd->qhd", weights, values, preferred_element_type=jnp.float32)
    contexts = (context / jnp.transpose(totals)[:, :, None]).reshape(BLOCK, WIDTH)
    return (query_rows.astype(jnp.float32) + gain_out * contexts).astype(jnp.bfloat16)


def local(earlier_span, span_inputs, next_inputs, block_list, q_gain, k_gain, out_gain):
    group_size = lax.axis_size("ctx")
    position = lax.axis_index("ctx")
    section_pos = lax.axis_index("section")
    query_entries = lax.dynamic_index_in_dim(block_list, position, 0, keepdims=False)
    full_entries = block_list[group_size - 1]
    global_block = group_size + position
    gain_query = q_gain[0]
    gain_key = k_gain[0]
    gain_out = out_gain[0]

    def previous(earlier_rows, current_rows):
        payload = jnp.where(position == group_size - 1, earlier_rows, current_rows)
        return from_behind(payload, "ctx", 1)

    def strided(earlier_rows, current_rows, block_entry):
        payload = jnp.where(block_entry < group_size, earlier_rows, current_rows)
        return broadcast(payload, "ctx", block_entry % group_size)

    first_earlier = earlier_span[0]
    first_current = span_inputs[0]
    fetched_one = [
        strided(first_earlier, first_current, full_entries[LOCAL + slot]) for slot in range(2 * NR)
    ]
    key_one = jnp.stack([first_current, previous(first_earlier, first_current)] + fetched_one)
    first_result = attend_block(
        first_current, key_one, query_entries, global_block, gain_query, gain_key, gain_out
    )
    received = passed_along(first_result, "section", 1)
    second_current = jnp.where(section_pos == 0, next_inputs, received)
    fetched_two = [
        strided(first_current, second_current, full_entries[LOCAL + slot]) for slot in range(2 * NR)
    ]
    key_two = jnp.stack([second_current, previous(first_current, second_current)] + fetched_two)
    second_result = attend_block(
        second_current, key_two, query_entries, global_block, gain_query, gain_key, gain_out
    )
    return second_result[None]


def solution(mesh):
    in_specs = (
        P("section", "ctx", None),
        P("section", "ctx", None),
        P("ctx", None),
        P(),
        P("section", None),
        P("section", None),
        P("section", None),
    )
    out_specs = P("section", "ctx", None)
    return jax.shard_map(local, mesh=mesh, in_specs=in_specs, out_specs=out_specs, check_vma=False)
```

profile of v0, /device:TPU:25, one launch (start us, length us, event | category | flops | bytes accessed | tf_op | source)
XLA Modules:
  0.0 521.9 jit_solution(1600502842453796869)
XLA Ops:
  6.5 1.5 fusion.51
  13.4 3.4 bitcast_select_fusion.2
  16.8 5.0 collective-permute-start
  22.7 0.6 multiply_reduce_fusion.1
  23.5 0.9 multiply_convert_fusion.1
  24.4 201.6 %all-reduce.7.cloned.1.call-done = (bf16[1,128,4096]{2,1,0:T(8,128)(2,1)}, bf16[1,128,4096]{2,1,0:T(8,128)(2,1)}) async-done(((bf16[1,128,4096]{2,1,0:T(8,128)(2,1)}, bf16[1,128,4096]{2,1,0:T(8,128)(2,1)}), (bf16[1,128,4096]{2,1,0:T(8,128)(2,1)}, bf16[1,128,4096]{2,1,0:T(8,128)(2,1)})) %all-reduce.7.cloned.1.call-update) | async-done | bytes 2097168 | tf_op jit(solution)/shard_map/psum | solution.py:23
  225.9 2.1 pad_maximum_fusion
  228.1 3.2 copy.28
  231.3 7.6 %copy.26 = bf16[512,32,128]{0,2,1:T(8,128)(2,1)} copy(bf16[512,32,128]{2,1,0:T(8,128)(2,1)} %bitcast.79) | data formatting | bytes 8388608 | tf_op jit(solution)/shard_map/reshape;reshape | solution.py:43
  238.8 3.3 fusion
  242.3 2.7 select_reduce_fusion.1
  245.0 2.2 fusion.6
  247.2 3.3 bitcast_divide_fusion.1
  250.6 1.9 copy.19
  252.5 1.2 add_convert_fusion
  253.7 3.3 collective-permute-start.1
  257.1 21.0 %collective-permute-done.1 = bf16[128,4096]{1,0:T(8,128)(2,1)S(1)} collective-permute-done((bf16[128,4096]{1,0:T(8,128)(2,1)}, bf16[128,4096]{1,0:T(8,128)(2,1)S(1)}, u32[]{:S(2)}, u32[]{:S(2)}) %collective-permute-start.1) | collective-permute-done | bytes 1048608 | tf_op jit(solution)/shard_map/ppermute | solution.py:29
  278.1 2.8 convert_bitcast_fusion
  280.9 1.5 bitcast_select_fusion.5
  282.4 3.9 collective-permute-start.2
  286.4 2.0 copy.31
  289.0 0.9 multiply_convert_fusion
  289.9 194.9 %all-reduce.5.cloned.1.call-done = (bf16[1,128,4096]{2,1,0:T(8,128)(2,1)}, bf16[1,128,4096]{2,1,0:T(8,128)(2,1)}) async-done(((bf16[1,128,4096]{2,1,0:T(8,128)(2,1)}, bf16[1,128,4096]{2,1,0:T(8,128)(2,1)}), (bf16[1,128,4096]{2,1,0:T(8,128)(2,1)}, bf16[1,128,4096]{2,1,0:T(8,128)(2,1)})) %all-reduce.5.cloned.1.call-update) | async-done | bytes 2097168 | tf_op jit(solution)/shard_map/psum | solution.py:23
  484.8 2.1 pad_maximum_fusion.1
  486.9 3.2 copy.30
  490.1 7.6 %copy.27 = bf16[512,32,128]{0,2,1:T(8,128)(2,1)} copy(bf16[512,32,128]{2,1,0:T(8,128)(2,1)} %bitcast.80) | data formatting | bytes 8388608 | tf_op jit(solution)/shard_map/reshape;reshape | solution.py:43
  497.7 3.3 fusion.3
  501.1 2.7 select_reduce_fusion
  503.8 2.2 fusion.8
  506.0 3.3 bitcast_divide_fusion
  509.4 2.9 copy.23
  512.2 2.8 fusion.33
  (31 shorter events, 2.0 us)
Async XLA Ops:
  6.5 15.3 %copy-start = (bf16[1,128,4096]{2,1,0:T(8,128)(2,1)S(1)}, bf16[1,128,4096]{2,1,0:T(8,128)(2,1)}, u32[]{:S(2)}) copy-start(bf16[1,128,4096]{2,1,0:T(8,128)(2,1)} %param.8) | copy-start | bytes 3145732
  6.5 219.4 %all-reduce.7.cloned.1.call-start = ((), (), s32[]{:S(2)}) async-start(), calls=%async_computation.1 | async-start | bytes 4194304 | tf_op jit(solution)/shard_map/psum | solution.py:23
  13.4 8.7 %copy-start.5 = (s32[64,4]{0,1:T(4,128)S(1)}, s32[64,4]{0,1:T(4,128)}, u32[]{:S(2)}) copy-start(s32[64,4]{0,1:T(4,128)} %param.10) | copy-start | bytes 3076
  16.8 209.1 %collective-permute-start = (bf16[128,4096]{1,0:T(8,128)(2,1)}, bf16[128,4096]{1,0:T(8,128)(2,1)}, u32[]{:S(2)}, u32[]{:S(2)}) collective-permute-start(bf16[128,4096]{1,0:T(8,128)(2,1)} %get-tuple-element.16), channel_id=1, source_target_pairs={{0,1},{1,2},{2,3},{3,4},{4,5},{5,6},{6,7},{7,8},{8,9},{9,10},{10,1... | collective-permute-start | bytes 3145736 | tf_op jit(solution)/shard_map/ppermute | solution.py:18
  21.8 463.0 %all-reduce.5.cloned.1.call-start = ((), (), s32[]{:S(2)}) async-start(), calls=%async_computation | async-start | bytes 4194304 | tf_op jit(solution)/shard_map/psum | solution.py:23
  21.9 1.6 copy-start.3
  238.8 3.4 copy-start.2
  238.8 3.4 copy-start.6
  250.6 1.9 copy-start.4
  253.7 24.4 %collective-permute-start.1 = (bf16[128,4096]{1,0:T(8,128)(2,1)}, bf16[128,4096]{1,0:T(8,128)(2,1)S(1)}, u32[]{:S(2)}, u32[]{:S(2)}) collective-permute-start(bf16[128,4096]{1,0:T(8,128)(2,1)} %add_convert_fusion), channel_id=1, source_target_pairs={{0,64},{64,128},{128,192},{192,256},{256,320},{320,384},{384,448},... | collective-permute-start | bytes 3145736 | tf_op jit(solution)/shard_map/ppermute | solution.py:29
  282.4 202.3 %collective-permute-start.2 = (bf16[128,4096]{1,0:T(8,128)(2,1)S(1)}, bf16[128,4096]{1,0:T(8,128)(2,1)}, u32[]{:S(2)}, u32[]{:S(2)}) collective-permute-start(bf16[128,4096]{1,0:T(8,128)(2,1)S(1)} %get-tuple-element.13), channel_id=1, source_target_pairs={{0,1},{1,2},{2,3},{3,4},{4,5},{5,6},{6,7},{7,8},{8,9},{9,10},{10,1... | collective-permute-start | bytes 3145736 | tf_op jit(solution)/shard_map/ppermute | solution.py:18
  497.7 3.4 copy-start.1
Sparse Core Ops, SparseCore 0:
  21.9 203.9 all-reduce.6
  282.6 202.1 all-reduce.4
where the time goes:
time: 523 us; the launch traced here: 522 us
  waiting for transfers between devices  418 us (80%)
  local copies, waits for them, and re-layouts  30.5 us (6%)
  other arithmetic  30.5 us (6%)
  between operations  19 us (4%)
  starting transfers between devices  12.3 us (2%)
  matrix products  12 us (2%)
    psum x2, waiting for transfers between devices, broadcast(): return lax.psum(kept, axis)  396 us
    ppermute x1, waiting for transfers between devices, passed_along(): lax.ppermute(value, axis, [(source, source + steps) for source in range(i...  21 us
    another operation x2, local copies, waits for them, and re-layouts, attend_block(): values = key_flat.reshape(NSEL * BLOCK, HEADS, HD)  15.1 us
  transfers between devices with their start and end apart: 5, of which 3 were waited for; matrix products, arithmetic and copies ran while one was open for 1% of the time, Pallas kernels for 0%

commit v1 on v0

--- a/solution.py
+++ b/solution.py
@@ -12,21 +12,20 @@
 NSEL = 4
 
 
-def from_behind(value, axis, steps):
+def shifted(value, axis, steps):
     count = lax.axis_size(axis)
     pairs = [(source, (source + steps) % count) for source in range(count)]
     return lax.ppermute(value, axis, pairs)
 
 
-def broadcast(value, axis, source):
-    kept = jnp.where(lax.axis_index(axis) == source, value, 0).astype(value.dtype)
-    return lax.psum(kept, axis)
-
-
-def passed_along(value, axis, steps):
+def spread(payload, axis, root):
     count = lax.axis_size(axis)
-    initial, last = (max(0, -steps), min(count, count - steps))
-    return lax.ppermute(value, axis, [(source, source + steps) for source in range(initial, last)])
+    rows = payload.shape[0]
+    pieces = payload.reshape(count, rows // count, payload.shape[1])
+    received = lax.all_to_all(pieces, axis, 0, 0, tiled=True)
+    mine = lax.dynamic_index_in_dim(received, root, 0, keepdims=True)
+    gathered = lax.all_to_all(jnp.broadcast_to(mine, pieces.shape), axis, 0, 0, tiled=True)
+    return gathered.reshape(payload.shape)
 
 
 def normalize(rows):
@@ -60,6 +59,7 @@
 
 def local(earlier_span, span_inputs, next_inputs, block_list, q_gain, k_gain, out_gain):
     group_size = lax.axis_size("ctx")
+    sections = lax.axis_size("section")
     position = lax.axis_index("ctx")
     section_pos = lax.axis_index("section")
     query_entries = lax.dynamic_index_in_dim(block_list, position, 0, keepdims=False)
@@ -68,30 +68,43 @@
     gain_query = q_gain[0]
     gain_key = k_gain[0]
     gain_out = out_gain[0]
-
-    def previous(earlier_rows, current_rows):
-        payload = jnp.where(position == group_size - 1, earlier_rows, current_rows)
-        return from_behind(payload, "ctx", 1)
-
-    def strided(earlier_rows, current_rows, block_entry):
-        payload = jnp.where(block_entry < group_size, earlier_rows, current_rows)
-        return broadcast(payload, "ctx", block_entry % group_size)
+    last = position == group_size - 1
 
     first_earlier = earlier_span[0]
     first_current = span_inputs[0]
-    fetched_one = [
-        strided(first_earlier, first_current, full_entries[LOCAL + slot]) for slot in range(2 * NR)
-    ]
-    key_one = jnp.stack([first_current, previous(first_earlier, first_current)] + fetched_one)
+    root = full_entries[LOCAL] % group_size
+    both = spread(jnp.concatenate([first_earlier, first_current]), "ctx", root)
+    strided_earlier, strided_current = both[:BLOCK], both[BLOCK:]
+
+    early = shifted(
+        jnp.concatenate(
+            [jnp.where(last, first_earlier, first_current), jnp.where(last, first_current, next_inputs)]
+        ),
+        "ctx",
+        1,
+    )
+    previous_one, previous_early = early[:BLOCK], early[BLOCK:]
+
+    key_one = jnp.stack([first_current, previous_one, strided_earlier, strided_current])
     first_result = attend_block(
         first_current, key_one, query_entries, global_block, gain_query, gain_key, gain_out
     )
-    received = passed_along(first_result, "section", 1)
+
+    straight = [(s, s + 1) for s in range(sections - 1)]
+    received = lax.ppermute(first_result, "section", straight)
+    diagonal = [
+        (s * group_size + i, (s + 1) * group_size + i + 1)
+        for s in range(sections - 1)
+        for i in range(group_size - 1)
+    ]
+    received_previous = lax.ppermute(first_result, ("section", "ctx"), diagonal)
     second_current = jnp.where(section_pos == 0, next_inputs, received)
-    fetched_two = [
-        strided(first_current, second_current, full_entries[LOCAL + slot]) for slot in range(2 * NR)
-    ]
-    key_two = jnp.stack([second_current, previous(first_current, second_current)] + fetched_two)
+    previous_two = jnp.where(
+        (position == 0) | (section_pos == 0), previous_early, received_previous
+    )
+    later_root = full_entries[LOCAL + NR] % group_size
+    strided_later = spread(second_current, "ctx", later_root)
+    key_two = jnp.stack([second_current, previous_two, strided_current, strided_later])
     second_result = attend_block(
         second_current, key_two, query_entries, global_block, gain_query, gain_key, gain_out
     )

time: 523 us -> 329 us (0.63)
  the two profiles are of different devices: /device:TPU:25 before, /device:TPU:326 now
where the time goes in v1:
time: 329 us; the launch traced here: 328 us
  waiting for transfers between devices  186 us (57%)
  starting transfers between devices  46.4 us (14%)
  local copies, waits for them, and re-layouts  46.1 us (14%)
  other arithmetic  32.6 us (10%)
  matrix products  12 us (4%)
  between operations  4.53 us (1%)
    all_to_all x2, waiting for transfers between devices, spread(): received = lax.all_to_all(pieces, axis, 0, 0, tiled=True)  70.6 us
    ppermute x1, waiting for transfers between devices, shifted(): return lax.ppermute(value, axis, pairs)  63.8 us
    ppermute x1, waiting for transfers between devices, local(): received_previous = lax.ppermute(first_result, ('section', 'ctx'), diagonal)  31.3 us
    all_to_all x2, starting transfers between devices, spread(): received = lax.all_to_all(pieces, axis, 0, 0, tiled=True)  21.3 us
    ppermute x1, waiting for transfers between devices, local(): received = lax.ppermute(first_result, 'section', straight)  20.6 us
    all_to_all x2, starting transfers between devices, spread(): lax.all_to_all(jnp.broadcast_to(mine, pieces.shape), axis, 0, 0, tiled=True)  16.4 us
    another operation x2, local copies, waits for them, and re-layouts, attend_block(): values = key_flat.reshape(NSEL * BLOCK, HEADS, HD)  15.2 us
    unnamed x28, local copies, waits for them, and re-layouts  9.14 us
  transfers between devices with their start and end apart: 7, of which 5 were waited for; matrix products, arithmetic and copies ran while one was open for 5% of the time, Pallas kernels for 0%

profile of v1, /device:TPU:326, one launch (start us, length us, event | category | flops | bytes accessed | tf_op | source)
XLA Modules:
  0.0 328.0 jit_solution(6633239052549019488)
XLA Ops:
  1.7 2.2 reshape.151
  3.9 11.0 %all-to-all-start = ((bf16[64,4,4096]{2,1,0:T(4,128)(2,1)}), bf16[64,4,4096]{2,1,0:T(4,128)(2,1)}, u32[]{:S(2)}, u32[]{:S(2)}) async-start(bf16[64,4,4096]{2,1,0:T(4,128)(2,1)} %reshape.151), calls=%async_computation | async-start | bytes 4194304 | tf_op jit(solution)/shard_map/all_to_all | solution.py:25
  17.8 45.9 %all-to-all-done = bf16[64,4,4096]{2,1,0:T(4,128)(2,1)} async-done(((bf16[64,4,4096]{2,1,0:T(4,128)(2,1)}), bf16[64,4,4096]{2,1,0:T(4,128)(2,1)}, u32[]{:S(2)}, u32[]{:S(2)}) %all-to-all-start) | async-done | bytes 2097184 | tf_op jit(solution)/shard_map/all_to_all | solution.py:25
  64.5 2.3 broadcast_in_dim.31
  66.8 8.3 %all-to-all-start.1 = ((bf16[64,4,4096]{2,1,0:T(4,128)(2,1)}), bf16[64,4,4096]{2,1,0:T(4,128)(2,1)}, u32[]{:S(2)}, u32[]{:S(2)}) async-start(bf16[64,4,4096]{2,1,0:T(4,128)(2,1)} %broadcast_in_dim.31), calls=%async_computation.1 | async-start | bytes 4194304 | tf_op jit(solution)/shard_map/all_to_all | solution.py:27
  76.9 2.2 collective-permute-start
  82.4 63.8 %collective-permute-done = bf16[256,4096]{1,0:T(8,128)(2,1)} collective-permute-done((bf16[256,4096]{1,0:T(8,128)(2,1)}, bf16[256,4096]{1,0:T(8,128)(2,1)}, u32[]{:S(2)}, u32[]{:S(2)}) %collective-permute-start) | collective-permute-done | bytes 2097184 | tf_op jit(solution)/shard_map/ppermute | solution.py:18
  146.2 2.3 slice_bitcast_fusion
  148.5 2.4 fusion.44
  154.2 3.2 copy.28
  157.4 7.6 %copy.26 = bf16[512,32,128]{0,2,1:T(8,128)(2,1)} copy(bf16[512,32,128]{2,1,0:T(8,128)(2,1)} %bitcast.56) | data formatting | bytes 8388608 | tf_op jit(solution)/shard_map/reshape;reshape | solution.py:42
  165.0 3.3 fusion
  168.5 2.7 select_reduce_fusion.1
  171.2 2.2 fusion.6
  173.4 3.3 %bitcast_divide_fusion.1 = f32[128,32,128]{0,2,1:T(8,128)} fusion(bf16[512,32,128]{0,2,1:T(8,128)(2,1)S(1)} %copy-done.2, f32[32,128,512]{2,1,0:T(8,128)S(1)} %get-tuple-element.16, f32[32,128]{1,0:T(8,128)S(1)} %get-tuple-element.15, pred[128,512]{1,0:T(8,128)(4,1)S(1)} %fusion.38, f32[128,32]{0,1:T(8,128)S(1)} %bitcast.67), kind=kOutput, calls=%fused_computation.40 | convolution fusion | flops 543686656 | bytes 14778368 | tf_op jit(solution)/shard_map/hqk,khd->qhd/dot_general | solution.py:55
  176.8 3.0 copy.19
  179.8 2.8 add_convert_fusion
  182.6 3.4 %collective-permute-start.1 = (bf16[128,4096]{1,0:T(8,128)(2,1)}, bf16[128,4096]{1,0:T(8,128)(2,1)}, u32[]{:S(2)}, u32[]{:S(2)}) collective-permute-start(bf16[128,4096]{1,0:T(8,128)(2,1)} %add_convert_fusion), channel_id=1, source_target_pairs={{0,64},{64,128},{128,192},{192,256},{256,320},{320,384},{384,448},... | collective-permute-start | bytes 3145736 | tf_op jit(solution)/shard_map/ppermute | solution.py:94
  185.9 20.6 %collective-permute-done.1 = bf16[128,4096]{1,0:T(8,128)(2,1)} collective-permute-done((bf16[128,4096]{1,0:T(8,128)(2,1)}, bf16[128,4096]{1,0:T(8,128)(2,1)}, u32[]{:S(2)}, u32[]{:S(2)}) %collective-permute-start.1) | collective-permute-done | bytes 1048608 | tf_op jit(solution)/shard_map/ppermute | solution.py:94
  206.5 2.8 convert_bitcast_fusion
  210.8 10.3 %all-to-all-start.2 = ((bf16[64,2,4096]{2,1,0:T(2,128)(2,1)}), bf16[64,2,4096]{2,1,0:T(2,128)(2,1)S(1)}, u32[]{:S(2)}, u32[]{:S(2)}) async-start(bf16[64,2,4096]{2,1,0:T(2,128)(2,1)} %reshape.153), calls=%async_computation.2 | async-start | bytes 2097152 | tf_op jit(solution)/shard_map/all_to_all | solution.py:25
  223.1 24.7 %all-to-all-done.2 = bf16[64,2,4096]{2,1,0:T(2,128)(2,1)S(1)} async-done(((bf16[64,2,4096]{2,1,0:T(2,128)(2,1)}), bf16[64,2,4096]{2,1,0:T(2,128)(2,1)S(1)}, u32[]{:S(2)}, u32[]{:S(2)}) %all-to-all-start.2) | async-done | bytes 1048608 | tf_op jit(solution)/shard_map/all_to_all | solution.py:25
  249.8 8.1 %all-to-all-start.3 = ((bf16[64,2,4096]{2,1,0:T(2,128)(2,1)}), bf16[64,2,4096]{2,1,0:T(2,128)(2,1)S(1)}, u32[]{:S(2)}, u32[]{:S(2)}) async-start(bf16[64,2,4096]{2,1,0:T(2,128)(2,1)} %broadcast_in_dim.64), calls=%async_computation.3 | async-start | bytes 2097152 | tf_op jit(solution)/shard_map/all_to_all | solution.py:27
  257.9 3.1 collective-permute-start.2
  265.3 31.3 %collective-permute-done.2 = bf16[128,4096]{1,0:T(8,128)(2,1)} collective-permute-done((bf16[128,4096]{1,0:T(8,128)(2,1)}, bf16[128,4096]{1,0:T(8,128)(2,1)}, u32[]{:S(2)}, u32[]{:S(2)}) %collective-permute-start.2) | collective-permute-done | bytes 1048608 | tf_op jit(solution)/shard_map/ppermute | solution.py:100
  296.7 2.6 fusion.34
  302.3 3.2 copy.30
  305.5 7.6 %copy.27 = bf16[512,32,128]{0,2,1:T(8,128)(2,1)} copy(bf16[512,32,128]{2,1,0:T(8,128)(2,1)} %bitcast.57) | data formatting | bytes 8388608 | tf_op jit(solution)/shard_map/reshape;reshape | solution.py:42
  313.1 3.3 fusion.3
  316.6 2.7 select_reduce_fusion
  319.3 2.2 fusion.8
  321.5 3.3 %bitcast_divide_fusion = f32[128,32,128]{0,2,1:T(8,128)} fusion(bf16[512,32,128]{0,2,1:T(8,128)(2,1)S(1)} %copy-done.1, f32[32,128,512]{2,1,0:T(8,128)S(1)} %get-tuple-element.18, f32[32,128]{1,0:T(8,128)S(1)} %get-tuple-element.17, pred[128,512]{1,0:T(8,128)(4,1)S(1)} %fusion.38, f32[128,32]{0,1:T(8,128)S(1)} %bitcast.66), kind=kOutput, calls=%fused_computation.39 | convolution fusion | flops 543686656 | bytes 14778368 | tf_op jit(solution)/shard_map/hqk,khd->qhd/dot_general | solution.py:55
  (56 shorter events, 25.5 us)
Async XLA Ops:
  1.7 13.3 %copy-start.10 = (s32[64,4]{0,1:T(4,128)S(1)}, s32[64,4]{0,1:T(4,128)}, u32[]{:S(2)}) copy-start(s32[64,4]{0,1:T(4,128)} %param.10) | copy-start | bytes 3076
  3.9 59.8 %all-to-all-start = ((bf16[64,4,4096]{2,1,0:T(4,128)(2,1)}), bf16[64,4,4096]{2,1,0:T(4,128)(2,1)}, u32[]{:S(2)}, u32[]{:S(2)}) async-start(bf16[64,4,4096]{2,1,0:T(4,128)(2,1)} %reshape.151), calls=%async_computation | async-start | bytes 4194304 | tf_op jit(solution)/shard_map/all_to_all | solution.py:25
  14.9 60.2 %copy-start = (bf16[1,128,4096]{2,1,0:T(8,128)(2,1)S(1)}, bf16[1,128,4096]{2,1,0:T(8,128)(2,1)}, u32[]{:S(2)}) copy-start(bf16[1,128,4096]{2,1,0:T(8,128)(2,1)} %param.8) | copy-start | bytes 3145732
  14.9 60.2 %copy-start.3 = (bf16[1,128,4096]{2,1,0:T(8,128)(2,1)S(1)}, bf16[1,128,4096]{2,1,0:T(8,128)(2,1)}, u32[]{:S(2)}) copy-start(bf16[1,128,4096]{2,1,0:T(8,128)(2,1)} %param.7) | copy-start | bytes 3145732
  14.9 60.2 %copy-start.4 = (bf16[128,4096]{1,0:T(8,128)(2,1)S(1)}, bf16[128,4096]{1,0:T(8,128)(2,1)}, u32[]{:S(2)}) copy-start(bf16[128,4096]{1,0:T(8,128)(2,1)} %param.9) | copy-start | bytes 3145732
  66.8 81.7 %all-to-all-start.1 = ((bf16[64,4,4096]{2,1,0:T(4,128)(2,1)}), bf16[64,4,4096]{2,1,0:T(4,128)(2,1)}, u32[]{:S(2)}, u32[]{:S(2)}) async-start(bf16[64,4,4096]{2,1,0:T(4,128)(2,1)} %broadcast_in_dim.31), calls=%async_computation.1 | async-start | bytes 4194304 | tf_op jit(solution)/shard_map/all_to_all | solution.py:27
  76.9 69.3 %collective-permute-start = (bf16[256,4096]{1,0:T(8,128)(2,1)}, bf16[256,4096]{1,0:T(8,128)(2,1)}, u32[]{:S(2)}, u32[]{:S(2)}) collective-permute-start(bf16[256,4096]{1,0:T(8,128)(2,1)} %pad_maximum_fusion.2), channel_id=1, source_target_pairs={{0,1},{1,2},{2,3},{3,4},{4,5},{5,6},{6,7},{7,8},{8,9},{9,10},{10,1... | collective-permute-start | bytes 6291464 | tf_op jit(solution)/shard_map/ppermute | solution.py:18
  79.1 1.6 copy-start.8
  157.4 10.9 %copy-start.6 = (bf16[128,32,128]{2,1,0:T(8,128)(2,1)S(1)}, bf16[128,32,128]{2,1,0:T(8,128)(2,1)}, u32[]{:S(2)}) copy-start(bf16[128,32,128]{2,1,0:T(8,128)(2,1)} %multiply_convert_fusion.1) | copy-start | bytes 3145732
  165.0 3.4 %copy-start.2 = (bf16[512,32,128]{0,2,1:T(8,128)(2,1)S(1)}, bf16[512,32,128]{0,2,1:T(8,128)(2,1)}, u32[]{:S(2)}) copy-start(bf16[512,32,128]{0,2,1:T(8,128)(2,1)} %copy.26) | copy-start | bytes 12582916
  165.0 3.4 %copy-start.11 = (f32[1,4096]{1,0:T(1,128)S(1)}, f32[1,4096]{1,0:T(1,128)}, u32[]{:S(2)}) copy-start(f32[1,4096]{1,0:T(1,128)} %param.12) | copy-start | bytes 49156
  176.8 3.0 copy-start.9
  176.8 29.8 %copy-start.5 = (bf16[128,4096]{1,0:T(8,128)(2,1)S(1)}, bf16[128,4096]{1,0:T(8,128)(2,1)}, u32[]{:S(2)}) copy-start(bf16[128,4096]{1,0:T(8,128)(2,1)} %param.9) | copy-start | bytes 3145732
  182.6 24.0 %collective-permute-start.1 = (bf16[128,4096]{1,0:T(8,128)(2,1)}, bf16[128,4096]{1,0:T(8,128)(2,1)}, u32[]{:S(2)}, u32[]{:S(2)}) collective-permute-start(bf16[128,4096]{1,0:T(8,128)(2,1)} %add_convert_fusion), channel_id=1, source_target_pairs={{0,64},{64,128},{128,192},{192,256},{256,320},{320,384},{384,448},... | collective-permute-start | bytes 3145736 | tf_op jit(solution)/shard_map/ppermute | solution.py:94
  210.8 37.0 %all-to-all-start.2 = ((bf16[64,2,4096]{2,1,0:T(2,128)(2,1)}), bf16[64,2,4096]{2,1,0:T(2,128)(2,1)S(1)}, u32[]{:S(2)}, u32[]{:S(2)}) async-start(bf16[64,2,4096]{2,1,0:T(2,128)(2,1)} %reshape.153), calls=%async_computation.2 | async-start | bytes 2097152 | tf_op jit(solution)/shard_map/all_to_all | solution.py:25
  249.8 49.5 %all-to-all-start.3 = ((bf16[64,2,4096]{2,1,0:T(2,128)(2,1)}), bf16[64,2,4096]{2,1,0:T(2,128)(2,1)S(1)}, u32[]{:S(2)}, u32[]{:S(2)}) async-start(bf16[64,2,4096]{2,1,0:T(2,128)(2,1)} %broadcast_in_dim.64), calls=%async_computation.3 | async-start | bytes 2097152 | tf_op jit(solution)/shard_map/all_to_all | solution.py:27
  257.9 38.8 %collective-permute-start.2 = (bf16[128,4096]{1,0:T(8,128)(2,1)}, bf16[128,4096]{1,0:T(8,128)(2,1)}, u32[]{:S(2)}, u32[]{:S(2)}) collective-permute-start(bf16[128,4096]{1,0:T(8,128)(2,1)} %add_convert_fusion), channel_id=1, source_target_pairs={{0,65},{1,66},{2,67},{3,68},{4,69},{5,70},{6,71},{7,72},{8,73},{9,... | collective-permute-start | bytes 3145736 | tf_op jit(solution)/shard_map/ppermute | solution.py:100
  305.5 10.9 %copy-start.7 = (bf16[128,32,128]{2,1,0:T(8,128)(2,1)S(1)}, bf16[128,32,128]{2,1,0:T(8,128)(2,1)}, u32[]{:S(2)}) copy-start(bf16[128,32,128]{2,1,0:T(8,128)(2,1)} %multiply_convert_fusion) | copy-start | bytes 3145732
  313.1 3.4 %copy-start.1 = (bf16[512,32,128]{0,2,1:T(8,128)(2,1)S(1)}, bf16[512,32,128]{0,2,1:T(8,128)(2,1)}, u32[]{:S(2)}) copy-start(bf16[512,32,128]{0,2,1:T(8,128)(2,1)} %copy.27) | copy-start | bytes 12582916

commit v2 on v1

--- a/solution.py
+++ b/solution.py
@@ -2,6 +2,9 @@
 import jax.numpy as jnp
 from jax import lax
 from jax.sharding import PartitionSpec as P
+from jax.experimental import pallas as pl
+from jax.experimental.pallas import tpu as pltpu
+import functools
 
 HEADS = 32
 HD = 128
@@ -10,6 +13,7 @@
 NR = 1
 WIDTH = 4096
 NSEL = 4
+GROUP = 4
 
 
 def shifted(value, axis, steps):
@@ -28,33 +32,53 @@
     return gathered.reshape(payload.shape)
 
 
-def normalize(rows):
-    widened = rows.astype(jnp.float32).reshape(rows.shape[0], HEADS, HD)
-    return widened * lax.rsqrt(jnp.mean(widened * widened, axis=-1, keepdims=True) + 1e-06)
+def attend_kernel(meta_ref, q_ref, k0_ref, k1_ref, k2_ref, k3_ref, gq_ref, gk_ref, go_ref, out_ref):
+    key_refs = (k0_ref, k1_ref, k2_ref, k3_ref)
+    global_block = meta_ref[NSEL]
+    query_pos = lax.broadcasted_iota(jnp.int32, (BLOCK, BLOCK), 0)
+    key_pos = lax.broadcasted_iota(jnp.int32, (BLOCK, BLOCK), 1)
+    allowed = []
+    for b in range(NSEL):
+        entry = meta_ref[b]
+        allowed.append((entry >= 0) & ((entry != global_block) | (key_pos <= query_pos)))
+    for h in range(GROUP):
+        lanes = slice(h * HD, (h + 1) * HD)
+        rows = q_ref[:, lanes].astype(jnp.float32)
+        normed = rows * lax.rsqrt(jnp.mean(rows * rows, axis=-1, keepdims=True) + 1e-06)
+        queries = (normed * gq_ref[:, lanes] * HD ** (-0.5)).astype(jnp.bfloat16)
+        scores = []
+        for b in range(NSEL):
+            raw_keys = key_refs[b][:, lanes]
+            wide = raw_keys.astype(jnp.float32)
+            keys = (wide * lax.rsqrt(jnp.mean(wide * wide, axis=-1, keepdims=True) + 1e-06) * gk_ref[:, lanes]).astype(jnp.bfloat16)
+            s = lax.dot_general(queries, keys, (((1,), (1,)), ((), ())), preferred_element_type=jnp.float32)
+            scores.append(jnp.where(allowed[b], s, -jnp.inf))
+        maxima = functools.reduce(jnp.maximum, [jnp.max(s, axis=-1, keepdims=True) for s in scores])
+        raws = [jnp.exp(s - maxima) for s in scores]
+        totals = functools.reduce(jnp.add, [jnp.sum(r, axis=-1, keepdims=True) for r in raws])
+        context = None
+        for b in range(NSEL):
+            part = jnp.dot(raws[b].astype(jnp.bfloat16), key_refs[b][:, lanes], preferred_element_type=jnp.float32)
+            context = part if context is None else context + part
+        out_ref[:, lanes] = (rows + go_ref[:, lanes] * (context / totals)).astype(jnp.bfloat16)
 
 
-def attend_block(query_rows, key_rows, entries, global_block, gain_query, gain_key, gain_out):
-    key_flat = key_rows.reshape(NSEL * BLOCK, WIDTH)
-    queries = (normalize(query_rows) * gain_query.reshape(HEADS, HD) * HD ** (-0.5)).astype(
-        jnp.bfloat16
+def attend_pallas(query_rows, key_blocks, entries, global_block, gain_query, gain_key, gain_out):
+    meta = jnp.concatenate([entries.astype(jnp.int32), jnp.reshape(global_block, (1,)).astype(jnp.int32)])
+    lanes = GROUP * HD
+    row_spec = pl.BlockSpec((BLOCK, lanes), lambda g, meta: (0, g))
+    gain_spec = pl.BlockSpec((1, lanes), lambda g, meta: (0, g))
+    grid_spec = pltpu.PrefetchScalarGridSpec(
+        num_scalar_prefetch=1,
+        grid=(HEADS // GROUP,),
+        in_specs=[row_spec] * (1 + NSEL) + [gain_spec] * 3,
+        out_specs=row_spec,
     )
-    keys = (normalize(key_flat) * gain_key.reshape(HEADS, HD)).astype(jnp.bfloat16)
-    values = key_flat.reshape(NSEL * BLOCK, HEADS, HD)
-    key_entry = jnp.repeat(entries, BLOCK)
-    key_pos = jnp.arange(NSEL * BLOCK, dtype=jnp.int32) % BLOCK
-    query_pos = jnp.arange(BLOCK, dtype=jnp.int32)
-    allowed = (key_entry >= 0)[None, :] & (
-        (key_entry != global_block)[None, :] | (key_pos[None, :] <= query_pos[:, None])
-    )
-    scores = jnp.einsum("qhd,khd->hqk", queries, keys, preferred_element_type=jnp.float32)
-    scores = jnp.where(allowed[None], scores, -jnp.inf)
-    maxima = jnp.max(scores, axis=-1, keepdims=True)
-    raw = jnp.exp(scores - maxima)
-    totals = jnp.sum(raw, axis=-1)
-    weights = raw.astype(jnp.bfloat16)
-    context = jnp.einsum("hqk,khd->qhd", weights, values, preferred_element_type=jnp.float32)
-    contexts = (context / jnp.transpose(totals)[:, :, None]).reshape(BLOCK, WIDTH)
-    return (query_rows.astype(jnp.float32) + gain_out * contexts).astype(jnp.bfloat16)
+    return pl.pallas_call(
+        attend_kernel,
+        grid_spec=grid_spec,
+        out_shape=jax.ShapeDtypeStruct((BLOCK, WIDTH), jnp.bfloat16),
+    )(meta, query_rows, *key_blocks, gain_query.reshape(1, WIDTH), gain_key.reshape(1, WIDTH), gain_out.reshape(1, WIDTH))
 
 
 def local(earlier_span, span_inputs, next_inputs, block_list, q_gain, k_gain, out_gain):
@@ -85,8 +109,8 @@
     )
     previous_one, previous_early = early[:BLOCK], early[BLOCK:]
 
-    key_one = jnp.stack([first_current, previous_one, strided_earlier, strided_current])
-    first_result = attend_block(
+    key_one = (first_current, previous_one, strided_earlier, strided_current)
+    first_result = attend_pallas(
         first_current, key_one, query_entries, global_block, gain_query, gain_key, gain_out
     )
 
@@ -104,8 +128,8 @@
     )
     later_root = full_entries[LOCAL + NR] % group_size
     strided_later = spread(second_current, "ctx", later_root)
-    key_two = jnp.stack([second_current, previous_two, strided_current, strided_later])
-    second_result = attend_block(
+    key_two = (second_current, previous_two, strided_current, strided_later)
+    second_result = attend_pallas(
         second_current, key_two, query_entries, global_block, gain_query, gain_key, gain_out
     )
     return second_result[None]

time: 329 us -> 302 us (0.918)
  Pallas kernels: 0 us -> 33 us
  local copies, waits for them, and re-layouts: 46.1 us -> 17.8 us
  other arithmetic: 32.6 us -> 8.05 us
  matrix products: 12 us -> 0 us
  waiting for transfers between devices: 186 us -> 192 us
    pallas_call x0 -> x2, Pallas kernels: none -> 33 us  [attend_pallas(): pl.pallas_call(attend_kernel, grid_spec=grid_spec, out_shape=jax.ShapeDty...]
    another operation x6 -> x0, local copies, waits for them, and re-layouts: 20.1 us -> none  [the longest x2 15.2 us: attend_block(): values = key_flat.reshape(NSEL * BLOCK, HEADS, HD)]
    reduce_sum x6 -> x0, other arithmetic: 12.2 us -> none  [the longest x4 7.74 us: normalize(): jnp.mean(widened * widened, axis=-1, keepdims=True) + 1e-06]
    dot_general x4 -> x0, matrix products: 12 us -> none  [the longest x2 6.66 us: attend_block(): jnp.einsum('hqk,khd->qhd', weights, values, preferred_element_type=jnp.fl...]
    unnamed x28 -> x10, local copies, waits for them, and re-layouts: 9.14 us -> 0.02 us
    another operation x3 -> x0, other arithmetic: 6.23 us -> none  [the longest x2 4.42 us: local(): jnp.stack([second_current, previous_two, strided_current, strided_later])]
    convert_element_type x3 -> x0, other arithmetic: 6.22 us -> none  [the longest x2 3.41 us: attend_block(): (normalize(query_rows) * gain_query.reshape(HEADS, HD) * HD ** (-0.5)).as...]
    ppermute x1, waiting for transfers between devices: 31.3 us -> 35.5 us  [local(): received_previous = lax.ppermute(first_result, ('section', 'ctx'), diagonal)]
  transfers between devices with their start and end apart: 7 -> 7, of which waited for: 5 -> 5; matrix products, arithmetic and copies ran while one was open for 5% -> 3% of each run, Pallas kernels for 0% -> 0%
where the time goes in v2:
time: 302 us; the launch traced here: 301 us
  waiting for transfers between devices  192 us (64%)
  starting transfers between devices  46.1 us (15%)
  Pallas kernels  33 us (11%)
  local copies, waits for them, and re-layouts  17.8 us (6%)
  other arithmetic  8.05 us (3%)
  between operations  3.94 us (1%)
    all_to_all x2, waiting for transfers between devices, spread(): received = lax.all_to_all(pieces, axis, 0, 0, tiled=True)  71.1 us
    ppermute x1, waiting for transfers between devices, shifted(): return lax.ppermute(value, axis, pairs)  65.1 us
    ppermute x1, waiting for transfers between devices, local(): received_previous = lax.ppermute(first_result, ('section', 'ctx'), diagonal)  35.5 us
    pallas_call x2, Pallas kernels, attend_pallas(): pl.pallas_call(attend_kernel, grid_spec=grid_spec, out_shape=jax.ShapeDty...  33 us
    all_to_all x2, starting transfers between devices, spread(): received = lax.all_to_all(pieces, axis, 0, 0, tiled=True)  21.3 us
    ppermute x1, waiting for transfers between devices, local(): received = lax.ppermute(first_result, 'section', straight)  20.5 us
    all_to_all x2, starting transfers between devices, spread(): lax.all_to_all(jnp.broadcast_to(mine, pieces.shape), axis, 0, 0, tiled=True)  16.4 us
  transfers between devices with their start and end apart: 7, of which 5 were waited for; matrix products, arithmetic and copies ran while one was open for 3% of the time, Pallas kernels for 0%

profile of v2, /device:TPU:326, one launch (start us, length us, event | category | flops | bytes accessed | tf_op | source)
XLA Modules:
  0.0 301.2 jit_solution(2891506059539983249)
XLA Ops:
  0.0 1.7 pad_maximum_fusion.1
  1.7 2.2 reshape.21
  3.9 10.9 %all-to-all-start = ((bf16[64,4,4096]{2,1,0:T(4,128)(2,1)}), bf16[64,4,4096]{2,1,0:T(4,128)(2,1)S(1)}, u32[]{:S(2)}, u32[]{:S(2)}) async-start(bf16[64,4,4096]{2,1,0:T(4,128)(2,1)} %reshape.21), calls=%async_computation | async-start | bytes 4194304 | tf_op jit(solution)/shard_map/all_to_all | solution.py:29
  14.9 0.6 fusion.1
  17.4 46.3 %all-to-all-done = bf16[64,4,4096]{2,1,0:T(4,128)(2,1)S(1)} async-done(((bf16[64,4,4096]{2,1,0:T(4,128)(2,1)}), bf16[64,4,4096]{2,1,0:T(4,128)(2,1)S(1)}, u32[]{:S(2)}, u32[]{:S(2)}) %all-to-all-start) | async-done | bytes 2097184 | tf_op jit(solution)/shard_map/all_to_all | solution.py:29
  63.8 2.3 broadcast_in_dim.18
  66.1 8.3 %all-to-all-start.1 = ((bf16[64,4,4096]{2,1,0:T(4,128)(2,1)}), bf16[64,4,4096]{2,1,0:T(4,128)(2,1)S(1)}, u32[]{:S(2)}, u32[]{:S(2)}) async-start(bf16[64,4,4096]{2,1,0:T(4,128)(2,1)} %broadcast_in_dim.18), calls=%async_computation.1 | async-start | bytes 4194304 | tf_op jit(solution)/shard_map/all_to_all | solution.py:31
  74.4 1.7 broadcast_select_fusion.1
  76.1 1.6 pad_maximum_fusion
  77.7 2.0 collective-permute-start
  79.7 0.2 dynamic-slice_reduce_fusion
  79.9 0.7 pad_add_fusion.meta_ref
  80.6 65.1 %collective-permute-done = bf16[256,4096]{1,0:T(8,128)(2,1)} collective-permute-done((bf16[256,4096]{1,0:T(8,128)(2,1)}, bf16[256,4096]{1,0:T(8,128)(2,1)}, u32[]{:S(2)}, u32[]{:S(2)}) %collective-permute-start) | collective-permute-done | bytes 2097184 | tf_op jit(solution)/shard_map/ppermute | solution.py:22
  145.7 2.3 slice.37.k1_ref
  148.0 0.0 all-to-all-done.1
  148.0 2.2 fusion
  150.2 2.1 slice.34.k3_ref.k2_ref
  152.3 1.1 slice.32.k2_ref
  153.4 16.6 %shard_map.73 = bf16[128,4096]{1,0:T(8,128)(2,1)} custom-call(s32[5]{0:T(128)} %pad_add_fusion.meta_ref, bf16[128,4096]{1,0:T(8,128)(2,1)} %bitcast.14, bf16[128,4096]{1,0:T(8,128)(2,1)} %bitcast.15, bf16[128,4096]{1,0:T(8,128)(2,1)} %slice.37.k1_ref, bf16[128,4096]{1,0:T(8,128)(2,1)} %slice.32.k2_ref, bf16[128,4096]{1,0:T(8,128)(2,1)} %slice.34.k3_ref.k2_ref, ...), custom_call_target="tpu_custom_call" | custom-call | tf_op jit(solution)/shard_map/pallas_call | solution.py:77
  170.0 3.4 %collective-permute-start.1 = (bf16[128,4096]{1,0:T(8,128)(2,1)}, bf16[128,4096]{1,0:T(8,128)(2,1)S(1)}, u32[]{:S(2)}, u32[]{:S(2)}) collective-permute-start(bf16[128,4096]{1,0:T(8,128)(2,1)} %shard_map.73), channel_id=1, source_target_pairs={{0,64},{64,128},{128,192},{192,256},{256,320},{320,384},{384,448},... | collective-permute-start | bytes 3145736 | tf_op jit(solution)/shard_map/ppermute | solution.py:118
  173.4 20.5 %collective-permute-done.1 = bf16[128,4096]{1,0:T(8,128)(2,1)S(1)} collective-permute-done((bf16[128,4096]{1,0:T(8,128)(2,1)}, bf16[128,4096]{1,0:T(8,128)(2,1)S(1)}, u32[]{:S(2)}, u32[]{:S(2)}) %collective-permute-start.1) | collective-permute-done | bytes 1048608 | tf_op jit(solution)/shard_map/ppermute | solution.py:118
  193.9 0.1 broadcast_select_fusion.2.q_ref.k0_ref
  194.0 1.5 reshape.22
  195.5 10.3 %all-to-all-start.2 = ((bf16[64,2,4096]{2,1,0:T(2,128)(2,1)}), bf16[64,2,4096]{2,1,0:T(2,128)(2,1)S(1)}, u32[]{:S(2)}, u32[]{:S(2)}) async-start(bf16[64,2,4096]{2,1,0:T(2,128)(2,1)} %reshape.22), calls=%async_computation.2 | async-start | bytes 2097152 | tf_op jit(solution)/shard_map/all_to_all | solution.py:29
  207.7 24.8 %all-to-all-done.2 = bf16[64,2,4096]{2,1,0:T(2,128)(2,1)S(1)} async-done(((bf16[64,2,4096]{2,1,0:T(2,128)(2,1)}), bf16[64,2,4096]{2,1,0:T(2,128)(2,1)S(1)}, u32[]{:S(2)}, u32[]{:S(2)}) %all-to-all-start.2) | async-done | bytes 1048608 | tf_op jit(solution)/shard_map/all_to_all | solution.py:29
  232.5 2.0 broadcast_in_dim.20
  234.5 8.1 %all-to-all-start.3 = ((bf16[64,2,4096]{2,1,0:T(2,128)(2,1)}), bf16[64,2,4096]{2,1,0:T(2,128)(2,1)S(1)}, u32[]{:S(2)}, u32[]{:S(2)}) async-start(bf16[64,2,4096]{2,1,0:T(2,128)(2,1)} %broadcast_in_dim.20), calls=%async_computation.3 | async-start | bytes 2097152 | tf_op jit(solution)/shard_map/all_to_all | solution.py:31
  242.6 3.1 %collective-permute-start.2 = (bf16[128,4096]{1,0:T(8,128)(2,1)S(1)}, bf16[128,4096]{1,0:T(8,128)(2,1)S(1)}, u32[]{:S(2)}, u32[]{:S(2)}) collective-permute-start(bf16[128,4096]{1,0:T(8,128)(2,1)S(1)} %copy-done.3), channel_id=1, source_target_pairs={{0,65},{1,66},{2,67},{3,68},{4,69},{5,70},{6,71},{7,72},{8,73},{9,... | collective-permute-start | bytes 3145736 | tf_op jit(solution)/shard_map/ppermute | solution.py:124
  245.7 35.5 %collective-permute-done.2 = bf16[128,4096]{1,0:T(8,128)(2,1)S(1)} collective-permute-done((bf16[128,4096]{1,0:T(8,128)(2,1)S(1)}, bf16[128,4096]{1,0:T(8,128)(2,1)S(1)}, u32[]{:S(2)}, u32[]{:S(2)}) %collective-permute-start.2) | collective-permute-done | bytes 1048608 | tf_op jit(solution)/shard_map/ppermute | solution.py:124
  281.2 2.3 slice_select_fusion.k1_ref
  283.5 1.2 reshape.23.k3_ref
  284.8 16.4 %shard_map.74 = bf16[128,4096]{1,0:T(8,128)(2,1)} custom-call(s32[5]{0:T(128)} %pad_add_fusion.meta_ref, bf16[128,4096]{1,0:T(8,128)(2,1)} %copy-done, bf16[128,4096]{1,0:T(8,128)(2,1)} %copy-done, bf16[128,4096]{1,0:T(8,128)(2,1)} %slice_select_fusion.k1_ref, bf16[128,4096]{1,0:T(8,128)(2,1)} %slice.34.k3_ref.k2_ref, bf16[128,4096]{1,0:T(8,128)(2,1)} %reshape.23.k3_ref, ...), custom_call_target="tpu_custom_call" | custom-call | tf_op jit(solution)/shard_map/pallas_call | solution.py:77
  (13 shorter events, 0.0 us)
Async XLA Ops:
  3.9 10.9 %copy-start.4 = (s32[64,4]{0,1:T(4,128)S(1)}, s32[64,4]{0,1:T(4,128)}, u32[]{:S(2)}) copy-start(s32[64,4]{0,1:T(4,128)} %param.10) | copy-start | bytes 3076
  3.9 59.8 %all-to-all-start = ((bf16[64,4,4096]{2,1,0:T(4,128)(2,1)}), bf16[64,4,4096]{2,1,0:T(4,128)(2,1)S(1)}, u32[]{:S(2)}, u32[]{:S(2)}) async-start(bf16[64,4,4096]{2,1,0:T(4,128)(2,1)} %reshape.21), calls=%async_computation | async-start | bytes 4194304 | tf_op jit(solution)/shard_map/all_to_all | solution.py:29
  66.1 8.3 %copy-start.1 = (bf16[1,128,4096]{2,1,0:T(8,128)(2,1)S(1)}, bf16[1,128,4096]{2,1,0:T(8,128)(2,1)}, u32[]{:S(2)}) copy-start(bf16[1,128,4096]{2,1,0:T(8,128)(2,1)} %param.8) | copy-start | bytes 3145732
  66.1 81.8 %all-to-all-start.1 = ((bf16[64,4,4096]{2,1,0:T(4,128)(2,1)}), bf16[64,4,4096]{2,1,0:T(4,128)(2,1)S(1)}, u32[]{:S(2)}, u32[]{:S(2)}) async-start(bf16[64,4,4096]{2,1,0:T(4,128)(2,1)} %broadcast_in_dim.18), calls=%async_computation.1 | async-start | bytes 4194304 | tf_op jit(solution)/shard_map/all_to_all | solution.py:31
  77.7 68.0 %collective-permute-start = (bf16[256,4096]{1,0:T(8,128)(2,1)}, bf16[256,4096]{1,0:T(8,128)(2,1)}, u32[]{:S(2)}, u32[]{:S(2)}) collective-permute-start(bf16[256,4096]{1,0:T(8,128)(2,1)} %pad_maximum_fusion), channel_id=1, source_target_pairs={{0,1},{1,2},{2,3},{3,4},{4,5},{5,6},{6,7},{7,8},{8,9},{9,10},{10,1... | collective-permute-start | bytes 6291464 | tf_op jit(solution)/shard_map/ppermute | solution.py:22
  153.4 40.4 %copy-start.2 = (bf16[128,4096]{1,0:T(8,128)(2,1)S(1)}, bf16[128,4096]{1,0:T(8,128)(2,1)}, u32[]{:S(2)}) copy-start(bf16[128,4096]{1,0:T(8,128)(2,1)} %param.9) | copy-start | bytes 3145732
  170.0 23.9 %collective-permute-start.1 = (bf16[128,4096]{1,0:T(8,128)(2,1)}, bf16[128,4096]{1,0:T(8,128)(2,1)S(1)}, u32[]{:S(2)}, u32[]{:S(2)}) collective-permute-start(bf16[128,4096]{1,0:T(8,128)(2,1)} %shard_map.73), channel_id=1, source_target_pairs={{0,64},{64,128},{128,192},{192,256},{256,320},{320,384},{384,448},... | collective-permute-start | bytes 3145736 | tf_op jit(solution)/shard_map/ppermute | solution.py:118
  194.0 1.5 copy-start
  195.5 37.0 %all-to-all-start.2 = ((bf16[64,2,4096]{2,1,0:T(2,128)(2,1)}), bf16[64,2,4096]{2,1,0:T(2,128)(2,1)S(1)}, u32[]{:S(2)}, u32[]{:S(2)}) async-start(bf16[64,2,4096]{2,1,0:T(2,128)(2,1)} %reshape.22), calls=%async_computation.2 | async-start | bytes 2097152 | tf_op jit(solution)/shard_map/all_to_all | solution.py:29
  205.8 36.7 %copy-start.3 = (bf16[128,4096]{1,0:T(8,128)(2,1)S(1)}, bf16[128,4096]{1,0:T(8,128)(2,1)}, u32[]{:S(2)}) copy-start(bf16[128,4096]{1,0:T(8,128)(2,1)} %shard_map.73) | copy-start | bytes 3145732
  234.5 49.1 %all-to-all-start.3 = ((bf16[64,2,4096]{2,1,0:T(2,128)(2,1)}), bf16[64,2,4096]{2,1,0:T(2,128)(2,1)S(1)}, u32[]{:S(2)}, u32[]{:S(2)}) async-start(bf16[64,2,4096]{2,1,0:T(2,128)(2,1)} %broadcast_in_dim.20), calls=%async_computation.3 | async-start | bytes 2097152 | tf_op jit(solution)/shard_map/all_to_all | solution.py:31
  242.6 38.7 %collective-permute-start.2 = (bf16[128,4096]{1,0:T(8,128)(2,1)S(1)}, bf16[128,4096]{1,0:T(8,128)(2,1)S(1)}, u32[]{:S(2)}, u32[]{:S(2)}) collective-permute-start(bf16[128,4096]{1,0:T(8,128)(2,1)S(1)} %copy-done.3), channel_id=1, source_target_pairs={{0,65},{1,66},{2,67},{3,68},{4,69},{5,70},{6,71},{7,72},{8,73},{9,... | collective-permute-start | bytes 3145736 | tf_op jit(solution)/shard_map/ppermute | solution.py:124

commit v3 on v2

--- a/solution.py
+++ b/solution.py
@@ -22,14 +22,19 @@
     return lax.ppermute(value, axis, pairs)
 
 
-def spread(payload, axis, root):
+def scatter_piece(payload, axis, root):
     count = lax.axis_size(axis)
     rows = payload.shape[0]
     pieces = payload.reshape(count, rows // count, payload.shape[1])
     received = lax.all_to_all(pieces, axis, 0, 0, tiled=True)
-    mine = lax.dynamic_index_in_dim(received, root, 0, keepdims=True)
-    gathered = lax.all_to_all(jnp.broadcast_to(mine, pieces.shape), axis, 0, 0, tiled=True)
-    return gathered.reshape(payload.shape)
+    return lax.dynamic_index_in_dim(received, root, 0, keepdims=True)
+
+
+def gather_pieces(piece, axis):
+    count = lax.axis_size(axis)
+    shape = (count,) + piece.shape[1:]
+    gathered = lax.all_to_all(jnp.broadcast_to(piece, shape), axis, 0, 0, tiled=True)
+    return gathered.reshape(count * piece.shape[1], piece.shape[2])
 
 
 def attend_kernel(meta_ref, q_ref, k0_ref, k1_ref, k2_ref, k3_ref, gq_ref, gk_ref, go_ref, out_ref):
@@ -66,19 +71,29 @@
 def attend_pallas(query_rows, key_blocks, entries, global_block, gain_query, gain_key, gain_out):
     meta = jnp.concatenate([entries.astype(jnp.int32), jnp.reshape(global_block, (1,)).astype(jnp.int32)])
     lanes = GROUP * HD
-    row_spec = pl.BlockSpec((BLOCK, lanes), lambda g, meta: (0, g))
+
+    def row_spec(block):
+        return pl.BlockSpec((BLOCK, lanes), lambda g, meta: (block, g))
+
     gain_spec = pl.BlockSpec((1, lanes), lambda g, meta: (0, g))
     grid_spec = pltpu.PrefetchScalarGridSpec(
         num_scalar_prefetch=1,
         grid=(HEADS // GROUP,),
-        in_specs=[row_spec] * (1 + NSEL) + [gain_spec] * 3,
-        out_specs=row_spec,
+        in_specs=[row_spec(0)] + [row_spec(block) for _, block in key_blocks] + [gain_spec] * 3,
+        out_specs=row_spec(0),
     )
     return pl.pallas_call(
         attend_kernel,
         grid_spec=grid_spec,
         out_shape=jax.ShapeDtypeStruct((BLOCK, WIDTH), jnp.bfloat16),
-    )(meta, query_rows, *key_blocks, gain_query.reshape(1, WIDTH), gain_key.reshape(1, WIDTH), gain_out.reshape(1, WIDTH))
+    )(
+        meta,
+        query_rows,
+        *[array for array, _ in key_blocks],
+        gain_query.reshape(1, WIDTH),
+        gain_key.reshape(1, WIDTH),
+        gain_out.reshape(1, WIDTH),
+    )
 
 
 def local(earlier_span, span_inputs, next_inputs, block_list, q_gain, k_gain, out_gain):
@@ -97,19 +112,14 @@
     first_earlier = earlier_span[0]
     first_current = span_inputs[0]
     root = full_entries[LOCAL] % group_size
-    both = spread(jnp.concatenate([first_earlier, first_current]), "ctx", root)
-    strided_earlier, strided_current = both[:BLOCK], both[BLOCK:]
+    both = gather_pieces(
+        scatter_piece(jnp.concatenate([first_earlier, first_current]), "ctx", root), "ctx"
+    )
+    previous_one = shifted(jnp.where(last, first_earlier, first_current), "ctx", 1)
+    held, both = lax.optimization_barrier((jnp.where(last, first_current, next_inputs), both))
+    previous_early = shifted(held, "ctx", 1)
 
-    early = shifted(
-        jnp.concatenate(
-            [jnp.where(last, first_earlier, first_current), jnp.where(last, first_current, next_inputs)]
-        ),
-        "ctx",
-        1,
-    )
-    previous_one, previous_early = early[:BLOCK], early[BLOCK:]
-
-    key_one = (first_current, previous_one, strided_earlier, strided_current)
+    key_one = ((first_current, 0), (previous_one, 0), (both, 0), (both, 1))
     first_result = attend_pallas(
         first_current, key_one, query_entries, global_block, gain_query, gain_key, gain_out
     )
@@ -123,12 +133,12 @@
     ]
     received_previous = lax.ppermute(first_result, ("section", "ctx"), diagonal)
     second_current = jnp.where(section_pos == 0, next_inputs, received)
+    later_root = full_entries[LOCAL + NR] % group_size
+    strided_later = gather_pieces(scatter_piece(second_current, "ctx", later_root), "ctx")
     previous_two = jnp.where(
         (position == 0) | (section_pos == 0), previous_early, received_previous
     )
-    later_root = full_entries[LOCAL + NR] % group_size
-    strided_later = spread(second_current, "ctx", later_root)
-    key_two = (second_current, previous_two, strided_current, strided_later)
+    key_two = ((second_current, 0), (previous_two, 0), (both, 1), (strided_later, 0))
     second_result = attend_pallas(
         second_current, key_two, query_entries, global_block, gain_query, gain_key, gain_out
     )

time: 302 us -> 295 us (0.977)
  the two profiles are of different devices: /device:TPU:326 before, /device:TPU:262 now
where the time goes in v3:
time: 295 us; the launch traced here: 294 us
  waiting for transfers between devices  188 us (64%)
  starting transfers between devices  48.3 us (16%)
  Pallas kernels  32.8 us (11%)
  local copies, waits for them, and re-layouts  13.2 us (4%)
  other arithmetic  7.75 us (3%)
  between operations  4.09 us (1%)
    all_to_all x2, waiting for transfers between devices, scatter_piece(): received = lax.all_to_all(pieces, axis, 0, 0, tiled=True)  71 us
    all_to_all x2, waiting for transfers between devices, gather_pieces(): lax.all_to_all(jnp.broadcast_to(piece, shape), axis, 0, 0, tiled=True)  43.4 us
    ppermute x2, waiting for transfers between devices, shifted(): return lax.ppermute(value, axis, pairs)  41.7 us
    pallas_call x2, Pallas kernels, attend_pallas(): pl.pallas_call(attend_kernel, grid_spec=grid_spec, out_shape=jax.ShapeDty...  32.8 us
    ppermute x1, waiting for transfers between devices, local(): received = lax.ppermute(first_result, 'section', straight)  21.8 us
    all_to_all x2, starting transfers between devices, scatter_piece(): received = lax.all_to_all(pieces, axis, 0, 0, tiled=True)  21.3 us
    all_to_all x2, starting transfers between devices, gather_pieces(): lax.all_to_all(jnp.broadcast_to(piece, shape), axis, 0, 0, tiled=True)  16.4 us
    ppermute x1, waiting for transfers between devices, local(): received_previous = lax.ppermute(first_result, ('section', 'ctx'), diagonal)  10.4 us
  transfers between devices with their start and end apart: 8, of which 7 were waited for; matrix products, arithmetic and copies ran while one was open for 3% of the time, Pallas kernels for 0%

profile of v3, /device:TPU:262, one launch (start us, length us, event | category | flops | bytes accessed | tf_op | source)
XLA Modules:
  0.0 294.4 jit_solution(15317425482300651077)
XLA Ops:
  0.0 1.7 pad_maximum_fusion
  1.7 2.2 reshape.21
  3.9 10.9 %all-to-all-start = ((bf16[64,4,4096]{2,1,0:T(4,128)(2,1)}), bf16[64,4,4096]{2,1,0:T(4,128)(2,1)S(1)}, u32[]{:S(2)}, u32[]{:S(2)}) async-start(bf16[64,4,4096]{2,1,0:T(4,128)(2,1)} %reshape.21), calls=%async_computation | async-start | bytes 4194304 | tf_op jit(solution)/shard_map/all_to_all | solution.py:29
  14.9 0.6 fusion
  17.4 46.3 %all-to-all-done = bf16[64,4,4096]{2,1,0:T(4,128)(2,1)S(1)} async-done(((bf16[64,4,4096]{2,1,0:T(4,128)(2,1)}), bf16[64,4,4096]{2,1,0:T(4,128)(2,1)S(1)}, u32[]{:S(2)}, u32[]{:S(2)}) %all-to-all-start) | async-done | bytes 2097184 | tf_op jit(solution)/shard_map/all_to_all | solution.py:29
  63.8 2.4 broadcast_in_dim.18
  66.1 8.3 %all-to-all-start.1 = ((bf16[64,4,4096]{2,1,0:T(4,128)(2,1)}), bf16[64,4,4096]{2,1,0:T(4,128)(2,1)S(1)}, u32[]{:S(2)}, u32[]{:S(2)}) async-start(bf16[64,4,4096]{2,1,0:T(4,128)(2,1)} %broadcast_in_dim.18), calls=%async_computation.1 | async-start | bytes 4194304 | tf_op jit(solution)/shard_map/all_to_all | solution.py:36
  74.4 3.0 %broadcast_select_fusion.1 = (bf16[128,4096]{1,0:T(8,128)(2,1)}, bf16[128,4096]{1,0:T(8,128)(2,1)}) fusion(bf16[128,4096]{1,0:T(8,128)(2,1)} %param.9, pred[]{:T(512)S(6)} %eq.14, bf16[1,128,4096]{2,1,0:T(8,128)(2,1)S(1)} %copy-done, bf16[1,128,4096]{2,1,0:T(8,128)(2,1)} %param.7), kind=kLoop, calls=%fused_computation.2 | loop fusion | flops 1048576 | bytes 5242881 | tf_op jit(solution)/shard_map/jit(_where)/select_n | solution.py:119
  77.5 2.0 collective-permute-start
  79.5 0.2 dynamic-slice_reduce_fusion
  79.7 0.6 pad_add_fusion.meta_ref
  80.3 43.4 %all-to-all-done.1 = bf16[64,4,4096]{2,1,0:T(4,128)(2,1)S(1)} async-done(((bf16[64,4,4096]{2,1,0:T(4,128)(2,1)}), bf16[64,4,4096]{2,1,0:T(4,128)(2,1)S(1)}, u32[]{:S(2)}, u32[]{:S(2)}) %all-to-all-start.1) | async-done | bytes 2097184 | tf_op jit(solution)/shard_map/all_to_all | solution.py:36
  123.7 2.0 reshape.22.k2_ref.k3_ref
  125.7 8.6 %collective-permute-done.k1_ref = bf16[128,4096]{1,0:T(8,128)(2,1)S(1)} collective-permute-done((bf16[128,4096]{1,0:T(8,128)(2,1)}, bf16[128,4096]{1,0:T(8,128)(2,1)S(1)}, u32[]{:S(2)}, u32[]{:S(2)}) %collective-permute-start) | collective-permute-done | bytes 1048608 | tf_op jit(solution)/shard_map/ppermute | solution.py:22
  134.4 1.0 copy-done.4
  135.3 16.4 %shard_map.73 = bf16[128,4096]{1,0:T(8,128)(2,1)} custom-call(s32[5]{0:T(128)} %pad_add_fusion.meta_ref, bf16[128,4096]{1,0:T(8,128)(2,1)} %bitcast.14, bf16[128,4096]{1,0:T(8,128)(2,1)} %bitcast.15, bf16[128,4096]{1,0:T(8,128)(2,1)} %copy-done.4, bf16[256,4096]{1,0:T(8,128)(2,1)} %reshape.22.k2_ref.k3_ref, bf16[256,4096]{1,0:T(8,128)(2,1)} %reshape.22.k2_ref.k3_ref, ...), custom_call_target="tpu_custom_call" | custom-call | tf_op jit(solution)/shard_map/pallas_call | solution.py:85
  151.7 3.4 %collective-permute-start.1 = (bf16[128,4096]{1,0:T(8,128)(2,1)}, bf16[128,4096]{1,0:T(8,128)(2,1)S(1)}, u32[]{:S(2)}, u32[]{:S(2)}) collective-permute-start(bf16[128,4096]{1,0:T(8,128)(2,1)} %shard_map.73), channel_id=1, source_target_pairs={{0,64},{64,128},{128,192},{192,256},{256,320},{320,384},{384,448},... | collective-permute-start | bytes 3145736 | tf_op jit(solution)/shard_map/ppermute | solution.py:128
  155.1 21.8 %collective-permute-done.1 = bf16[128,4096]{1,0:T(8,128)(2,1)S(1)} collective-permute-done((bf16[128,4096]{1,0:T(8,128)(2,1)}, bf16[128,4096]{1,0:T(8,128)(2,1)S(1)}, u32[]{:S(2)}, u32[]{:S(2)}) %collective-permute-start.1) | collective-permute-done | bytes 1048608 | tf_op jit(solution)/shard_map/ppermute | solution.py:128
  176.9 0.1 broadcast_select_fusion.3.q_ref.k0_ref
  177.0 1.5 reshape.23
  178.6 10.3 %all-to-all-start.2 = ((bf16[64,2,4096]{2,1,0:T(2,128)(2,1)}), bf16[64,2,4096]{2,1,0:T(2,128)(2,1)S(1)}, u32[]{:S(2)}, u32[]{:S(2)}) async-start(bf16[64,2,4096]{2,1,0:T(2,128)(2,1)} %reshape.23), calls=%async_computation.2 | async-start | bytes 2097152 | tf_op jit(solution)/shard_map/all_to_all | solution.py:29
  190.9 24.6 %all-to-all-done.2 = bf16[64,2,4096]{2,1,0:T(2,128)(2,1)S(1)} async-done(((bf16[64,2,4096]{2,1,0:T(2,128)(2,1)}), bf16[64,2,4096]{2,1,0:T(2,128)(2,1)S(1)}, u32[]{:S(2)}, u32[]{:S(2)}) %all-to-all-start.2) | async-done | bytes 1048608 | tf_op jit(solution)/shard_map/all_to_all | solution.py:29
  215.5 2.0 broadcast_in_dim.20
  217.5 8.1 %all-to-all-start.3 = ((bf16[64,2,4096]{2,1,0:T(2,128)(2,1)}), bf16[64,2,4096]{2,1,0:T(2,128)(2,1)S(1)}, u32[]{:S(2)}, u32[]{:S(2)}) async-start(bf16[64,2,4096]{2,1,0:T(2,128)(2,1)} %broadcast_in_dim.20), calls=%async_computation.3 | async-start | bytes 2097152 | tf_op jit(solution)/shard_map/all_to_all | solution.py:36
  225.6 2.0 collective-permute-start.2
  227.7 3.2 %collective-permute-start.3 = (bf16[128,4096]{1,0:T(8,128)(2,1)S(1)}, bf16[128,4096]{1,0:T(8,128)(2,1)}, u32[]{:S(2)}, u32[]{:S(2)}) collective-permute-start(bf16[128,4096]{1,0:T(8,128)(2,1)S(1)} %copy-done.3), channel_id=1, source_target_pairs={{0,65},{1,66},{2,67},{3,68},{4,69},{5,70},{6,71},{7,72},{8,73},{9,... | collective-permute-start | bytes 3145736 | tf_op jit(solution)/shard_map/ppermute | solution.py:134
  230.9 33.1 %collective-permute-done.2 = bf16[128,4096]{1,0:T(8,128)(2,1)S(1)} collective-permute-done((bf16[128,4096]{1,0:T(8,128)(2,1)}, bf16[128,4096]{1,0:T(8,128)(2,1)S(1)}, u32[]{:S(2)}, u32[]{:S(2)}) %collective-permute-start.2) | collective-permute-done | bytes 1048608 | tf_op jit(solution)/shard_map/ppermute | solution.py:22
  264.0 10.4 %collective-permute-done.3 = bf16[128,4096]{1,0:T(8,128)(2,1)} collective-permute-done((bf16[128,4096]{1,0:T(8,128)(2,1)S(1)}, bf16[128,4096]{1,0:T(8,128)(2,1)}, u32[]{:S(2)}, u32[]{:S(2)}) %collective-permute-start.3) | collective-permute-done | bytes 1048608 | tf_op jit(solution)/shard_map/ppermute | solution.py:134
  274.4 2.3 broadcast_select_fusion.k1_ref
  276.8 0.0 all-to-all-done.3
  276.8 1.2 reshape.24.k3_ref
  278.0 16.4 %shard_map.74 = bf16[128,4096]{1,0:T(8,128)(2,1)} custom-call(s32[5]{0:T(128)} %pad_add_fusion.meta_ref, bf16[128,4096]{1,0:T(8,128)(2,1)} %copy-done.1, bf16[128,4096]{1,0:T(8,128)(2,1)} %copy-done.1, bf16[128,4096]{1,0:T(8,128)(2,1)} %broadcast_select_fusion.k1_ref, bf16[256,4096]{1,0:T(8,128)(2,1)} %reshape.22.k2_ref.k3_ref, ...), custom_call_target="tpu_custom_call" | custom-call | tf_op jit(solution)/shard_map/pallas_call | solution.py:85
  (13 shorter events, 0.0 us)
Async XLA Ops:
  3.9 10.9 %copy-start.5 = (s32[64,4]{0,1:T(4,128)S(1)}, s32[64,4]{0,1:T(4,128)}, u32[]{:S(2)}) copy-start(s32[64,4]{0,1:T(4,128)} %param.10) | copy-start | bytes 3076
  3.9 59.8 %all-to-all-start = ((bf16[64,4,4096]{2,1,0:T(4,128)(2,1)}), bf16[64,4,4096]{2,1,0:T(4,128)(2,1)S(1)}, u32[]{:S(2)}, u32[]{:S(2)}) async-start(bf16[64,4,4096]{2,1,0:T(4,128)(2,1)} %reshape.21), calls=%async_computation | async-start | bytes 4194304 | tf_op jit(solution)/shard_map/all_to_all | solution.py:29
  66.1 8.3 %copy-start = (bf16[1,128,4096]{2,1,0:T(8,128)(2,1)S(1)}, bf16[1,128,4096]{2,1,0:T(8,128)(2,1)}, u32[]{:S(2)}) copy-start(bf16[1,128,4096]{2,1,0:T(8,128)(2,1)} %param.8) | copy-start | bytes 3145732
  66.1 57.5 %all-to-all-start.1 = ((bf16[64,4,4096]{2,1,0:T(4,128)(2,1)}), bf16[64,4,4096]{2,1,0:T(4,128)(2,1)S(1)}, u32[]{:S(2)}, u32[]{:S(2)}) async-start(bf16[64,4,4096]{2,1,0:T(4,128)(2,1)} %broadcast_in_dim.18), calls=%async_computation.1 | async-start | bytes 4194304 | tf_op jit(solution)/shard_map/all_to_all | solution.py:36
  77.5 56.9 %collective-permute-start = (bf16[128,4096]{1,0:T(8,128)(2,1)}, bf16[128,4096]{1,0:T(8,128)(2,1)S(1)}, u32[]{:S(2)}, u32[]{:S(2)}) collective-permute-start(bf16[128,4096]{1,0:T(8,128)(2,1)} %get-tuple-element.10), channel_id=1, source_target_pairs={{0,1},{1,2},{2,3},{3,4},{4,5},{5,6},{6,7},{7,8},{8,9},{9,10},{10,1... | collective-permute-start | bytes 3145736 | tf_op jit(solution)/shard_map/ppermute | solution.py:22
  125.7 51.2 %copy-start.2 = (bf16[128,4096]{1,0:T(8,128)(2,1)S(1)}, bf16[128,4096]{1,0:T(8,128)(2,1)}, u32[]{:S(2)}) copy-start(bf16[128,4096]{1,0:T(8,128)(2,1)} %param.9) | copy-start | bytes 3145732
  134.4 1.0 copy-start.4
  151.7 25.2 %collective-permute-start.1 = (bf16[128,4096]{1,0:T(8,128)(2,1)}, bf16[128,4096]{1,0:T(8,128)(2,1)S(1)}, u32[]{:S(2)}, u32[]{:S(2)}) collective-permute-start(bf16[128,4096]{1,0:T(8,128)(2,1)} %shard_map.73), channel_id=1, source_target_pairs={{0,64},{64,128},{128,192},{192,256},{256,320},{320,384},{384,448},... | collective-permute-start | bytes 3145736 | tf_op jit(solution)/shard_map/ppermute | solution.py:128
  177.0 1.5 copy-start.1
  178.6 37.0 %all-to-all-start.2 = ((bf16[64,2,4096]{2,1,0:T(2,128)(2,1)}), bf16[64,2,4096]{2,1,0:T(2,128)(2,1)S(1)}, u32[]{:S(2)}, u32[]{:S(2)}) async-start(bf16[64,2,4096]{2,1,0:T(2,128)(2,1)} %reshape.23), calls=%async_computation.2 | async-start | bytes 2097152 | tf_op jit(solution)/shard_map/all_to_all | solution.py:29
  188.9 38.8 %copy-start.3 = (bf16[128,4096]{1,0:T(8,128)(2,1)S(1)}, bf16[128,4096]{1,0:T(8,128)(2,1)}, u32[]{:S(2)}) copy-start(bf16[128,4096]{1,0:T(8,128)(2,1)} %shard_map.73) | copy-start | bytes 3145732
  217.5 59.3 %all-to-all-start.3 = ((bf16[64,2,4096]{2,1,0:T(2,128)(2,1)}), bf16[64,2,4096]{2,1,0:T(2,128)(2,1)S(1)}, u32[]{:S(2)}, u32[]{:S(2)}) async-start(bf16[64,2,4096]{2,1,0:T(2,128)(2,1)} %broadcast_in_dim.20), calls=%async_computation.3 | async-start | bytes 2097152 | tf_op jit(solution)/shard_map/all_to_all | solution.py:36
  225.6 38.4 %collective-permute-start.2 = (bf16[128,4096]{1,0:T(8,128)(2,1)}, bf16[128,4096]{1,0:T(8,128)(2,1)S(1)}, u32[]{:S(2)}, u32[]{:S(2)}) collective-permute-start(bf16[128,4096]{1,0:T(8,128)(2,1)} %get-tuple-element.8), channel_id=1, source_target_pairs={{0,1},{1,2},{2,3},{3,4},{4,5},{5,6},{6,7},{7,8},{8,9},{9,10},{10,1... | collective-permute-start | bytes 3145736 | tf_op jit(solution)/shard_map/ppermute | solution.py:22
  227.7 46.8 %collective-permute-start.3 = (bf16[128,4096]{1,0:T(8,128)(2,1)S(1)}, bf16[128,4096]{1,0:T(8,128)(2,1)}, u32[]{:S(2)}, u32[]{:S(2)}) collective-permute-start(bf16[128,4096]{1,0:T(8,128)(2,1)S(1)} %copy-done.3), channel_id=1, source_target_pairs={{0,65},{1,66},{2,67},{3,68},{4,69},{5,70},{6,71},{7,72},{8,73},{9,... | collective-permute-start | bytes 3145736 | tf_op jit(solution)/shard_map/ppermute | solution.py:134

commit v4 on v3

--- a/solution.py
+++ b/solution.py
@@ -112,10 +112,10 @@
     first_earlier = earlier_span[0]
     first_current = span_inputs[0]
     root = full_entries[LOCAL] % group_size
-    both = gather_pieces(
-        scatter_piece(jnp.concatenate([first_earlier, first_current]), "ctx", root), "ctx"
-    )
+    piece_one = scatter_piece(jnp.concatenate([first_earlier, first_current]), "ctx", root)
     previous_one = shifted(jnp.where(last, first_earlier, first_current), "ctx", 1)
+    piece_one, previous_one = lax.optimization_barrier((piece_one, previous_one))
+    both = gather_pieces(piece_one, "ctx")
     held, both = lax.optimization_barrier((jnp.where(last, first_current, next_inputs), both))
     previous_early = shifted(held, "ctx", 1)
 
@@ -133,6 +133,7 @@
     ]
     received_previous = lax.ppermute(first_result, ("section", "ctx"), diagonal)
     second_current = jnp.where(section_pos == 0, next_inputs, received)
+    second_current, previous_early = lax.optimization_barrier((second_current, previous_early))
     later_root = full_entries[LOCAL + NR] % group_size
     strided_later = gather_pieces(scatter_piece(second_current, "ctx", later_root), "ctx")
     previous_two = jnp.where(

time: 295 us -> 287 us (0.973)
  the two profiles are of different devices: /device:TPU:262 before, /device:TPU:326 now
where the time goes in v4:
time: 287 us; the launch traced here: 286 us
  waiting for transfers between devices  181 us (63%)
  starting transfers between devices  47.7 us (17%)
  Pallas kernels  32.8 us (11%)
  local copies, waits for them, and re-layouts  13 us (5%)
  other arithmetic  7.51 us (3%)
  between operations  4.24 us (1%)
    all_to_all x2, waiting for transfers between devices, scatter_piece(): received = lax.all_to_all(pieces, axis, 0, 0, tiled=True)  67.5 us
    all_to_all x2, waiting for transfers between devices, gather_pieces(): lax.all_to_all(jnp.broadcast_to(piece, shape), axis, 0, 0, tiled=True)  48.1 us
    ppermute x1, waiting for transfers between devices, local(): received_previous = lax.ppermute(first_result, ('section', 'ctx'), diagonal)  35.6 us
    pallas_call x2, Pallas kernels, attend_pallas(): pl.pallas_call(attend_kernel, grid_spec=grid_spec, out_shape=jax.ShapeDty...  32.8 us
    ppermute x1, waiting for transfers between devices, local(): received = lax.ppermute(first_result, 'section', straight)  20 us
    all_to_all x2, starting transfers between devices, scatter_piece(): received = lax.all_to_all(pieces, axis, 0, 0, tiled=True)  19.4 us
    all_to_all x2, starting transfers between devices, gather_pieces(): lax.all_to_all(jnp.broadcast_to(piece, shape), axis, 0, 0, tiled=True)  16 us
    ppermute x2, waiting for transfers between devices, shifted(): return lax.ppermute(value, axis, pairs)  9.79 us
  transfers between devices with their start and end apart: 8, of which 6 were waited for; matrix products, arithmetic and copies ran while one was open for 3% of the time, Pallas kernels for 0%

profile of v4, /device:TPU:326, one launch (start us, length us, event | category | flops | bytes accessed | tf_op | source)
XLA Modules:
  0.0 286.1 jit_solution(13781422427567706502)
XLA Ops:
  0.0 1.7 pad_maximum_fusion
  1.7 2.2 reshape.21
  3.9 11.3 %all-to-all-start = ((bf16[64,4,4096]{2,1,0:T(4,128)(2,1)}), bf16[64,4,4096]{2,1,0:T(4,128)(2,1)}, u32[]{:S(2)}, u32[]{:S(2)}) async-start(bf16[64,4,4096]{2,1,0:T(4,128)(2,1)} %reshape.21), calls=%async_computation | async-start | bytes 4194304 | tf_op jit(solution)/shard_map/all_to_all | solution.py:29
  15.2 0.0 copy-start.6
  15.2 1.5 broadcast_select_fusion.1
  16.7 2.0 collective-permute-start
  18.7 0.7 fusion
  21.5 42.9 %all-to-all-done = bf16[64,4,4096]{2,1,0:T(4,128)(2,1)} async-done(((bf16[64,4,4096]{2,1,0:T(4,128)(2,1)}), bf16[64,4,4096]{2,1,0:T(4,128)(2,1)}, u32[]{:S(2)}, u32[]{:S(2)}) %all-to-all-start) | async-done | bytes 2097184 | tf_op jit(solution)/shard_map/all_to_all | solution.py:29
  64.4 0.8 constant_dynamic-slice_fusion
  65.1 9.8 %collective-permute-done.k1_ref = bf16[128,4096]{1,0:T(8,128)(2,1)S(1)} collective-permute-done((bf16[128,4096]{1,0:T(8,128)(2,1)}, bf16[128,4096]{1,0:T(8,128)(2,1)S(1)}, u32[]{:S(2)}, u32[]{:S(2)}) %collective-permute-start) | collective-permute-done | bytes 1048608 | tf_op jit(solution)/shard_map/ppermute | solution.py:22
  74.9 2.4 broadcast_in_dim.18
  77.3 7.9 %all-to-all-start.1 = ((bf16[64,4,4096]{2,1,0:T(4,128)(2,1)}), bf16[64,4,4096]{2,1,0:T(4,128)(2,1)S(1)}, u32[]{:S(2)}, u32[]{:S(2)}) async-start(bf16[64,4,4096]{2,1,0:T(4,128)(2,1)} %broadcast_in_dim.18), calls=%async_computation.1 | async-start | bytes 4194304 | tf_op jit(solution)/shard_map/all_to_all | solution.py:36
  85.2 0.2 dynamic-slice_reduce_fusion
  85.4 0.7 pad_add_fusion.meta_ref
  86.1 48.0 %all-to-all-done.1 = bf16[64,4,4096]{2,1,0:T(4,128)(2,1)S(1)} async-done(((bf16[64,4,4096]{2,1,0:T(4,128)(2,1)}), bf16[64,4,4096]{2,1,0:T(4,128)(2,1)S(1)}, u32[]{:S(2)}, u32[]{:S(2)}) %all-to-all-start.1) | async-done | bytes 2097184 | tf_op jit(solution)/shard_map/all_to_all | solution.py:36
  134.1 2.0 reshape.22.k2_ref.k3_ref
  136.2 16.4 %shard_map.73 = bf16[128,4096]{1,0:T(8,128)(2,1)} custom-call(s32[5]{0:T(128)} %pad_add_fusion.meta_ref, bf16[128,4096]{1,0:T(8,128)(2,1)} %bitcast.13, bf16[128,4096]{1,0:T(8,128)(2,1)} %bitcast.14, bf16[128,4096]{1,0:T(8,128)(2,1)} %copy-done.5, bf16[256,4096]{1,0:T(8,128)(2,1)} %reshape.22.k2_ref.k3_ref, bf16[256,4096]{1,0:T(8,128)(2,1)} %reshape.22.k2_ref.k3_ref, ...), custom_call_target="tpu_custom_call" | custom-call | tf_op jit(solution)/shard_map/pallas_call | solution.py:85
  152.6 3.4 %collective-permute-start.1 = (bf16[128,4096]{1,0:T(8,128)(2,1)}, bf16[128,4096]{1,0:T(8,128)(2,1)}, u32[]{:S(2)}, u32[]{:S(2)}) collective-permute-start(bf16[128,4096]{1,0:T(8,128)(2,1)} %shard_map.73), channel_id=1, source_target_pairs={{0,64},{64,128},{128,192},{192,256},{256,320},{320,384},{384,448},... | collective-permute-start | bytes 3145736 | tf_op jit(solution)/shard_map/ppermute | solution.py:128
  155.9 3.7 %collective-permute-start.2 = (bf16[128,4096]{1,0:T(8,128)(2,1)}, bf16[128,4096]{1,0:T(8,128)(2,1)S(1)}, u32[]{:S(2)}, u32[]{:S(2)}) collective-permute-start(bf16[128,4096]{1,0:T(8,128)(2,1)} %get-tuple-element.14), channel_id=1, source_target_pairs={{0,1},{1,2},{2,3},{3,4},{4,5},{5,6},{6,7},{7,8},{8,9},{9,10},{10,1... | collective-permute-start | bytes 3145736 | tf_op jit(solution)/shard_map/ppermute | solution.py:22
  159.7 20.0 %collective-permute-done.1 = bf16[128,4096]{1,0:T(8,128)(2,1)} collective-permute-done((bf16[128,4096]{1,0:T(8,128)(2,1)}, bf16[128,4096]{1,0:T(8,128)(2,1)}, u32[]{:S(2)}, u32[]{:S(2)}) %collective-permute-start.1) | collective-permute-done | bytes 1048608 | tf_op jit(solution)/shard_map/ppermute | solution.py:128
  179.7 1.3 broadcast_select_fusion.3.q_ref.k0_ref
  181.0 0.0 collective-permute-done.2
  181.0 1.5 reshape.23
  182.5 8.2 %all-to-all-start.2 = ((bf16[64,2,4096]{2,1,0:T(2,128)(2,1)}), bf16[64,2,4096]{2,1,0:T(2,128)(2,1)S(1)}, u32[]{:S(2)}, u32[]{:S(2)}) async-start(bf16[64,2,4096]{2,1,0:T(2,128)(2,1)} %reshape.23), calls=%async_computation.2 | async-start | bytes 2097152 | tf_op jit(solution)/shard_map/all_to_all | solution.py:29
  192.7 24.7 %all-to-all-done.2 = bf16[64,2,4096]{2,1,0:T(2,128)(2,1)S(1)} async-done(((bf16[64,2,4096]{2,1,0:T(2,128)(2,1)}), bf16[64,2,4096]{2,1,0:T(2,128)(2,1)S(1)}, u32[]{:S(2)}, u32[]{:S(2)}) %all-to-all-start.2) | async-done | bytes 1048608 | tf_op jit(solution)/shard_map/all_to_all | solution.py:29
  217.3 2.0 broadcast_in_dim.20
  219.3 8.1 %all-to-all-start.3 = ((bf16[64,2,4096]{2,1,0:T(2,128)(2,1)}), bf16[64,2,4096]{2,1,0:T(2,128)(2,1)S(1)}, u32[]{:S(2)}, u32[]{:S(2)}) async-start(bf16[64,2,4096]{2,1,0:T(2,128)(2,1)} %broadcast_in_dim.20), calls=%async_computation.3 | async-start | bytes 2097152 | tf_op jit(solution)/shard_map/all_to_all | solution.py:36
  227.4 3.1 %collective-permute-start.3 = (bf16[128,4096]{1,0:T(8,128)(2,1)S(1)}, bf16[128,4096]{1,0:T(8,128)(2,1)}, u32[]{:S(2)}, u32[]{:S(2)}) collective-permute-start(bf16[128,4096]{1,0:T(8,128)(2,1)S(1)} %copy-done.4), channel_id=1, source_target_pairs={{0,65},{1,66},{2,67},{3,68},{4,69},{5,70},{6,71},{7,72},{8,73},{9,... | collective-permute-start | bytes 3145736 | tf_op jit(solution)/shard_map/ppermute | solution.py:134
  230.6 35.6 %collective-permute-done.3 = bf16[128,4096]{1,0:T(8,128)(2,1)} collective-permute-done((bf16[128,4096]{1,0:T(8,128)(2,1)S(1)}, bf16[128,4096]{1,0:T(8,128)(2,1)}, u32[]{:S(2)}, u32[]{:S(2)}) %collective-permute-start.3) | collective-permute-done | bytes 1048608 | tf_op jit(solution)/shard_map/ppermute | solution.py:134
  266.2 2.3 broadcast_select_fusion.k1_ref
  268.5 1.2 reshape.24.k3_ref
  269.7 16.4 %shard_map.74 = bf16[128,4096]{1,0:T(8,128)(2,1)} custom-call(s32[5]{0:T(128)} %pad_add_fusion.meta_ref, bf16[128,4096]{1,0:T(8,128)(2,1)} %copy-done.1, bf16[128,4096]{1,0:T(8,128)(2,1)} %copy-done.1, bf16[128,4096]{1,0:T(8,128)(2,1)} %broadcast_select_fusion.k1_ref, bf16[256,4096]{1,0:T(8,128)(2,1)} %reshape.22.k2_ref.k3_ref, ...), custom_call_target="tpu_custom_call" | custom-call | tf_op jit(solution)/shard_map/pallas_call | solution.py:85
  (15 shorter events, 0.0 us)
Async XLA Ops:
  3.9 11.3 %copy-start = (bf16[1,128,4096]{2,1,0:T(8,128)(2,1)S(1)}, bf16[1,128,4096]{2,1,0:T(8,128)(2,1)}, u32[]{:S(2)}) copy-start(bf16[1,128,4096]{2,1,0:T(8,128)(2,1)} %param.8) | copy-start | bytes 3145732
  3.9 11.3 %copy-start.2 = (bf16[128,4096]{1,0:T(8,128)(2,1)S(1)}, bf16[128,4096]{1,0:T(8,128)(2,1)}, u32[]{:S(2)}) copy-start(bf16[128,4096]{1,0:T(8,128)(2,1)} %param.9) | copy-start | bytes 3145732
  3.9 11.3 %copy-start.3 = (bf16[1,128,4096]{2,1,0:T(8,128)(2,1)S(1)}, bf16[1,128,4096]{2,1,0:T(8,128)(2,1)}, u32[]{:S(2)}) copy-start(bf16[1,128,4096]{2,1,0:T(8,128)(2,1)} %param.7) | copy-start | bytes 3145732
  3.9 60.5 %all-to-all-start = ((bf16[64,4,4096]{2,1,0:T(4,128)(2,1)}), bf16[64,4,4096]{2,1,0:T(4,128)(2,1)}, u32[]{:S(2)}, u32[]{:S(2)}) async-start(bf16[64,4,4096]{2,1,0:T(4,128)(2,1)} %reshape.21), calls=%async_computation | async-start | bytes 4194304 | tf_op jit(solution)/shard_map/all_to_all | solution.py:29
  15.2 3.5 %copy-start.6 = (s32[64,4]{0,1:T(4,128)S(1)}, s32[64,4]{0,1:T(4,128)}, u32[]{:S(2)}) copy-start(s32[64,4]{0,1:T(4,128)} %param.10) | copy-start | bytes 3076
  16.7 58.2 %collective-permute-start = (bf16[128,4096]{1,0:T(8,128)(2,1)}, bf16[128,4096]{1,0:T(8,128)(2,1)S(1)}, u32[]{:S(2)}, u32[]{:S(2)}) collective-permute-start(bf16[128,4096]{1,0:T(8,128)(2,1)} %get-tuple-element.18), channel_id=1, source_target_pairs={{0,1},{1,2},{2,3},{3,4},{4,5},{5,6},{6,7},{7,8},{8,9},{9,10},{10,1... | collective-permute-start | bytes 3145736 | tf_op jit(solution)/shard_map/ppermute | solution.py:22
  74.9 2.4 copy-start.5
  77.3 56.8 %all-to-all-start.1 = ((bf16[64,4,4096]{2,1,0:T(4,128)(2,1)}), bf16[64,4,4096]{2,1,0:T(4,128)(2,1)S(1)}, u32[]{:S(2)}, u32[]{:S(2)}) async-start(bf16[64,4,4096]{2,1,0:T(4,128)(2,1)} %broadcast_in_dim.18), calls=%async_computation.1 | async-start | bytes 4194304 | tf_op jit(solution)/shard_map/all_to_all | solution.py:36
  152.6 27.1 %collective-permute-start.1 = (bf16[128,4096]{1,0:T(8,128)(2,1)}, bf16[128,4096]{1,0:T(8,128)(2,1)}, u32[]{:S(2)}, u32[]{:S(2)}) collective-permute-start(bf16[128,4096]{1,0:T(8,128)(2,1)} %shard_map.73), channel_id=1, source_target_pairs={{0,64},{64,128},{128,192},{192,256},{256,320},{320,384},{384,448},... | collective-permute-start | bytes 3145736 | tf_op jit(solution)/shard_map/ppermute | solution.py:128
  155.9 25.1 %collective-permute-start.2 = (bf16[128,4096]{1,0:T(8,128)(2,1)}, bf16[128,4096]{1,0:T(8,128)(2,1)S(1)}, u32[]{:S(2)}, u32[]{:S(2)}) collective-permute-start(bf16[128,4096]{1,0:T(8,128)(2,1)} %get-tuple-element.14), channel_id=1, source_target_pairs={{0,1},{1,2},{2,3},{3,4},{4,5},{5,6},{6,7},{7,8},{8,9},{9,10},{10,1... | collective-permute-start | bytes 3145736 | tf_op jit(solution)/shard_map/ppermute | solution.py:22
  181.0 1.5 copy-start.1
  182.5 34.8 %all-to-all-start.2 = ((bf16[64,2,4096]{2,1,0:T(2,128)(2,1)}), bf16[64,2,4096]{2,1,0:T(2,128)(2,1)S(1)}, u32[]{:S(2)}, u32[]{:S(2)}) async-start(bf16[64,2,4096]{2,1,0:T(2,128)(2,1)} %reshape.23), calls=%async_computation.2 | async-start | bytes 2097152 | tf_op jit(solution)/shard_map/all_to_all | solution.py:29
  190.7 36.7 %copy-start.4 = (bf16[128,4096]{1,0:T(8,128)(2,1)S(1)}, bf16[128,4096]{1,0:T(8,128)(2,1)}, u32[]{:S(2)}) copy-start(bf16[128,4096]{1,0:T(8,128)(2,1)} %shard_map.73) | copy-start | bytes 3145732
  219.3 49.2 %all-to-all-start.3 = ((bf16[64,2,4096]{2,1,0:T(2,128)(2,1)}), bf16[64,2,4096]{2,1,0:T(2,128)(2,1)S(1)}, u32[]{:S(2)}, u32[]{:S(2)}) async-start(bf16[64,2,4096]{2,1,0:T(2,128)(2,1)} %broadcast_in_dim.20), calls=%async_computation.3 | async-start | bytes 2097152 | tf_op jit(solution)/shard_map/all_to_all | solution.py:36
  227.4 38.8 %collective-permute-start.3 = (bf16[128,4096]{1,0:T(8,128)(2,1)S(1)}, bf16[128,4096]{1,0:T(8,128)(2,1)}, u32[]{:S(2)}, u32[]{:S(2)}) collective-permute-start(bf16[128,4096]{1,0:T(8,128)(2,1)S(1)} %copy-done.4), channel_id=1, source_target_pairs={{0,65},{1,66},{2,67},{3,68},{4,69},{5,70},{6,71},{7,72},{8,73},{9,... | collective-permute-start | bytes 3145736 | tf_op jit(solution)/shard_map/ppermute | solution.py:134

commit v5 on v4

--- a/solution.py
+++ b/solution.py
@@ -124,18 +124,21 @@
         first_current, key_one, query_entries, global_block, gain_query, gain_key, gain_out
     )
 
+    later_root = full_entries[LOCAL + NR] % group_size
+    source = jnp.where(section_pos == sections - 1, next_inputs, first_result)
+    source, previous_early = lax.optimization_barrier((source, previous_early))
+    piece = shifted(scatter_piece(source, "ctx", later_root), "section", 1)
+    outgoing, piece = lax.optimization_barrier((first_result, piece))
     straight = [(s, s + 1) for s in range(sections - 1)]
-    received = lax.ppermute(first_result, "section", straight)
+    received = lax.ppermute(outgoing, "section", straight)
     diagonal = [
         (s * group_size + i, (s + 1) * group_size + i + 1)
         for s in range(sections - 1)
         for i in range(group_size - 1)
     ]
-    received_previous = lax.ppermute(first_result, ("section", "ctx"), diagonal)
+    received_previous = lax.ppermute(outgoing, ("section", "ctx"), diagonal)
+    strided_later = gather_pieces(piece, "ctx")
     second_current = jnp.where(section_pos == 0, next_inputs, received)
-    second_current, previous_early = lax.optimization_barrier((second_current, previous_early))
-    later_root = full_entries[LOCAL + NR] % group_size
-    strided_later = gather_pieces(scatter_piece(second_current, "ctx", later_root), "ctx")
     previous_two = jnp.where(
         (position == 0) | (section_pos == 0), previous_early, received_previous
     )

time: 287 us -> 275 us (0.958)
  the two profiles are of different devices: /device:TPU:326 before, /device:TPU:70 now
where the time goes in v5:
time: 275 us
  waiting for transfers between devices  160 us (58%)
  starting transfers between devices  54.6 us (20%)
  Pallas kernels  32.8 us (12%)
  local copies, waits for them, and re-layouts  13 us (5%)
  other arithmetic  9.76 us (4%)
  between operations  4.14 us (2%)
    all_to_all x2, waiting for transfers between devices, scatter_piece(): received = lax.all_to_all(pieces, axis, 0, 0, tiled=True)  67.6 us
    all_to_all x2, waiting for transfers between devices, gather_pieces(): lax.all_to_all(jnp.broadcast_to(piece, shape), axis, 0, 0, tiled=True)  48.7 us
    pallas_call x2, Pallas kernels, attend_pallas(): pl.pallas_call(attend_kernel, grid_spec=grid_spec, out_shape=jax.ShapeDty...  32.8 us
    ppermute x1, waiting for transfers between devices, local(): received_previous = lax.ppermute(outgoing, ('section', 'ctx'), diagonal)  22 us
    all_to_all x2, starting transfers between devices, scatter_piece(): received = lax.all_to_all(pieces, axis, 0, 0, tiled=True)  18.8 us
    all_to_all x2, starting transfers between devices, gather_pieces(): lax.all_to_all(jnp.broadcast_to(piece, shape), axis, 0, 0, tiled=True)  16 us
    ppermute x3, waiting for transfers between devices, shifted(): return lax.ppermute(value, axis, pairs)  11.2 us
    ppermute x1, waiting for transfers between devices, local(): received = lax.ppermute(outgoing, 'section', straight)  10.8 us
  transfers between devices with their start and end apart: 9, of which 7 were waited for; matrix products, arithmetic and copies ran while one was open for 4% of the time, Pallas kernels for 6%

profile of v5, /device:TPU:70, one launch (start us, length us, event | category | flops | bytes accessed | tf_op | source)
XLA Modules:
  0.0 274.5 jit_solution(15368143668566142630)
XLA Ops:
  0.0 1.7 pad_maximum_fusion
  1.7 2.2 reshape.21
  3.9 11.3 %all-to-all-start = ((bf16[64,4,4096]{2,1,0:T(4,128)(2,1)}), bf16[64,4,4096]{2,1,0:T(4,128)(2,1)}, u32[]{:S(2)}, u32[]{:S(2)}) async-start(bf16[64,4,4096]{2,1,0:T(4,128)(2,1)} %reshape.21), calls=%async_computation | async-start | bytes 4194304 | tf_op jit(solution)/shard_map/all_to_all | solution.py:29
  15.2 1.5 broadcast_select_fusion.2
  16.7 2.0 collective-permute-start
  18.7 0.7 fusion
  21.5 42.9 %all-to-all-done = bf16[64,4,4096]{2,1,0:T(4,128)(2,1)} async-done(((bf16[64,4,4096]{2,1,0:T(4,128)(2,1)}), bf16[64,4,4096]{2,1,0:T(4,128)(2,1)}, u32[]{:S(2)}, u32[]{:S(2)}) %all-to-all-start) | async-done | bytes 2097184 | tf_op jit(solution)/shard_map/all_to_all | solution.py:29
  64.4 0.8 constant_dynamic-slice_fusion.1
  65.1 9.8 %collective-permute-done.k1_ref = bf16[128,4096]{1,0:T(8,128)(2,1)S(1)} collective-permute-done((bf16[128,4096]{1,0:T(8,128)(2,1)}, bf16[128,4096]{1,0:T(8,128)(2,1)S(1)}, u32[]{:S(2)}, u32[]{:S(2)}) %collective-permute-start) | collective-permute-done | bytes 1048608 | tf_op jit(solution)/shard_map/ppermute | solution.py:22
  74.9 2.4 broadcast_in_dim.18
  77.3 7.9 %all-to-all-start.1 = ((bf16[64,4,4096]{2,1,0:T(4,128)(2,1)}), bf16[64,4,4096]{2,1,0:T(4,128)(2,1)S(1)}, u32[]{:S(2)}, u32[]{:S(2)}) async-start(bf16[64,4,4096]{2,1,0:T(4,128)(2,1)} %broadcast_in_dim.18), calls=%async_computation.1 | async-start | bytes 4194304 | tf_op jit(solution)/shard_map/all_to_all | solution.py:36
  85.4 48.7 %all-to-all-done.1 = bf16[64,4,4096]{2,1,0:T(4,128)(2,1)S(1)} async-done(((bf16[64,4,4096]{2,1,0:T(4,128)(2,1)}), bf16[64,4,4096]{2,1,0:T(4,128)(2,1)S(1)}, u32[]{:S(2)}, u32[]{:S(2)}) %all-to-all-start.1) | async-done | bytes 2097184 | tf_op jit(solution)/shard_map/all_to_all | solution.py:36
  134.1 2.0 reshape.22.k2_ref.k3_ref
  136.2 4.0 %collective-permute-start.1 = (bf16[128,4096]{1,0:T(8,128)(2,1)}, bf16[128,4096]{1,0:T(8,128)(2,1)}, u32[]{:S(2)}, u32[]{:S(2)}) collective-permute-start(bf16[128,4096]{1,0:T(8,128)(2,1)} %get-tuple-element.16), channel_id=1, source_target_pairs={{0,1},{1,2},{2,3},{3,4},{4,5},{5,6},{6,7},{7,8},{8,9},{9,10},{10,1... | collective-permute-start | bytes 3145736 | tf_op jit(solution)/shard_map/ppermute | solution.py:22
  140.2 0.6 pad_add_fusion.meta_ref
  140.8 16.4 %shard_map.73 = bf16[128,4096]{1,0:T(8,128)(2,1)} custom-call(s32[5]{0:T(128)} %pad_add_fusion.meta_ref, bf16[128,4096]{1,0:T(8,128)(2,1)} %bitcast.12, bf16[128,4096]{1,0:T(8,128)(2,1)} %bitcast.13, bf16[128,4096]{1,0:T(8,128)(2,1)} %copy-done.4, bf16[256,4096]{1,0:T(8,128)(2,1)} %reshape.22.k2_ref.k3_ref, bf16[256,4096]{1,0:T(8,128)(2,1)} %reshape.22.k2_ref.k3_ref, ...), custom_call_target="tpu_custom_call" | custom-call | tf_op jit(solution)/shard_map/pallas_call | solution.py:85
  157.2 1.3 broadcast_select_fusion.1
  158.5 1.5 reshape.23
  160.0 7.5 %all-to-all-start.2 = ((bf16[64,2,4096]{2,1,0:T(2,128)(2,1)}), bf16[64,2,4096]{2,1,0:T(2,128)(2,1)S(1)}, u32[]{:S(2)}, u32[]{:S(2)}) async-start(bf16[64,2,4096]{2,1,0:T(2,128)(2,1)} %reshape.23), calls=%async_computation.2 | async-start | bytes 2097152 | tf_op jit(solution)/shard_map/all_to_all | solution.py:29
  169.4 24.8 %all-to-all-done.2 = bf16[64,2,4096]{2,1,0:T(2,128)(2,1)S(1)} async-done(((bf16[64,2,4096]{2,1,0:T(2,128)(2,1)}), bf16[64,2,4096]{2,1,0:T(2,128)(2,1)S(1)}, u32[]{:S(2)}, u32[]{:S(2)}) %all-to-all-start.2) | async-done | bytes 1048608 | tf_op jit(solution)/shard_map/all_to_all | solution.py:29
  194.2 4.3 %collective-permute-start.2 = (bf16[1,2,4096]{2,1,0:T(2,128)(2,1)S(1)}, bf16[1,2,4096]{2,1,0:T(2,128)(2,1)S(1)}, u32[]{:S(2)}, u32[]{:S(2)}) collective-permute-start(bf16[1,2,4096]{2,1,0:T(2,128)(2,1)S(1)} %constant_dynamic-slice_fusion), channel_id=1, source_target_pairs={{0,64},{64,128},{128,192},{192,256},{256,320},{320,384},{384,448},... | collective-permute-start | bytes 49160 | tf_op jit(solution)/shard_map/ppermute | solution.py:22
  198.5 1.4 collective-permute-done.2
  199.9 4.3 %collective-permute-start.3 = (bf16[128,4096]{1,0:T(8,128)(2,1)S(1)}, bf16[128,4096]{1,0:T(8,128)(2,1)}, u32[]{:S(2)}, u32[]{:S(2)}) collective-permute-start(bf16[128,4096]{1,0:T(8,128)(2,1)S(1)} %copy-done.2), channel_id=1, source_target_pairs={{0,64},{64,128},{128,192},{192,256},{256,320},{320,384},{384,448},... | collective-permute-start | bytes 3145736 | tf_op jit(solution)/shard_map/ppermute | solution.py:133
  204.2 2.0 broadcast_in_dim.20
  206.2 8.1 %all-to-all-start.3 = ((bf16[64,2,4096]{2,1,0:T(2,128)(2,1)}), bf16[64,2,4096]{2,1,0:T(2,128)(2,1)S(1)}, u32[]{:S(2)}, u32[]{:S(2)}) async-start(bf16[64,2,4096]{2,1,0:T(2,128)(2,1)} %broadcast_in_dim.20), calls=%async_computation.3 | async-start | bytes 2097152 | tf_op jit(solution)/shard_map/all_to_all | solution.py:36
  214.3 5.2 %collective-permute-start.4 = (bf16[128,4096]{1,0:T(8,128)(2,1)S(1)}, bf16[128,4096]{1,0:T(8,128)(2,1)}, u32[]{:S(2)}, u32[]{:S(2)}) collective-permute-start(bf16[128,4096]{1,0:T(8,128)(2,1)S(1)} %copy-done.2), channel_id=1, source_target_pairs={{0,65},{1,66},{2,67},{3,68},{4,69},{5,70},{6,71},{7,72},{8,73},{9,... | collective-permute-start | bytes 3145736 | tf_op jit(solution)/shard_map/ppermute | solution.py:139
  219.5 10.8 %collective-permute-done.3 = bf16[128,4096]{1,0:T(8,128)(2,1)} collective-permute-done((bf16[128,4096]{1,0:T(8,128)(2,1)S(1)}, bf16[128,4096]{1,0:T(8,128)(2,1)}, u32[]{:S(2)}, u32[]{:S(2)}) %collective-permute-start.3) | collective-permute-done | bytes 1048608 | tf_op jit(solution)/shard_map/ppermute | solution.py:133
  230.3 2.3 broadcast_select_fusion.4.q_ref.k0_ref
  232.7 22.0 %collective-permute-done.4 = bf16[128,4096]{1,0:T(8,128)(2,1)} collective-permute-done((bf16[128,4096]{1,0:T(8,128)(2,1)S(1)}, bf16[128,4096]{1,0:T(8,128)(2,1)}, u32[]{:S(2)}, u32[]{:S(2)}) %collective-permute-start.4) | collective-permute-done | bytes 1048608 | tf_op jit(solution)/shard_map/ppermute | solution.py:139
  254.6 2.3 broadcast_select_fusion.k1_ref
  257.0 1.2 reshape.24.k3_ref
  258.2 16.4 %shard_map.74 = bf16[128,4096]{1,0:T(8,128)(2,1)} custom-call(s32[5]{0:T(128)} %pad_add_fusion.meta_ref, bf16[128,4096]{1,0:T(8,128)(2,1)} %broadcast_select_fusion.4.q_ref.k0_ref, bf16[128,4096]{1,0:T(8,128)(2,1)} %broadcast_select_fusion.4.q_ref.k0_ref, bf16[128,4096]{1,0:T(8,128)(2,1)} %broadcast_select_fusion.k1_ref, ...), custom_call_target="tpu_custom_call" | custom-call | tf_op jit(solution)/shard_map/pallas_call | solution.py:85
  (16 shorter events, 0.2 us)
Async XLA Ops:
  3.9 11.3 %copy-start = (bf16[1,128,4096]{2,1,0:T(8,128)(2,1)S(1)}, bf16[1,128,4096]{2,1,0:T(8,128)(2,1)}, u32[]{:S(2)}) copy-start(bf16[1,128,4096]{2,1,0:T(8,128)(2,1)} %param.8) | copy-start | bytes 3145732
  3.9 11.3 %copy-start.1 = (bf16[128,4096]{1,0:T(8,128)(2,1)S(1)}, bf16[128,4096]{1,0:T(8,128)(2,1)}, u32[]{:S(2)}) copy-start(bf16[128,4096]{1,0:T(8,128)(2,1)} %param.9) | copy-start | bytes 3145732
  3.9 11.3 %copy-start.3 = (bf16[1,128,4096]{2,1,0:T(8,128)(2,1)S(1)}, bf16[1,128,4096]{2,1,0:T(8,128)(2,1)}, u32[]{:S(2)}) copy-start(bf16[1,128,4096]{2,1,0:T(8,128)(2,1)} %param.7) | copy-start | bytes 3145732
  3.9 60.5 %all-to-all-start = ((bf16[64,4,4096]{2,1,0:T(4,128)(2,1)}), bf16[64,4,4096]{2,1,0:T(4,128)(2,1)}, u32[]{:S(2)}, u32[]{:S(2)}) async-start(bf16[64,4,4096]{2,1,0:T(4,128)(2,1)} %reshape.21), calls=%async_computation | async-start | bytes 4194304 | tf_op jit(solution)/shard_map/all_to_all | solution.py:29
  15.2 3.5 %copy-start.5 = (s32[64,4]{0,1:T(4,128)S(1)}, s32[64,4]{0,1:T(4,128)}, u32[]{:S(2)}) copy-start(s32[64,4]{0,1:T(4,128)} %param.10) | copy-start | bytes 3076
  16.7 58.2 %collective-permute-start = (bf16[128,4096]{1,0:T(8,128)(2,1)}, bf16[128,4096]{1,0:T(8,128)(2,1)S(1)}, u32[]{:S(2)}, u32[]{:S(2)}) collective-permute-start(bf16[128,4096]{1,0:T(8,128)(2,1)} %get-tuple-element.22), channel_id=1, source_target_pairs={{0,1},{1,2},{2,3},{3,4},{4,5},{5,6},{6,7},{7,8},{8,9},{9,10},{10,1... | collective-permute-start | bytes 3145736 | tf_op jit(solution)/shard_map/ppermute | solution.py:22
  74.9 2.4 copy-start.4
  77.3 56.8 %all-to-all-start.1 = ((bf16[64,4,4096]{2,1,0:T(4,128)(2,1)}), bf16[64,4,4096]{2,1,0:T(4,128)(2,1)S(1)}, u32[]{:S(2)}, u32[]{:S(2)}) async-start(bf16[64,4,4096]{2,1,0:T(4,128)(2,1)} %broadcast_in_dim.18), calls=%async_computation.1 | async-start | bytes 4194304 | tf_op jit(solution)/shard_map/all_to_all | solution.py:36
  136.2 22.4 %collective-permute-start.1 = (bf16[128,4096]{1,0:T(8,128)(2,1)}, bf16[128,4096]{1,0:T(8,128)(2,1)}, u32[]{:S(2)}, u32[]{:S(2)}) collective-permute-start(bf16[128,4096]{1,0:T(8,128)(2,1)} %get-tuple-element.16), channel_id=1, source_target_pairs={{0,1},{1,2},{2,3},{3,4},{4,5},{5,6},{6,7},{7,8},{8,9},{9,10},{10,1... | collective-permute-start | bytes 3145736 | tf_op jit(solution)/shard_map/ppermute | solution.py:22
  158.5 41.4 %copy-start.2 = (bf16[128,4096]{1,0:T(8,128)(2,1)S(1)}, bf16[128,4096]{1,0:T(8,128)(2,1)}, u32[]{:S(2)}) copy-start(bf16[128,4096]{1,0:T(8,128)(2,1)} %shard_map.73) | copy-start | bytes 3145732
  160.0 34.1 %all-to-all-start.2 = ((bf16[64,2,4096]{2,1,0:T(2,128)(2,1)}), bf16[64,2,4096]{2,1,0:T(2,128)(2,1)S(1)}, u32[]{:S(2)}, u32[]{:S(2)}) async-start(bf16[64,2,4096]{2,1,0:T(2,128)(2,1)} %reshape.23), calls=%async_computation.2 | async-start | bytes 2097152 | tf_op jit(solution)/shard_map/all_to_all | solution.py:29
  194.2 5.7 %collective-permute-start.2 = (bf16[1,2,4096]{2,1,0:T(2,128)(2,1)S(1)}, bf16[1,2,4096]{2,1,0:T(2,128)(2,1)S(1)}, u32[]{:S(2)}, u32[]{:S(2)}) collective-permute-start(bf16[1,2,4096]{2,1,0:T(2,128)(2,1)S(1)} %constant_dynamic-slice_fusion), channel_id=1, source_target_pairs={{0,64},{64,128},{128,192},{192,256},{256,320},{320,384},{384,448},... | collective-permute-start | bytes 49160 | tf_op jit(solution)/shard_map/ppermute | solution.py:22
  199.9 30.4 %collective-permute-start.3 = (bf16[128,4096]{1,0:T(8,128)(2,1)S(1)}, bf16[128,4096]{1,0:T(8,128)(2,1)}, u32[]{:S(2)}, u32[]{:S(2)}) collective-permute-start(bf16[128,4096]{1,0:T(8,128)(2,1)S(1)} %copy-done.2), channel_id=1, source_target_pairs={{0,64},{64,128},{128,192},{192,256},{256,320},{320,384},{384,448},... | collective-permute-start | bytes 3145736 | tf_op jit(solution)/shard_map/ppermute | solution.py:133
  206.2 50.8 %all-to-all-start.3 = ((bf16[64,2,4096]{2,1,0:T(2,128)(2,1)}), bf16[64,2,4096]{2,1,0:T(2,128)(2,1)S(1)}, u32[]{:S(2)}, u32[]{:S(2)}) async-start(bf16[64,2,4096]{2,1,0:T(2,128)(2,1)} %broadcast_in_dim.20), calls=%async_computation.3 | async-start | bytes 2097152 | tf_op jit(solution)/shard_map/all_to_all | solution.py:36
  214.3 40.4 %collective-permute-start.4 = (bf16[128,4096]{1,0:T(8,128)(2,1)S(1)}, bf16[128,4096]{1,0:T(8,128)(2,1)}, u32[]{:S(2)}, u32[]{:S(2)}) collective-permute-start(bf16[128,4096]{1,0:T(8,128)(2,1)S(1)} %copy-done.2), channel_id=1, source_target_pairs={{0,65},{1,66},{2,67},{3,68},{4,69},{5,70},{6,71},{7,72},{8,73},{9,... | collective-permute-start | bytes 3145736 | tf_op jit(solution)/shard_map/ppermute | solution.py:139

commit v6 on v5

--- a/solution.py
+++ b/solution.py
@@ -13,7 +13,7 @@
 NR = 1
 WIDTH = 4096
 NSEL = 4
-GROUP = 4
+GROUP = 8
 
 
 def shifted(value, axis, steps):
@@ -113,9 +113,13 @@
     first_current = span_inputs[0]
     root = full_entries[LOCAL] % group_size
     piece_one = scatter_piece(jnp.concatenate([first_earlier, first_current]), "ctx", root)
-    previous_one = shifted(jnp.where(last, first_earlier, first_current), "ctx", 1)
-    piece_one, previous_one = lax.optimization_barrier((piece_one, previous_one))
+    behind = jnp.where(last, first_earlier, first_current)
+    front = shifted(behind[: BLOCK // 2], "ctx", 1)
+    piece_one, front = lax.optimization_barrier((piece_one, front))
+    back = shifted(behind[BLOCK // 2 :], "ctx", 1)
     both = gather_pieces(piece_one, "ctx")
+    both, back = lax.optimization_barrier((both, back))
+    previous_one = jnp.concatenate([front, back])
     held, both = lax.optimization_barrier((jnp.where(last, first_current, next_inputs), both))
     previous_early = shifted(held, "ctx", 1)
 

time: 275 us -> 273 us (level)
  waiting for transfers between devices: 160 us -> 155 us
    ppermute x3 -> x4, waiting for transfers between devices: 11.2 us -> 8.7 us  [shifted(): return lax.ppermute(value, axis, pairs)]
    ppermute x3 -> x4, starting transfers between devices: 10.3 us -> 10.2 us  [shifted(): return lax.ppermute(value, axis, pairs)]
  transfers between devices with their start and end apart: 9 -> 10, of which waited for: 7 -> 8; matrix products, arithmetic and copies ran while one was open for 4% -> 6% of each run, Pallas kernels for 6% -> 6%
where the time goes in v6:
time: 273 us; the launch traced here: 272 us
  waiting for transfers between devices  155 us (57%)
  starting transfers between devices  56.8 us (21%)
  Pallas kernels  31 us (11%)
  local copies, waits for them, and re-layouts  13.8 us (5%)
  other arithmetic  11.7 us (4%)
  between operations  3.74 us (1%)
    all_to_all x2, waiting for transfers between devices, scatter_piece(): received = lax.all_to_all(pieces, axis, 0, 0, tiled=True)  67.5 us
    all_to_all x2, waiting for transfers between devices, gather_pieces(): lax.all_to_all(jnp.broadcast_to(piece, shape), axis, 0, 0, tiled=True)  46.4 us
    pallas_call x2, Pallas kernels, attend_pallas(): pl.pallas_call(attend_kernel, grid_spec=grid_spec, out_shape=jax.ShapeDty...  31 us
    ppermute x1, waiting for transfers between devices, local(): received_previous = lax.ppermute(outgoing, ('section', 'ctx'), diagonal)  22 us
    all_to_all x2, starting transfers between devices, scatter_piece(): received = lax.all_to_all(pieces, axis, 0, 0, tiled=True)  20.8 us
    all_to_all x2, starting transfers between devices, gather_pieces(): lax.all_to_all(jnp.broadcast_to(piece, shape), axis, 0, 0, tiled=True)  16 us
    ppermute x1, waiting for transfers between devices, local(): received = lax.ppermute(outgoing, 'section', straight)  10.6 us
    ppermute x4, starting transfers between devices, shifted(): return lax.ppermute(value, axis, pairs)  10.2 us
  transfers between devices with their start and end apart: 10, of which 8 were waited for; matrix products, arithmetic and copies ran while one was open for 6% of the time, Pallas kernels for 6%

profile of v6, /device:TPU:70, one launch (start us, length us, event | category | flops | bytes accessed | tf_op | source)
XLA Modules:
  0.0 272.3 jit_solution(4806350068912400965)
XLA Ops:
  0.0 1.7 pad_maximum_fusion
  1.7 2.2 reshape.21
  3.9 11.3 %all-to-all-start = ((bf16[64,4,4096]{2,1,0:T(4,128)(2,1)}), bf16[64,4,4096]{2,1,0:T(4,128)(2,1)}, u32[]{:S(2)}, u32[]{:S(2)}) async-start(bf16[64,4,4096]{2,1,0:T(4,128)(2,1)} %reshape.21), calls=%async_computation | async-start | bytes 4194304 | tf_op jit(solution)/shard_map/all_to_all | solution.py:29
  15.2 1.1 broadcast_select_fusion.2
  17.2 2.0 collective-permute-start
  21.5 42.8 %all-to-all-done = bf16[64,4,4096]{2,1,0:T(4,128)(2,1)} async-done(((bf16[64,4,4096]{2,1,0:T(4,128)(2,1)}), bf16[64,4,4096]{2,1,0:T(4,128)(2,1)}, u32[]{:S(2)}, u32[]{:S(2)}) %all-to-all-start) | async-done | bytes 2097184 | tf_op jit(solution)/shard_map/all_to_all | solution.py:29
  65.1 4.2 %collective-permute-done = bf16[64,4096]{1,0:T(8,128)(2,1)S(1)} collective-permute-done((bf16[64,4096]{1,0:T(8,128)(2,1)S(1)}, bf16[64,4096]{1,0:T(8,128)(2,1)S(1)}, u32[]{:S(2)}, u32[]{:S(2)}) %collective-permute-start) | collective-permute-done | bytes 524320 | tf_op jit(solution)/shard_map/ppermute | solution.py:22
  69.3 2.4 broadcast_in_dim.18
  71.6 7.9 %all-to-all-start.1 = ((bf16[64,4,4096]{2,1,0:T(4,128)(2,1)}), bf16[64,4,4096]{2,1,0:T(4,128)(2,1)S(1)}, u32[]{:S(2)}, u32[]{:S(2)}) async-start(bf16[64,4,4096]{2,1,0:T(4,128)(2,1)} %broadcast_in_dim.18), calls=%async_computation.1 | async-start | bytes 4194304 | tf_op jit(solution)/shard_map/all_to_all | solution.py:36
  79.6 2.0 collective-permute-start.1
  82.4 46.4 %all-to-all-done.1 = bf16[64,4,4096]{2,1,0:T(4,128)(2,1)S(1)} async-done(((bf16[64,4,4096]{2,1,0:T(4,128)(2,1)}), bf16[64,4,4096]{2,1,0:T(4,128)(2,1)S(1)}, u32[]{:S(2)}, u32[]{:S(2)}) %all-to-all-start.1) | async-done | bytes 2097184 | tf_op jit(solution)/shard_map/all_to_all | solution.py:36
  128.9 2.1 reshape.22.k2_ref.k3_ref
  130.9 3.1 %collective-permute-done.1 = bf16[64,4096]{1,0:T(8,128)(2,1)} collective-permute-done((bf16[64,4096]{1,0:T(8,128)(2,1)}, bf16[64,4096]{1,0:T(8,128)(2,1)}, u32[]{:S(2)}, u32[]{:S(2)}) %collective-permute-start.1) | collective-permute-done | bytes 524320 | tf_op jit(solution)/shard_map/ppermute | solution.py:22
  134.0 1.9 collective-permute-start.2
  135.9 2.3 pad_maximum_fusion.1.k1_ref
  138.2 15.5 %shard_map.73 = bf16[128,4096]{1,0:T(8,128)(2,1)} custom-call(s32[5]{0:T(128)} %pad_add_fusion.meta_ref, bf16[128,4096]{1,0:T(8,128)(2,1)} %bitcast.12, bf16[128,4096]{1,0:T(8,128)(2,1)} %bitcast.13, bf16[128,4096]{1,0:T(8,128)(2,1)} %pad_maximum_fusion.1.k1_ref, bf16[256,4096]{1,0:T(8,128)(2,1)} %reshape.22.k2_ref.k3_ref, ...), custom_call_target="tpu_custom_call" | custom-call | tf_op jit(solution)/shard_map/pallas_call | solution.py:85
  153.7 1.3 broadcast_select_fusion.1
  155.0 1.5 reshape.23
  156.5 9.6 %all-to-all-start.2 = ((bf16[64,2,4096]{2,1,0:T(2,128)(2,1)}), bf16[64,2,4096]{2,1,0:T(2,128)(2,1)S(1)}, u32[]{:S(2)}, u32[]{:S(2)}) async-start(bf16[64,2,4096]{2,1,0:T(2,128)(2,1)} %reshape.23), calls=%async_computation.2 | async-start | bytes 2097152 | tf_op jit(solution)/shard_map/all_to_all | solution.py:29
  168.0 24.7 %all-to-all-done.2 = bf16[64,2,4096]{2,1,0:T(2,128)(2,1)S(1)} async-done(((bf16[64,2,4096]{2,1,0:T(2,128)(2,1)}), bf16[64,2,4096]{2,1,0:T(2,128)(2,1)S(1)}, u32[]{:S(2)}, u32[]{:S(2)}) %all-to-all-start.2) | async-done | bytes 1048608 | tf_op jit(solution)/shard_map/all_to_all | solution.py:29
  192.8 4.3 %collective-permute-start.3 = (bf16[1,2,4096]{2,1,0:T(2,128)(2,1)S(1)}, bf16[1,2,4096]{2,1,0:T(2,128)(2,1)S(1)}, u32[]{:S(2)}, u32[]{:S(2)}) collective-permute-start(bf16[1,2,4096]{2,1,0:T(2,128)(2,1)S(1)} %constant_dynamic-slice_fusion), channel_id=1, source_target_pairs={{0,64},{64,128},{128,192},{192,256},{256,320},{320,384},{384,448},... | collective-permute-start | bytes 49160 | tf_op jit(solution)/shard_map/ppermute | solution.py:22
  197.1 1.4 collective-permute-done.3
  198.5 4.3 %collective-permute-start.4 = (bf16[128,4096]{1,0:T(8,128)(2,1)S(1)}, bf16[128,4096]{1,0:T(8,128)(2,1)}, u32[]{:S(2)}, u32[]{:S(2)}) collective-permute-start(bf16[128,4096]{1,0:T(8,128)(2,1)S(1)} %copy-done.2), channel_id=1, source_target_pairs={{0,64},{64,128},{128,192},{192,256},{256,320},{320,384},{384,448},... | collective-permute-start | bytes 3145736 | tf_op jit(solution)/shard_map/ppermute | solution.py:137
  202.8 2.0 broadcast_in_dim.20
  204.7 8.1 %all-to-all-start.3 = ((bf16[64,2,4096]{2,1,0:T(2,128)(2,1)}), bf16[64,2,4096]{2,1,0:T(2,128)(2,1)S(1)}, u32[]{:S(2)}, u32[]{:S(2)}) async-start(bf16[64,2,4096]{2,1,0:T(2,128)(2,1)} %broadcast_in_dim.20), calls=%async_computation.3 | async-start | bytes 2097152 | tf_op jit(solution)/shard_map/all_to_all | solution.py:36
  212.8 5.4 %collective-permute-start.5 = (bf16[128,4096]{1,0:T(8,128)(2,1)S(1)}, bf16[128,4096]{1,0:T(8,128)(2,1)}, u32[]{:S(2)}, u32[]{:S(2)}) collective-permute-start(bf16[128,4096]{1,0:T(8,128)(2,1)S(1)} %copy-done.2), channel_id=1, source_target_pairs={{0,65},{1,66},{2,67},{3,68},{4,69},{5,70},{6,71},{7,72},{8,73},{9,... | collective-permute-start | bytes 3145736 | tf_op jit(solution)/shard_map/ppermute | solution.py:143
  218.3 10.6 %collective-permute-done.4 = bf16[128,4096]{1,0:T(8,128)(2,1)} collective-permute-done((bf16[128,4096]{1,0:T(8,128)(2,1)S(1)}, bf16[128,4096]{1,0:T(8,128)(2,1)}, u32[]{:S(2)}, u32[]{:S(2)}) %collective-permute-start.4) | collective-permute-done | bytes 1048608 | tf_op jit(solution)/shard_map/ppermute | solution.py:137
  228.9 2.3 broadcast_select_fusion.4.q_ref.k0_ref
  231.2 22.0 %collective-permute-done.5 = bf16[128,4096]{1,0:T(8,128)(2,1)} collective-permute-done((bf16[128,4096]{1,0:T(8,128)(2,1)S(1)}, bf16[128,4096]{1,0:T(8,128)(2,1)}, u32[]{:S(2)}, u32[]{:S(2)}) %collective-permute-start.5) | collective-permute-done | bytes 1048608 | tf_op jit(solution)/shard_map/ppermute | solution.py:143
  253.2 2.3 broadcast_select_fusion.k1_ref
  255.6 1.2 reshape.24.k3_ref
  256.8 15.5 %shard_map.74 = bf16[128,4096]{1,0:T(8,128)(2,1)} custom-call(s32[5]{0:T(128)} %pad_add_fusion.meta_ref, bf16[128,4096]{1,0:T(8,128)(2,1)} %broadcast_select_fusion.4.q_ref.k0_ref, bf16[128,4096]{1,0:T(8,128)(2,1)} %broadcast_select_fusion.4.q_ref.k0_ref, bf16[128,4096]{1,0:T(8,128)(2,1)} %broadcast_select_fusion.k1_ref, ...), custom_call_target="tpu_custom_call" | custom-call | tf_op jit(solution)/shard_map/pallas_call | solution.py:85
  (20 shorter events, 3.1 us)
Async XLA Ops:
  3.9 11.3 %copy-start = (bf16[1,128,4096]{2,1,0:T(8,128)(2,1)S(1)}, bf16[1,128,4096]{2,1,0:T(8,128)(2,1)}, u32[]{:S(2)}) copy-start(bf16[1,128,4096]{2,1,0:T(8,128)(2,1)} %param.8) | copy-start | bytes 3145732
  3.9 11.3 %copy-start.1 = (bf16[128,4096]{1,0:T(8,128)(2,1)S(1)}, bf16[128,4096]{1,0:T(8,128)(2,1)}, u32[]{:S(2)}) copy-start(bf16[128,4096]{1,0:T(8,128)(2,1)} %param.9) | copy-start | bytes 3145732
  3.9 11.3 %copy-start.3 = (bf16[1,128,4096]{2,1,0:T(8,128)(2,1)S(1)}, bf16[1,128,4096]{2,1,0:T(8,128)(2,1)}, u32[]{:S(2)}) copy-start(bf16[1,128,4096]{2,1,0:T(8,128)(2,1)} %param.7) | copy-start | bytes 3145732
  3.9 60.5 %all-to-all-start = ((bf16[64,4,4096]{2,1,0:T(4,128)(2,1)}), bf16[64,4,4096]{2,1,0:T(4,128)(2,1)}, u32[]{:S(2)}, u32[]{:S(2)}) async-start(bf16[64,4,4096]{2,1,0:T(4,128)(2,1)} %reshape.21), calls=%async_computation | async-start | bytes 4194304 | tf_op jit(solution)/shard_map/all_to_all | solution.py:29
  16.3 2.9 %copy-start.5 = (s32[64,4]{0,1:T(4,128)S(1)}, s32[64,4]{0,1:T(4,128)}, u32[]{:S(2)}) copy-start(s32[64,4]{0,1:T(4,128)} %param.10) | copy-start | bytes 3076
  17.2 52.1 %collective-permute-start = (bf16[64,4096]{1,0:T(8,128)(2,1)S(1)}, bf16[64,4096]{1,0:T(8,128)(2,1)S(1)}, u32[]{:S(2)}, u32[]{:S(2)}) collective-permute-start(bf16[64,4096]{1,0:T(8,128)(2,1)S(1)} %get-tuple-element.28), channel_id=1, source_target_pairs={{0,1},{1,2},{2,3},{3,4},{4,5},{5,6},{6,7},{7,8},{8,9},{9,10},{10,1... | collective-permute-start | bytes 1572872 | tf_op jit(solution)/shard_map/ppermute | solution.py:22
  69.3 2.4 copy-start.4
  71.6 57.2 %all-to-all-start.1 = ((bf16[64,4,4096]{2,1,0:T(4,128)(2,1)}), bf16[64,4,4096]{2,1,0:T(4,128)(2,1)S(1)}, u32[]{:S(2)}, u32[]{:S(2)}) async-start(bf16[64,4,4096]{2,1,0:T(4,128)(2,1)} %broadcast_in_dim.18), calls=%async_computation.1 | async-start | bytes 4194304 | tf_op jit(solution)/shard_map/all_to_all | solution.py:36
  79.6 54.4 %collective-permute-start.1 = (bf16[64,4096]{1,0:T(8,128)(2,1)}, bf16[64,4096]{1,0:T(8,128)(2,1)}, u32[]{:S(2)}, u32[]{:S(2)}) collective-permute-start(bf16[64,4096]{1,0:T(8,128)(2,1)} %get-tuple-element.27), channel_id=1, source_target_pairs={{0,1},{1,2},{2,3},{3,4},{4,5},{5,6},{6,7},{7,8},{8,9},{9,10},{10,1... | collective-permute-start | bytes 1572872 | tf_op jit(solution)/shard_map/ppermute | solution.py:22
  134.0 21.0 %collective-permute-start.2 = (bf16[128,4096]{1,0:T(8,128)(2,1)}, bf16[128,4096]{1,0:T(8,128)(2,1)}, u32[]{:S(2)}, u32[]{:S(2)}) collective-permute-start(bf16[128,4096]{1,0:T(8,128)(2,1)} %get-tuple-element.20), channel_id=1, source_target_pairs={{0,1},{1,2},{2,3},{3,4},{4,5},{5,6},{6,7},{7,8},{8,9},{9,10},{10,1... | collective-permute-start | bytes 3145736 | tf_op jit(solution)/shard_map/ppermute | solution.py:22
  155.0 43.5 %copy-start.2 = (bf16[128,4096]{1,0:T(8,128)(2,1)S(1)}, bf16[128,4096]{1,0:T(8,128)(2,1)}, u32[]{:S(2)}) copy-start(bf16[128,4096]{1,0:T(8,128)(2,1)} %shard_map.73) | copy-start | bytes 3145732
  156.5 36.2 %all-to-all-start.2 = ((bf16[64,2,4096]{2,1,0:T(2,128)(2,1)}), bf16[64,2,4096]{2,1,0:T(2,128)(2,1)S(1)}, u32[]{:S(2)}, u32[]{:S(2)}) async-start(bf16[64,2,4096]{2,1,0:T(2,128)(2,1)} %reshape.23), calls=%async_computation.2 | async-start | bytes 2097152 | tf_op jit(solution)/shard_map/all_to_all | solution.py:29
  192.8 5.7 %collective-permute-start.3 = (bf16[1,2,4096]{2,1,0:T(2,128)(2,1)S(1)}, bf16[1,2,4096]{2,1,0:T(2,128)(2,1)S(1)}, u32[]{:S(2)}, u32[]{:S(2)}) collective-permute-start(bf16[1,2,4096]{2,1,0:T(2,128)(2,1)S(1)} %constant_dynamic-slice_fusion), channel_id=1, source_target_pairs={{0,64},{64,128},{128,192},{192,256},{256,320},{320,384},{384,448},... | collective-permute-start | bytes 49160 | tf_op jit(solution)/shard_map/ppermute | solution.py:22
  198.5 30.4 %collective-permute-start.4 = (bf16[128,4096]{1,0:T(8,128)(2,1)S(1)}, bf16[128,4096]{1,0:T(8,128)(2,1)}, u32[]{:S(2)}, u32[]{:S(2)}) collective-permute-start(bf16[128,4096]{1,0:T(8,128)(2,1)S(1)} %copy-done.2), channel_id=1, source_target_pairs={{0,64},{64,128},{128,192},{192,256},{256,320},{320,384},{384,448},... | collective-permute-start | bytes 3145736 | tf_op jit(solution)/shard_map/ppermute | solution.py:137
  204.7 50.8 %all-to-all-start.3 = ((bf16[64,2,4096]{2,1,0:T(2,128)(2,1)}), bf16[64,2,4096]{2,1,0:T(2,128)(2,1)S(1)}, u32[]{:S(2)}, u32[]{:S(2)}) async-start(bf16[64,2,4096]{2,1,0:T(2,128)(2,1)} %broadcast_in_dim.20), calls=%async_computation.3 | async-start | bytes 2097152 | tf_op jit(solution)/shard_map/all_to_all | solution.py:36
  212.8 40.4 %collective-permute-start.5 = (bf16[128,4096]{1,0:T(8,128)(2,1)S(1)}, bf16[128,4096]{1,0:T(8,128)(2,1)}, u32[]{:S(2)}, u32[]{:S(2)}) collective-permute-start(bf16[128,4096]{1,0:T(8,128)(2,1)S(1)} %copy-done.2), channel_id=1, source_target_pairs={{0,65},{1,66},{2,67},{3,68},{4,69},{5,70},{6,71},{7,72},{8,73},{9,... | collective-permute-start | bytes 3145736 | tf_op jit(solution)/shard_map/ppermute | solution.py:143

commit v7 on v6

--- a/solution.py
+++ b/solution.py
@@ -37,8 +37,15 @@
     return gathered.reshape(count * piece.shape[1], piece.shape[2])
 
 
-def attend_kernel(meta_ref, q_ref, k0_ref, k1_ref, k2_ref, k3_ref, gq_ref, gk_ref, go_ref, out_ref):
-    key_refs = (k0_ref, k1_ref, k2_ref, k3_ref)
+def attend_kernel(meta_ref, q_ref, k0_ref, k1a_ref, k1b_ref, k2_ref, k3_ref, gq_ref, gk_ref, go_ref, out_ref):
+    key_refs = (k0_ref, (k1a_ref, k1b_ref), k2_ref, k3_ref)
+
+    def key_rows(b, lanes):
+        ref = key_refs[b]
+        if isinstance(ref, tuple):
+            return jnp.concatenate([part[:, lanes] for part in ref], axis=0)
+        return ref[:, lanes]
+
     global_block = meta_ref[NSEL]
     query_pos = lax.broadcasted_iota(jnp.int32, (BLOCK, BLOCK), 0)
     key_pos = lax.broadcasted_iota(jnp.int32, (BLOCK, BLOCK), 1)
@@ -52,8 +59,9 @@
         normed = rows * lax.rsqrt(jnp.mean(rows * rows, axis=-1, keepdims=True) + 1e-06)
         queries = (normed * gq_ref[:, lanes] * HD ** (-0.5)).astype(jnp.bfloat16)
         scores = []
+        values = [key_rows(b, lanes) for b in range(NSEL)]
         for b in range(NSEL):
-            raw_keys = key_refs[b][:, lanes]
+            raw_keys = values[b]
             wide = raw_keys.astype(jnp.float32)
             keys = (wide * lax.rsqrt(jnp.mean(wide * wide, axis=-1, keepdims=True) + 1e-06) * gk_ref[:, lanes]).astype(jnp.bfloat16)
             s = lax.dot_general(queries, keys, (((1,), (1,)), ((), ())), preferred_element_type=jnp.float32)
@@ -63,7 +71,7 @@
         totals = functools.reduce(jnp.add, [jnp.sum(r, axis=-1, keepdims=True) for r in raws])
         context = None
         for b in range(NSEL):
-            part = jnp.dot(raws[b].astype(jnp.bfloat16), key_refs[b][:, lanes], preferred_element_type=jnp.float32)
+            part = jnp.dot(raws[b].astype(jnp.bfloat16), values[b], preferred_element_type=jnp.float32)
             context = part if context is None else context + part
         out_ref[:, lanes] = (rows + go_ref[:, lanes] * (context / totals)).astype(jnp.bfloat16)
 
@@ -72,14 +80,14 @@
     meta = jnp.concatenate([entries.astype(jnp.int32), jnp.reshape(global_block, (1,)).astype(jnp.int32)])
     lanes = GROUP * HD
 
-    def row_spec(block):
-        return pl.BlockSpec((BLOCK, lanes), lambda g, meta: (block, g))
+    def row_spec(block, rows=BLOCK):
+        return pl.BlockSpec((rows, lanes), lambda g, meta: (block, g))
 
     gain_spec = pl.BlockSpec((1, lanes), lambda g, meta: (0, g))
     grid_spec = pltpu.PrefetchScalarGridSpec(
         num_scalar_prefetch=1,
         grid=(HEADS // GROUP,),
-        in_specs=[row_spec(0)] + [row_spec(block) for _, block in key_blocks] + [gain_spec] * 3,
+        in_specs=[row_spec(0)] + [row_spec(block, rows) for _, block, rows in key_blocks] + [gain_spec] * 3,
         out_specs=row_spec(0),
     )
     return pl.pallas_call(
@@ -89,7 +97,7 @@
     )(
         meta,
         query_rows,
-        *[array for array, _ in key_blocks],
+        *[array for array, _, _ in key_blocks],
         gain_query.reshape(1, WIDTH),
         gain_key.reshape(1, WIDTH),
         gain_out.reshape(1, WIDTH),
@@ -119,11 +127,17 @@
     back = shifted(behind[BLOCK // 2 :], "ctx", 1)
     both = gather_pieces(piece_one, "ctx")
     both, back = lax.optimization_barrier((both, back))
-    previous_one = jnp.concatenate([front, back])
     held, both = lax.optimization_barrier((jnp.where(last, first_current, next_inputs), both))
     previous_early = shifted(held, "ctx", 1)
 
-    key_one = ((first_current, 0), (previous_one, 0), (both, 0), (both, 1))
+    half = BLOCK // 2
+    key_one = (
+        (first_current, 0, BLOCK),
+        (front, 0, half),
+        (back, 0, half),
+        (both, 0, BLOCK),
+        (both, 1, BLOCK),
+    )
     first_result = attend_pallas(
         first_current, key_one, query_entries, global_block, gain_query, gain_key, gain_out
     )
@@ -146,7 +160,13 @@
     previous_two = jnp.where(
         (position == 0) | (section_pos == 0), previous_early, received_previous
     )
-    key_two = ((second_current, 0), (previous_two, 0), (both, 1), (strided_later, 0))
+    key_two = (
+        (second_current, 0, BLOCK),
+        (previous_two, 0, half),
+        (previous_two, 1, half),
+        (both, 1, BLOCK),
+        (strided_later, 0, BLOCK),
+    )
     second_result = attend_pallas(
         second_current, key_two, query_entries, global_block, gain_query, gain_key, gain_out
     )

time: 273 us -> 272 us (level)
  transfers between devices with their start and end apart: 10 -> 10, of which waited for: 8 -> 8; matrix products, arithmetic and copies ran while one was open for 6% -> 5% of each run, Pallas kernels for 6% -> 6%
where the time goes in v7:
time: 272 us; the launch traced here: 271 us
  waiting for transfers between devices  156 us (57%)
  starting transfers between devices  56.8 us (21%)
  Pallas kernels  31.1 us (11%)
  local copies, waits for them, and re-layouts  13.8 us (5%)
  other arithmetic  9.42 us (3%)
  between operations  3.74 us (1%)
    all_to_all x2, waiting for transfers between devices, scatter_piece(): received = lax.all_to_all(pieces, axis, 0, 0, tiled=True)  67.5 us
    all_to_all x2, waiting for transfers between devices, gather_pieces(): lax.all_to_all(jnp.broadcast_to(piece, shape), axis, 0, 0, tiled=True)  47.1 us
    pallas_call x2, Pallas kernels, attend_pallas(): pl.pallas_call(attend_kernel, grid_spec=grid_spec, out_shape=jax.ShapeDty...  31.1 us
    ppermute x1, waiting for transfers between devices, local(): received_previous = lax.ppermute(outgoing, ('section', 'ctx'), diagonal)  22 us
    all_to_all x2, starting transfers between devices, scatter_piece(): received = lax.all_to_all(pieces, axis, 0, 0, tiled=True)  20.8 us
    all_to_all x2, starting transfers between devices, gather_pieces(): lax.all_to_all(jnp.broadcast_to(piece, shape), axis, 0, 0, tiled=True)  16 us
    ppermute x1, waiting for transfers between devices, local(): received = lax.ppermute(outgoing, 'section', straight)  10.6 us
    ppermute x4, starting transfers between devices, shifted(): return lax.ppermute(value, axis, pairs)  10.2 us
  transfers between devices with their start and end apart: 10, of which 8 were waited for; matrix products, arithmetic and copies ran while one was open for 5% of the time, Pallas kernels for 6%

profile of v7, /device:TPU:70, one launch (start us, length us, event | category | flops | bytes accessed | tf_op | source)
XLA Modules:
  0.0 270.7 jit_solution(15364970824139046183)
XLA Ops:
  0.0 1.7 pad_maximum_fusion
  1.7 2.2 reshape.21
  3.9 11.3 %all-to-all-start = ((bf16[64,4,4096]{2,1,0:T(4,128)(2,1)}), bf16[64,4,4096]{2,1,0:T(4,128)(2,1)}, u32[]{:S(2)}, u32[]{:S(2)}) async-start(bf16[64,4,4096]{2,1,0:T(4,128)(2,1)} %reshape.21), calls=%async_computation | async-start | bytes 4194304 | tf_op jit(solution)/shard_map/all_to_all | solution.py:29
  15.2 1.1 broadcast_select_fusion.2
  16.3 0.9 fusion
  17.2 2.0 collective-permute-start
  21.5 42.8 %all-to-all-done = bf16[64,4,4096]{2,1,0:T(4,128)(2,1)} async-done(((bf16[64,4,4096]{2,1,0:T(4,128)(2,1)}), bf16[64,4,4096]{2,1,0:T(4,128)(2,1)}, u32[]{:S(2)}, u32[]{:S(2)}) %all-to-all-start) | async-done | bytes 2097184 | tf_op jit(solution)/shard_map/all_to_all | solution.py:29
  65.1 4.2 %collective-permute-done.k1a_ref = bf16[64,4096]{1,0:T(8,128)(2,1)S(1)} collective-permute-done((bf16[64,4096]{1,0:T(8,128)(2,1)S(1)}, bf16[64,4096]{1,0:T(8,128)(2,1)S(1)}, u32[]{:S(2)}, u32[]{:S(2)}) %collective-permute-start) | collective-permute-done | bytes 524320 | tf_op jit(solution)/shard_map/ppermute | solution.py:22
  69.3 2.4 broadcast_in_dim.18
  71.6 7.9 %all-to-all-start.1 = ((bf16[64,4,4096]{2,1,0:T(4,128)(2,1)}), bf16[64,4,4096]{2,1,0:T(4,128)(2,1)S(1)}, u32[]{:S(2)}, u32[]{:S(2)}) async-start(bf16[64,4,4096]{2,1,0:T(4,128)(2,1)} %broadcast_in_dim.18), calls=%async_computation.1 | async-start | bytes 4194304 | tf_op jit(solution)/shard_map/all_to_all | solution.py:36
  79.6 2.0 collective-permute-start.1
  81.8 47.0 %all-to-all-done.1 = bf16[64,4,4096]{2,1,0:T(4,128)(2,1)S(1)} async-done(((bf16[64,4,4096]{2,1,0:T(4,128)(2,1)}), bf16[64,4,4096]{2,1,0:T(4,128)(2,1)S(1)}, u32[]{:S(2)}, u32[]{:S(2)}) %all-to-all-start.1) | async-done | bytes 2097184 | tf_op jit(solution)/shard_map/all_to_all | solution.py:36
  128.9 2.1 reshape.22.k2_ref.k3_ref
  130.9 3.1 %collective-permute-done.1.k1b_ref = bf16[64,4096]{1,0:T(8,128)(2,1)} collective-permute-done((bf16[64,4096]{1,0:T(8,128)(2,1)}, bf16[64,4096]{1,0:T(8,128)(2,1)}, u32[]{:S(2)}, u32[]{:S(2)}) %collective-permute-start.1) | collective-permute-done | bytes 524320 | tf_op jit(solution)/shard_map/ppermute | solution.py:22
  134.0 1.9 collective-permute-start.2
  136.6 15.5 %shard_map.73 = bf16[128,4096]{1,0:T(8,128)(2,1)} custom-call(s32[5]{0:T(128)} %pad_add_fusion.meta_ref, bf16[128,4096]{1,0:T(8,128)(2,1)} %bitcast.12, bf16[128,4096]{1,0:T(8,128)(2,1)} %bitcast.13, bf16[64,4096]{1,0:T(8,128)(2,1)} %copy-done.4, bf16[64,4096]{1,0:T(8,128)(2,1)} %collective-permute-done.1.k1b_ref, bf16[256,4096]{1,0:T(8,128)(2,1)} %reshape.22.k2_ref.k3_ref, ...), custom_call_target="tpu_custom_call" | custom-call | tf_op jit(solution)/shard_map/pallas_call | solution.py:93
  152.1 1.3 broadcast_select_fusion.1
  153.4 1.5 reshape.23
  154.9 9.6 %all-to-all-start.2 = ((bf16[64,2,4096]{2,1,0:T(2,128)(2,1)}), bf16[64,2,4096]{2,1,0:T(2,128)(2,1)S(1)}, u32[]{:S(2)}, u32[]{:S(2)}) async-start(bf16[64,2,4096]{2,1,0:T(2,128)(2,1)} %reshape.23), calls=%async_computation.2 | async-start | bytes 2097152 | tf_op jit(solution)/shard_map/all_to_all | solution.py:29
  166.4 24.7 %all-to-all-done.2 = bf16[64,2,4096]{2,1,0:T(2,128)(2,1)S(1)} async-done(((bf16[64,2,4096]{2,1,0:T(2,128)(2,1)}), bf16[64,2,4096]{2,1,0:T(2,128)(2,1)S(1)}, u32[]{:S(2)}, u32[]{:S(2)}) %all-to-all-start.2) | async-done | bytes 1048608 | tf_op jit(solution)/shard_map/all_to_all | solution.py:29
  191.2 4.3 %collective-permute-start.3 = (bf16[1,2,4096]{2,1,0:T(2,128)(2,1)S(1)}, bf16[1,2,4096]{2,1,0:T(2,128)(2,1)S(1)}, u32[]{:S(2)}, u32[]{:S(2)}) collective-permute-start(bf16[1,2,4096]{2,1,0:T(2,128)(2,1)S(1)} %constant_dynamic-slice_fusion), channel_id=1, source_target_pairs={{0,64},{64,128},{128,192},{192,256},{256,320},{320,384},{384,448},... | collective-permute-start | bytes 49160 | tf_op jit(solution)/shard_map/ppermute | solution.py:22
  195.5 1.4 collective-permute-done.3
  196.9 4.3 %collective-permute-start.4 = (bf16[128,4096]{1,0:T(8,128)(2,1)S(1)}, bf16[128,4096]{1,0:T(8,128)(2,1)}, u32[]{:S(2)}, u32[]{:S(2)}) collective-permute-start(bf16[128,4096]{1,0:T(8,128)(2,1)S(1)} %copy-done.2), channel_id=1, source_target_pairs={{0,64},{64,128},{128,192},{192,256},{256,320},{320,384},{384,448},... | collective-permute-start | bytes 3145736 | tf_op jit(solution)/shard_map/ppermute | solution.py:151
  201.2 2.0 broadcast_in_dim.20
  203.2 8.1 %all-to-all-start.3 = ((bf16[64,2,4096]{2,1,0:T(2,128)(2,1)}), bf16[64,2,4096]{2,1,0:T(2,128)(2,1)S(1)}, u32[]{:S(2)}, u32[]{:S(2)}) async-start(bf16[64,2,4096]{2,1,0:T(2,128)(2,1)} %broadcast_in_dim.20), calls=%async_computation.3 | async-start | bytes 2097152 | tf_op jit(solution)/shard_map/all_to_all | solution.py:36
  211.3 5.4 %collective-permute-start.5 = (bf16[128,4096]{1,0:T(8,128)(2,1)S(1)}, bf16[128,4096]{1,0:T(8,128)(2,1)}, u32[]{:S(2)}, u32[]{:S(2)}) collective-permute-start(bf16[128,4096]{1,0:T(8,128)(2,1)S(1)} %copy-done.2), channel_id=1, source_target_pairs={{0,65},{1,66},{2,67},{3,68},{4,69},{5,70},{6,71},{7,72},{8,73},{9,... | collective-permute-start | bytes 3145736 | tf_op jit(solution)/shard_map/ppermute | solution.py:157
  216.7 10.6 %collective-permute-done.4 = bf16[128,4096]{1,0:T(8,128)(2,1)} collective-permute-done((bf16[128,4096]{1,0:T(8,128)(2,1)S(1)}, bf16[128,4096]{1,0:T(8,128)(2,1)}, u32[]{:S(2)}, u32[]{:S(2)}) %collective-permute-start.4) | collective-permute-done | bytes 1048608 | tf_op jit(solution)/shard_map/ppermute | solution.py:151
  227.3 2.3 broadcast_select_fusion.4.q_ref.k0_ref
  229.6 22.0 %collective-permute-done.5 = bf16[128,4096]{1,0:T(8,128)(2,1)} collective-permute-done((bf16[128,4096]{1,0:T(8,128)(2,1)S(1)}, bf16[128,4096]{1,0:T(8,128)(2,1)}, u32[]{:S(2)}, u32[]{:S(2)}) %collective-permute-start.5) | collective-permute-done | bytes 1048608 | tf_op jit(solution)/shard_map/ppermute | solution.py:157
  251.6 2.3 broadcast_select_fusion.k1a_ref.k1b_ref
  254.0 1.2 reshape.24.k3_ref
  255.2 15.6 %shard_map.74 = bf16[128,4096]{1,0:T(8,128)(2,1)} custom-call(s32[5]{0:T(128)} %pad_add_fusion.meta_ref, bf16[128,4096]{1,0:T(8,128)(2,1)} %broadcast_select_fusion.4.q_ref.k0_ref, bf16[128,4096]{1,0:T(8,128)(2,1)} %broadcast_select_fusion.4.q_ref.k0_ref, bf16[128,4096]{1,0:T(8,128)(2,1)} %broadcast_select_fusion.k1a_ref.k1b_ref, ...), custom_call_target="tpu_custom_call" | custom-call | tf_op jit(solution)/shard_map/pallas_call | solution.py:93
  (19 shorter events, 2.2 us)
Async XLA Ops:
  3.9 11.3 %copy-start = (bf16[1,128,4096]{2,1,0:T(8,128)(2,1)S(1)}, bf16[1,128,4096]{2,1,0:T(8,128)(2,1)}, u32[]{:S(2)}) copy-start(bf16[1,128,4096]{2,1,0:T(8,128)(2,1)} %param.8) | copy-start | bytes 3145732
  3.9 11.3 %copy-start.1 = (bf16[128,4096]{1,0:T(8,128)(2,1)S(1)}, bf16[128,4096]{1,0:T(8,128)(2,1)}, u32[]{:S(2)}) copy-start(bf16[128,4096]{1,0:T(8,128)(2,1)} %param.9) | copy-start | bytes 3145732
  3.9 11.3 %copy-start.3 = (bf16[1,128,4096]{2,1,0:T(8,128)(2,1)S(1)}, bf16[1,128,4096]{2,1,0:T(8,128)(2,1)}, u32[]{:S(2)}) copy-start(bf16[1,128,4096]{2,1,0:T(8,128)(2,1)} %param.7) | copy-start | bytes 3145732
  3.9 60.5 %all-to-all-start = ((bf16[64,4,4096]{2,1,0:T(4,128)(2,1)}), bf16[64,4,4096]{2,1,0:T(4,128)(2,1)}, u32[]{:S(2)}, u32[]{:S(2)}) async-start(bf16[64,4,4096]{2,1,0:T(4,128)(2,1)} %reshape.21), calls=%async_computation | async-start | bytes 4194304 | tf_op jit(solution)/shard_map/all_to_all | solution.py:29
  16.3 2.9 %copy-start.5 = (s32[64,4]{0,1:T(4,128)S(1)}, s32[64,4]{0,1:T(4,128)}, u32[]{:S(2)}) copy-start(s32[64,4]{0,1:T(4,128)} %param.10) | copy-start | bytes 3076
  17.2 52.1 %collective-permute-start = (bf16[64,4096]{1,0:T(8,128)(2,1)S(1)}, bf16[64,4096]{1,0:T(8,128)(2,1)S(1)}, u32[]{:S(2)}, u32[]{:S(2)}) collective-permute-start(bf16[64,4096]{1,0:T(8,128)(2,1)S(1)} %get-tuple-element.28), channel_id=1, source_target_pairs={{0,1},{1,2},{2,3},{3,4},{4,5},{5,6},{6,7},{7,8},{8,9},{9,10},{10,1... | collective-permute-start | bytes 1572872 | tf_op jit(solution)/shard_map/ppermute | solution.py:22
  69.3 2.4 copy-start.4
  71.6 57.2 %all-to-all-start.1 = ((bf16[64,4,4096]{2,1,0:T(4,128)(2,1)}), bf16[64,4,4096]{2,1,0:T(4,128)(2,1)S(1)}, u32[]{:S(2)}, u32[]{:S(2)}) async-start(bf16[64,4,4096]{2,1,0:T(4,128)(2,1)} %broadcast_in_dim.18), calls=%async_computation.1 | async-start | bytes 4194304 | tf_op jit(solution)/shard_map/all_to_all | solution.py:36
  79.6 54.4 %collective-permute-start.1 = (bf16[64,4096]{1,0:T(8,128)(2,1)}, bf16[64,4096]{1,0:T(8,128)(2,1)}, u32[]{:S(2)}, u32[]{:S(2)}) collective-permute-start(bf16[64,4096]{1,0:T(8,128)(2,1)} %get-tuple-element.27), channel_id=1, source_target_pairs={{0,1},{1,2},{2,3},{3,4},{4,5},{5,6},{6,7},{7,8},{8,9},{9,10},{10,1... | collective-permute-start | bytes 1572872 | tf_op jit(solution)/shard_map/ppermute | solution.py:22
  134.0 19.4 %collective-permute-start.2 = (bf16[128,4096]{1,0:T(8,128)(2,1)}, bf16[128,4096]{1,0:T(8,128)(2,1)}, u32[]{:S(2)}, u32[]{:S(2)}) collective-permute-start(bf16[128,4096]{1,0:T(8,128)(2,1)} %get-tuple-element.20), channel_id=1, source_target_pairs={{0,1},{1,2},{2,3},{3,4},{4,5},{5,6},{6,7},{7,8},{8,9},{9,10},{10,1... | collective-permute-start | bytes 3145736 | tf_op jit(solution)/shard_map/ppermute | solution.py:22
  153.4 43.5 %copy-start.2 = (bf16[128,4096]{1,0:T(8,128)(2,1)S(1)}, bf16[128,4096]{1,0:T(8,128)(2,1)}, u32[]{:S(2)}) copy-start(bf16[128,4096]{1,0:T(8,128)(2,1)} %shard_map.73) | copy-start | bytes 3145732
  154.9 36.2 %all-to-all-start.2 = ((bf16[64,2,4096]{2,1,0:T(2,128)(2,1)}), bf16[64,2,4096]{2,1,0:T(2,128)(2,1)S(1)}, u32[]{:S(2)}, u32[]{:S(2)}) async-start(bf16[64,2,4096]{2,1,0:T(2,128)(2,1)} %reshape.23), calls=%async_computation.2 | async-start | bytes 2097152 | tf_op jit(solution)/shard_map/all_to_all | solution.py:29
  191.2 5.7 %collective-permute-start.3 = (bf16[1,2,4096]{2,1,0:T(2,128)(2,1)S(1)}, bf16[1,2,4096]{2,1,0:T(2,128)(2,1)S(1)}, u32[]{:S(2)}, u32[]{:S(2)}) collective-permute-start(bf16[1,2,4096]{2,1,0:T(2,128)(2,1)S(1)} %constant_dynamic-slice_fusion), channel_id=1, source_target_pairs={{0,64},{64,128},{128,192},{192,256},{256,320},{320,384},{384,448},... | collective-permute-start | bytes 49160 | tf_op jit(solution)/shard_map/ppermute | solution.py:22
  196.9 30.4 %collective-permute-start.4 = (bf16[128,4096]{1,0:T(8,128)(2,1)S(1)}, bf16[128,4096]{1,0:T(8,128)(2,1)}, u32[]{:S(2)}, u32[]{:S(2)}) collective-permute-start(bf16[128,4096]{1,0:T(8,128)(2,1)S(1)} %copy-done.2), channel_id=1, source_target_pairs={{0,64},{64,128},{128,192},{192,256},{256,320},{320,384},{384,448},... | collective-permute-start | bytes 3145736 | tf_op jit(solution)/shard_map/ppermute | solution.py:151
  203.2 50.8 %all-to-all-start.3 = ((bf16[64,2,4096]{2,1,0:T(2,128)(2,1)}), bf16[64,2,4096]{2,1,0:T(2,128)(2,1)S(1)}, u32[]{:S(2)}, u32[]{:S(2)}) async-start(bf16[64,2,4096]{2,1,0:T(2,128)(2,1)} %broadcast_in_dim.20), calls=%async_computation.3 | async-start | bytes 2097152 | tf_op jit(solution)/shard_map/all_to_all | solution.py:36
  211.3 40.4 %collective-permute-start.5 = (bf16[128,4096]{1,0:T(8,128)(2,1)S(1)}, bf16[128,4096]{1,0:T(8,128)(2,1)}, u32[]{:S(2)}, u32[]{:S(2)}) collective-permute-start(bf16[128,4096]{1,0:T(8,128)(2,1)S(1)} %copy-done.2), channel_id=1, source_target_pairs={{0,65},{1,66},{2,67},{3,68},{4,69},{5,70},{6,71},{7,72},{8,73},{9,... | collective-permute-start | bytes 3145736 | tf_op jit(solution)/shard_map/ppermute | solution.py:157

commit v8 on v7

--- a/solution.py
+++ b/solution.py
@@ -121,20 +121,33 @@
     first_current = span_inputs[0]
     root = full_entries[LOCAL] % group_size
     piece_one = scatter_piece(jnp.concatenate([first_earlier, first_current]), "ctx", root)
-    behind = jnp.where(last, first_earlier, first_current)
-    front = shifted(behind[: BLOCK // 2], "ctx", 1)
-    piece_one, front = lax.optimization_barrier((piece_one, front))
-    back = shifted(behind[BLOCK // 2 :], "ctx", 1)
+    previous_one = shifted(jnp.where(last, first_earlier, first_current), "ctx", 1)
+    piece_one, previous_one = lax.optimization_barrier((piece_one, previous_one))
     both = gather_pieces(piece_one, "ctx")
-    both, back = lax.optimization_barrier((both, back))
+    half = BLOCK // 2
+
+    own_keys = (
+        (first_current, 0, BLOCK),
+        (previous_one, 0, half),
+        (previous_one, 1, half),
+        (first_earlier, 0, BLOCK),
+        (first_earlier, 0, BLOCK),
+    )
+    own_result = attend_pallas(
+        first_current, own_keys, query_entries, global_block, gain_query, gain_key, gain_out
+    )
+    later_root = full_entries[LOCAL + NR] % group_size
+    source = jnp.where(section_pos == sections - 1, next_inputs, own_result)
+    piece = shifted(scatter_piece(source, "ctx", later_root), "section", 1)
+    strided_later = gather_pieces(piece, "ctx")
+
     held, both = lax.optimization_barrier((jnp.where(last, first_current, next_inputs), both))
     previous_early = shifted(held, "ctx", 1)
 
-    half = BLOCK // 2
     key_one = (
         (first_current, 0, BLOCK),
-        (front, 0, half),
-        (back, 0, half),
+        (previous_one, 0, half),
+        (previous_one, 1, half),
         (both, 0, BLOCK),
         (both, 1, BLOCK),
     )
@@ -142,20 +155,14 @@
         first_current, key_one, query_entries, global_block, gain_query, gain_key, gain_out
     )
 
-    later_root = full_entries[LOCAL + NR] % group_size
-    source = jnp.where(section_pos == sections - 1, next_inputs, first_result)
-    source, previous_early = lax.optimization_barrier((source, previous_early))
-    piece = shifted(scatter_piece(source, "ctx", later_root), "section", 1)
-    outgoing, piece = lax.optimization_barrier((first_result, piece))
     straight = [(s, s + 1) for s in range(sections - 1)]
-    received = lax.ppermute(outgoing, "section", straight)
+    received = lax.ppermute(first_result, "section", straight)
     diagonal = [
         (s * group_size + i, (s + 1) * group_size + i + 1)
         for s in range(sections - 1)
         for i in range(group_size - 1)
     ]
-    received_previous = lax.ppermute(outgoing, ("section", "ctx"), diagonal)
-    strided_later = gather_pieces(piece, "ctx")
+    received_previous = lax.ppermute(first_result, ("section", "ctx"), diagonal)
     second_current = jnp.where(section_pos == 0, next_inputs, received)
     previous_two = jnp.where(
         (position == 0) | (section_pos == 0), previous_early, received_previous

time: 272 us -> 287 us (1.055)
  the two profiles are of different devices: /device:TPU:70 before, /device:TPU:192 now
where the time goes in v8:
time: 287 us; the launch traced here: 286 us
  waiting for transfers between devices  134 us (47%)
  Pallas kernels  46.6 us (16%)
  starting transfers between devices  42.9 us (15%)
  blocking collectives  33.6 us (12%)
  local copies, waits for them, and re-layouts  14.3 us (5%)
  other arithmetic  10.7 us (4%)
  between operations  4.02 us (1%)
    pallas_call x3, Pallas kernels, attend_pallas(): pl.pallas_call(attend_kernel, grid_spec=grid_spec, out_shape=jax.ShapeDty...  46.6 us
    all_to_all x1, waiting for transfers between devices, scatter_piece(): received = lax.all_to_all(pieces, axis, 0, 0, tiled=True)  45 us
    all_to_all x2, waiting for transfers between devices, gather_pieces(): lax.all_to_all(jnp.broadcast_to(piece, shape), axis, 0, 0, tiled=True)  42.3 us
    all_to_all x1, blocking collectives, scatter_piece(): received = lax.all_to_all(pieces, axis, 0, 0, tiled=True)  33.6 us
    ppermute x1, waiting for transfers between devices, local(): received = lax.ppermute(first_result, 'section', straight)  26.5 us
    all_to_all x2, starting transfers between devices, gather_pieces(): lax.all_to_all(jnp.broadcast_to(piece, shape), axis, 0, 0, tiled=True)  12.6 us
    ppermute x3, waiting for transfers between devices, shifted(): return lax.ppermute(value, axis, pairs)  11.2 us
    ppermute x3, starting transfers between devices, shifted(): return lax.ppermute(value, axis, pairs)  11 us
  transfers between devices with their start and end apart: 8, of which 6 were waited for; matrix products, arithmetic and copies ran while one was open for 3% of the time, Pallas kernels for 5%

profile of v8, /device:TPU:192, one launch (start us, length us, event | category | flops | bytes accessed | tf_op | source)
XLA Modules:
  0.0 285.9 jit_solution(6220830857410019120)
XLA Ops:
  0.0 1.7 pad_maximum_fusion
  1.7 2.2 reshape.22
  3.9 11.0 %all-to-all-start = ((bf16[64,4,4096]{2,1,0:T(4,128)(2,1)}), bf16[64,4,4096]{2,1,0:T(4,128)(2,1)}, u32[]{:S(2)}, u32[]{:S(2)}) async-start(bf16[64,4,4096]{2,1,0:T(4,128)(2,1)} %reshape.22), calls=%async_computation | async-start | bytes 4194304 | tf_op jit(solution)/shard_map/all_to_all | solution.py:29
  14.9 1.1 broadcast_select_fusion.3
  16.0 1.9 collective-permute-start
  17.9 0.6 fusion
  21.3 45.0 %all-to-all-done = bf16[64,4,4096]{2,1,0:T(4,128)(2,1)} async-done(((bf16[64,4,4096]{2,1,0:T(4,128)(2,1)}), bf16[64,4,4096]{2,1,0:T(4,128)(2,1)}, u32[]{:S(2)}, u32[]{:S(2)}) %all-to-all-start) | async-done | bytes 2097184 | tf_op jit(solution)/shard_map/all_to_all | solution.py:29
  66.3 0.8 constant_dynamic-slice_fusion.1
  67.0 9.8 %collective-permute-done.k1a_ref.k1b_ref = bf16[128,4096]{1,0:T(8,128)(2,1)S(1)} collective-permute-done((bf16[128,4096]{1,0:T(8,128)(2,1)}, bf16[128,4096]{1,0:T(8,128)(2,1)S(1)}, u32[]{:S(2)}, u32[]{:S(2)}) %collective-permute-start) | collective-permute-done | bytes 1048608 | tf_op jit(solution)/shard_map/ppermute | solution.py:22
  76.8 1.0 copy-done.2
  77.8 15.5 %shard_map.74 = bf16[128,4096]{1,0:T(8,128)(2,1)} custom-call(s32[5]{0:T(128)} %pad_add_fusion.meta_ref, bf16[128,4096]{1,0:T(8,128)(2,1)} %bitcast.12, bf16[128,4096]{1,0:T(8,128)(2,1)} %bitcast.13, bf16[128,4096]{1,0:T(8,128)(2,1)} %copy-done.2, bf16[128,4096]{1,0:T(8,128)(2,1)} %copy-done.2, bf16[128,4096]{1,0:T(8,128)(2,1)} %bitcast.17, ...), custom_call_target="tpu_custom_call" | custom-call | tf_op jit(solution)/shard_map/pallas_call | solution.py:93
  93.4 2.7 broadcast_select_fusion
  96.1 1.7 reshape.24
  97.8 33.6 %all_to_all.20 = bf16[64,2,4096]{2,1,0:T(2,128)(2,1)S(1)} all-to-all(bf16[64,2,4096]{2,1,0:T(2,128)(2,1)S(1)} %reshape.24), channel_id=1, replica_groups=mesh['section'=8,'ctx'=64] {'ctx'}, dimensions={0} | all-to-all | bytes 2097152 | tf_op jit(solution)/shard_map/all_to_all | solution.py:29
  131.5 2.4 broadcast_in_dim.18
  133.8 6.6 %all-to-all-start.1 = ((bf16[64,4,4096]{2,1,0:T(4,128)(2,1)}), bf16[64,4,4096]{2,1,0:T(4,128)(2,1)S(1)}, u32[]{:S(2)}, u32[]{:S(2)}) async-start(bf16[64,4,4096]{2,1,0:T(4,128)(2,1)} %broadcast_in_dim.18), calls=%async_computation.1 | async-start | bytes 4194304 | tf_op jit(solution)/shard_map/all_to_all | solution.py:36
  142.3 5.5 %collective-permute-start.4 = (bf16[1,2,4096]{2,1,0:T(2,128)(2,1)S(1)}, bf16[1,2,4096]{2,1,0:T(2,128)(2,1)S(1)}, u32[]{:S(2)}, u32[]{:S(2)}) collective-permute-start(bf16[1,2,4096]{2,1,0:T(2,128)(2,1)S(1)} %constant_dynamic-slice_fusion), channel_id=1, source_target_pairs={{0,64},{64,128},{128,192},{192,256},{256,320},{320,384},{384,448},... | collective-permute-start | bytes 49160 | tf_op jit(solution)/shard_map/ppermute | solution.py:22
  147.8 1.4 collective-permute-done.4
  149.3 42.3 %all-to-all-done.1 = bf16[64,4,4096]{2,1,0:T(4,128)(2,1)S(1)} async-done(((bf16[64,4,4096]{2,1,0:T(4,128)(2,1)}), bf16[64,4,4096]{2,1,0:T(4,128)(2,1)S(1)}, u32[]{:S(2)}, u32[]{:S(2)}) %all-to-all-start.1) | async-done | bytes 2097184 | tf_op jit(solution)/shard_map/all_to_all | solution.py:36
  191.5 2.0 broadcast_in_dim.20
  193.6 6.1 %all-to-all-start.3 = ((bf16[64,2,4096]{2,1,0:T(2,128)(2,1)}), bf16[64,2,4096]{2,1,0:T(2,128)(2,1)S(1)}, u32[]{:S(2)}, u32[]{:S(2)}) async-start(bf16[64,2,4096]{2,1,0:T(2,128)(2,1)} %broadcast_in_dim.20), calls=%async_computation.3 | async-start | bytes 2097152 | tf_op jit(solution)/shard_map/all_to_all | solution.py:36
  199.6 2.1 reshape.23.k2_ref.k3_ref
  201.7 15.5 %shard_map.73 = bf16[128,4096]{1,0:T(8,128)(2,1)} custom-call(s32[5]{0:T(128)} %pad_add_fusion.meta_ref, bf16[128,4096]{1,0:T(8,128)(2,1)} %bitcast.14, bf16[128,4096]{1,0:T(8,128)(2,1)} %bitcast.15, bf16[128,4096]{1,0:T(8,128)(2,1)} %copy-done.2, bf16[128,4096]{1,0:T(8,128)(2,1)} %copy-done.2, bf16[256,4096]{1,0:T(8,128)(2,1)} %reshape.23.k2_ref.k3_ref, ...), custom_call_target="tpu_custom_call" | custom-call | tf_op jit(solution)/shard_map/pallas_call | solution.py:93
  217.2 5.6 %collective-permute-start.1 = (bf16[128,4096]{1,0:T(8,128)(2,1)}, bf16[128,4096]{1,0:T(8,128)(2,1)}, u32[]{:S(2)}, u32[]{:S(2)}) collective-permute-start(bf16[128,4096]{1,0:T(8,128)(2,1)} %shard_map.73), channel_id=1, source_target_pairs={{0,64},{64,128},{128,192},{192,256},{256,320},{320,384},{384,448},... | collective-permute-start | bytes 3145736 | tf_op jit(solution)/shard_map/ppermute | solution.py:159
  222.9 2.6 collective-permute-start.3
  225.5 3.6 %collective-permute-start.2 = (bf16[128,4096]{1,0:T(8,128)(2,1)}, bf16[128,4096]{1,0:T(8,128)(2,1)}, u32[]{:S(2)}, u32[]{:S(2)}) collective-permute-start(bf16[128,4096]{1,0:T(8,128)(2,1)} %get-tuple-element.12), channel_id=1, source_target_pairs={{0,1},{1,2},{2,3},{3,4},{4,5},{5,6},{6,7},{7,8},{8,9},{9,10},{10,1... | collective-permute-start | bytes 3145736 | tf_op jit(solution)/shard_map/ppermute | solution.py:22
  229.2 1.2 reshape.25.k3_ref
  230.4 26.5 %collective-permute-done.1 = bf16[128,4096]{1,0:T(8,128)(2,1)} collective-permute-done((bf16[128,4096]{1,0:T(8,128)(2,1)}, bf16[128,4096]{1,0:T(8,128)(2,1)}, u32[]{:S(2)}, u32[]{:S(2)}) %collective-permute-start.1) | collective-permute-done | bytes 1048608 | tf_op jit(solution)/shard_map/ppermute | solution.py:159
  256.9 2.3 broadcast_select_fusion.4.q_ref.k0_ref
  259.2 8.9 %collective-permute-done.3 = bf16[128,4096]{1,0:T(8,128)(2,1)S(1)} collective-permute-done((bf16[128,4096]{1,0:T(8,128)(2,1)}, bf16[128,4096]{1,0:T(8,128)(2,1)S(1)}, u32[]{:S(2)}, u32[]{:S(2)}) %collective-permute-start.3) | collective-permute-done | bytes 1048608 | tf_op jit(solution)/shard_map/ppermute | solution.py:165
  268.1 2.3 broadcast_select_fusion.1.k1a_ref.k1b_ref
  270.4 15.5 %shard_map.75 = bf16[128,4096]{1,0:T(8,128)(2,1)} custom-call(s32[5]{0:T(128)} %pad_add_fusion.meta_ref, bf16[128,4096]{1,0:T(8,128)(2,1)} %broadcast_select_fusion.4.q_ref.k0_ref, bf16[128,4096]{1,0:T(8,128)(2,1)} %broadcast_select_fusion.4.q_ref.k0_ref, bf16[128,4096]{1,0:T(8,128)(2,1)} %broadcast_select_fusion.1.k1a_ref.k1b_ref, ...), custom_call_target="tpu_custom_call" | custom-call | tf_op jit(solution)/shard_map/pallas_call | solution.py:93
  (18 shorter events, 0.8 us)
Async XLA Ops:
  3.9 11.0 %copy-start = (bf16[1,128,4096]{2,1,0:T(8,128)(2,1)S(1)}, bf16[1,128,4096]{2,1,0:T(8,128)(2,1)}, u32[]{:S(2)}) copy-start(bf16[1,128,4096]{2,1,0:T(8,128)(2,1)} %param.8) | copy-start | bytes 3145732
  3.9 11.0 %copy-start.3 = (bf16[1,128,4096]{2,1,0:T(8,128)(2,1)S(1)}, bf16[1,128,4096]{2,1,0:T(8,128)(2,1)}, u32[]{:S(2)}) copy-start(bf16[1,128,4096]{2,1,0:T(8,128)(2,1)} %param.7) | copy-start | bytes 3145732
  3.9 62.3 %all-to-all-start = ((bf16[64,4,4096]{2,1,0:T(4,128)(2,1)}), bf16[64,4,4096]{2,1,0:T(4,128)(2,1)}, u32[]{:S(2)}, u32[]{:S(2)}) async-start(bf16[64,4,4096]{2,1,0:T(4,128)(2,1)} %reshape.22), calls=%async_computation | async-start | bytes 4194304 | tf_op jit(solution)/shard_map/all_to_all | solution.py:29
  14.9 3.0 %copy-start.6 = (s32[64,4]{0,1:T(4,128)S(1)}, s32[64,4]{0,1:T(4,128)}, u32[]{:S(2)}) copy-start(s32[64,4]{0,1:T(4,128)} %param.10) | copy-start | bytes 3076
  16.0 60.8 %collective-permute-start = (bf16[128,4096]{1,0:T(8,128)(2,1)}, bf16[128,4096]{1,0:T(8,128)(2,1)S(1)}, u32[]{:S(2)}, u32[]{:S(2)}) collective-permute-start(bf16[128,4096]{1,0:T(8,128)(2,1)} %broadcast_select_fusion.3), channel_id=1, source_target_pairs={{0,1},{1,2},{2,3},{3,4},{4,5},{5,6},{6,7},{7,8},{8,9},{9,10},{10,1... | collective-permute-start | bytes 3145736 | tf_op jit(solution)/shard_map/ppermute | solution.py:22
  67.0 26.3 %copy-start.1 = (bf16[1,128,4096]{2,1,0:T(8,128)(2,1)S(1)}, bf16[1,128,4096]{2,1,0:T(8,128)(2,1)}, u32[]{:S(2)}) copy-start(bf16[1,128,4096]{2,1,0:T(8,128)(2,1)} %param.8) | copy-start | bytes 3145732
  67.0 26.3 %copy-start.4 = (bf16[128,4096]{1,0:T(8,128)(2,1)S(1)}, bf16[128,4096]{1,0:T(8,128)(2,1)}, u32[]{:S(2)}) copy-start(bf16[128,4096]{1,0:T(8,128)(2,1)} %param.9) | copy-start | bytes 3145732
  76.8 1.0 copy-start.2
  133.8 57.7 %all-to-all-start.1 = ((bf16[64,4,4096]{2,1,0:T(4,128)(2,1)}), bf16[64,4,4096]{2,1,0:T(4,128)(2,1)S(1)}, u32[]{:S(2)}, u32[]{:S(2)}) async-start(bf16[64,4,4096]{2,1,0:T(4,128)(2,1)} %broadcast_in_dim.18), calls=%async_computation.1 | async-start | bytes 4194304 | tf_op jit(solution)/shard_map/all_to_all | solution.py:36
  142.3 6.9 %collective-permute-start.4 = (bf16[1,2,4096]{2,1,0:T(2,128)(2,1)S(1)}, bf16[1,2,4096]{2,1,0:T(2,128)(2,1)S(1)}, u32[]{:S(2)}, u32[]{:S(2)}) collective-permute-start(bf16[1,2,4096]{2,1,0:T(2,128)(2,1)S(1)} %constant_dynamic-slice_fusion), channel_id=1, source_target_pairs={{0,64},{64,128},{128,192},{192,256},{256,320},{320,384},{384,448},... | collective-permute-start | bytes 49160 | tf_op jit(solution)/shard_map/ppermute | solution.py:22
  193.6 35.6 %all-to-all-start.3 = ((bf16[64,2,4096]{2,1,0:T(2,128)(2,1)}), bf16[64,2,4096]{2,1,0:T(2,128)(2,1)S(1)}, u32[]{:S(2)}, u32[]{:S(2)}) async-start(bf16[64,2,4096]{2,1,0:T(2,128)(2,1)} %broadcast_in_dim.20), calls=%async_computation.3 | async-start | bytes 2097152 | tf_op jit(solution)/shard_map/all_to_all | solution.py:36
  217.2 39.6 %copy-start.5 = (bf16[128,4096]{1,0:T(8,128)(2,1)S(1)}, bf16[128,4096]{1,0:T(8,128)(2,1)}, u32[]{:S(2)}) copy-start(bf16[128,4096]{1,0:T(8,128)(2,1)} %param.9) | copy-start | bytes 3145732
  217.2 39.6 %collective-permute-start.1 = (bf16[128,4096]{1,0:T(8,128)(2,1)}, bf16[128,4096]{1,0:T(8,128)(2,1)}, u32[]{:S(2)}, u32[]{:S(2)}) collective-permute-start(bf16[128,4096]{1,0:T(8,128)(2,1)} %shard_map.73), channel_id=1, source_target_pairs={{0,64},{64,128},{128,192},{192,256},{256,320},{320,384},{384,448},... | collective-permute-start | bytes 3145736 | tf_op jit(solution)/shard_map/ppermute | solution.py:159
  222.9 45.2 %collective-permute-start.3 = (bf16[128,4096]{1,0:T(8,128)(2,1)}, bf16[128,4096]{1,0:T(8,128)(2,1)S(1)}, u32[]{:S(2)}, u32[]{:S(2)}) collective-permute-start(bf16[128,4096]{1,0:T(8,128)(2,1)} %shard_map.73), channel_id=1, source_target_pairs={{0,65},{1,66},{2,67},{3,68},{4,69},{5,70},{6,71},{7,72},{8,73},{9,... | collective-permute-start | bytes 3145736 | tf_op jit(solution)/shard_map/ppermute | solution.py:165
  225.5 42.6 %collective-permute-start.2 = (bf16[128,4096]{1,0:T(8,128)(2,1)}, bf16[128,4096]{1,0:T(8,128)(2,1)}, u32[]{:S(2)}, u32[]{:S(2)}) collective-permute-start(bf16[128,4096]{1,0:T(8,128)(2,1)} %get-tuple-element.12), channel_id=1, source_target_pairs={{0,1},{1,2},{2,3},{3,4},{4,5},{5,6},{6,7},{7,8},{8,9},{9,10},{10,1... | collective-permute-start | bytes 3145736 | tf_op jit(solution)/shard_map/ppermute | solution.py:22

commit v9 on v7

--- a/solution.py
+++ b/solution.py
@@ -13,7 +13,7 @@
 NR = 1
 WIDTH = 4096
 NSEL = 4
-GROUP = 8
+GROUP = 16
 
 
 def shifted(value, axis, steps):
@@ -49,10 +49,12 @@
     global_block = meta_ref[NSEL]
     query_pos = lax.broadcasted_iota(jnp.int32, (BLOCK, BLOCK), 0)
     key_pos = lax.broadcasted_iota(jnp.int32, (BLOCK, BLOCK), 1)
-    allowed = []
-    for b in range(NSEL):
-        entry = meta_ref[b]
-        allowed.append((entry >= 0) & ((entry != global_block) | (key_pos <= query_pos)))
+    entry = meta_ref[0]
+    allowed = (entry >= 0) & ((entry != global_block) | (key_pos <= query_pos))
+    biases = [None] + [
+        jnp.where((meta_ref[b] >= 0) & (meta_ref[b] != global_block), 0.0, -jnp.inf).astype(jnp.float32)
+        for b in range(1, NSEL)
+    ]
     for h in range(GROUP):
         lanes = slice(h * HD, (h + 1) * HD)
         rows = q_ref[:, lanes].astype(jnp.float32)
@@ -65,9 +67,14 @@
             wide = raw_keys.astype(jnp.float32)
             keys = (wide * lax.rsqrt(jnp.mean(wide * wide, axis=-1, keepdims=True) + 1e-06) * gk_ref[:, lanes]).astype(jnp.bfloat16)
             s = lax.dot_general(queries, keys, (((1,), (1,)), ((), ())), preferred_element_type=jnp.float32)
-            scores.append(jnp.where(allowed[b], s, -jnp.inf))
-        maxima = functools.reduce(jnp.maximum, [jnp.max(s, axis=-1, keepdims=True) for s in scores])
-        raws = [jnp.exp(s - maxima) for s in scores]
+            scores.append(jnp.where(allowed, s, -jnp.inf) if b == 0 else s)
+        peaks = [jnp.max(s, axis=-1, keepdims=True) for s in scores]
+        maxima = functools.reduce(
+            jnp.maximum, [peaks[0]] + [peaks[b] + biases[b] for b in range(1, NSEL)]
+        )
+        raws = [jnp.exp(scores[0] - maxima)] + [
+            jnp.exp(scores[b] - (maxima - biases[b])) for b in range(1, NSEL)
+        ]
         totals = functools.reduce(jnp.add, [jnp.sum(r, axis=-1, keepdims=True) for r in raws])
         context = None
         for b in range(NSEL):

time: 272 us -> 272 us (level)
  no operation moved by 1% of the time
where the time goes in v9:
time: 272 us; the launch traced here: 271 us
  waiting for transfers between devices  156 us (57%)
  starting transfers between devices  56.6 us (21%)
  Pallas kernels  31.7 us (12%)
  local copies, waits for them, and re-layouts  13.8 us (5%)
  other arithmetic  9.42 us (3%)
  between operations  3.74 us (1%)
    all_to_all x2, waiting for transfers between devices, scatter_piece(): received = lax.all_to_all(pieces, axis, 0, 0, tiled=True)  67.5 us
    all_to_all x2, waiting for transfers between devices, gather_pieces(): lax.all_to_all(jnp.broadcast_to(piece, shape), axis, 0, 0, tiled=True)  47.1 us
    pallas_call x2, Pallas kernels, attend_pallas(): pl.pallas_call(attend_kernel, grid_spec=grid_spec, out_shape=jax.ShapeDty...  31.7 us
    ppermute x1, waiting for transfers between devices, local(): received_previous = lax.ppermute(outgoing, ('section', 'ctx'), diagonal)  22 us
    all_to_all x2, starting transfers between devices, scatter_piece(): received = lax.all_to_all(pieces, axis, 0, 0, tiled=True)  20.8 us
    all_to_all x2, starting transfers between devices, gather_pieces(): lax.all_to_all(jnp.broadcast_to(piece, shape), axis, 0, 0, tiled=True)  16 us
    ppermute x1, waiting for transfers between devices, local(): received = lax.ppermute(outgoing, 'section', straight)  10.8 us
    ppermute x4, starting transfers between devices, shifted(): return lax.ppermute(value, axis, pairs)  10.2 us
  transfers between devices with their start and end apart: 10, of which 8 were waited for; matrix products, arithmetic and copies ran while one was open for 5% of the time, Pallas kernels for 6%

profile of v9, /device:TPU:70, one launch (start us, length us, event | category | flops | bytes accessed | tf_op | source)
XLA Modules:
  0.0 271.4 jit_solution(15395665344746618666)
XLA Ops:
  0.0 1.7 pad_maximum_fusion
  1.7 2.2 reshape.21
  3.9 11.3 %all-to-all-start = ((bf16[64,4,4096]{2,1,0:T(4,128)(2,1)}), bf16[64,4,4096]{2,1,0:T(4,128)(2,1)}, u32[]{:S(2)}, u32[]{:S(2)}) async-start(bf16[64,4,4096]{2,1,0:T(4,128)(2,1)} %reshape.21), calls=%async_computation | async-start | bytes 4194304 | tf_op jit(solution)/shard_map/all_to_all | solution.py:29
  15.2 1.1 broadcast_select_fusion.2
  16.3 0.9 fusion
  17.2 2.0 collective-permute-start
  21.5 42.8 %all-to-all-done = bf16[64,4,4096]{2,1,0:T(4,128)(2,1)} async-done(((bf16[64,4,4096]{2,1,0:T(4,128)(2,1)}), bf16[64,4,4096]{2,1,0:T(4,128)(2,1)}, u32[]{:S(2)}, u32[]{:S(2)}) %all-to-all-start) | async-done | bytes 2097184 | tf_op jit(solution)/shard_map/all_to_all | solution.py:29
  65.1 4.2 %collective-permute-done.k1a_ref = bf16[64,4096]{1,0:T(8,128)(2,1)S(1)} collective-permute-done((bf16[64,4096]{1,0:T(8,128)(2,1)S(1)}, bf16[64,4096]{1,0:T(8,128)(2,1)S(1)}, u32[]{:S(2)}, u32[]{:S(2)}) %collective-permute-start) | collective-permute-done | bytes 524320 | tf_op jit(solution)/shard_map/ppermute | solution.py:22
  69.3 2.4 broadcast_in_dim.18
  71.6 7.9 %all-to-all-start.1 = ((bf16[64,4,4096]{2,1,0:T(4,128)(2,1)}), bf16[64,4,4096]{2,1,0:T(4,128)(2,1)S(1)}, u32[]{:S(2)}, u32[]{:S(2)}) async-start(bf16[64,4,4096]{2,1,0:T(4,128)(2,1)} %broadcast_in_dim.18), calls=%async_computation.1 | async-start | bytes 4194304 | tf_op jit(solution)/shard_map/all_to_all | solution.py:36
  79.6 2.0 collective-permute-start.1
  81.8 47.0 %all-to-all-done.1 = bf16[64,4,4096]{2,1,0:T(4,128)(2,1)S(1)} async-done(((bf16[64,4,4096]{2,1,0:T(4,128)(2,1)}), bf16[64,4,4096]{2,1,0:T(4,128)(2,1)S(1)}, u32[]{:S(2)}, u32[]{:S(2)}) %all-to-all-start.1) | async-done | bytes 2097184 | tf_op jit(solution)/shard_map/all_to_all | solution.py:36
  128.9 2.1 reshape.22.k2_ref.k3_ref
  130.9 3.1 %collective-permute-done.1.k1b_ref = bf16[64,4096]{1,0:T(8,128)(2,1)} collective-permute-done((bf16[64,4096]{1,0:T(8,128)(2,1)}, bf16[64,4096]{1,0:T(8,128)(2,1)}, u32[]{:S(2)}, u32[]{:S(2)}) %collective-permute-start.1) | collective-permute-done | bytes 524320 | tf_op jit(solution)/shard_map/ppermute | solution.py:22
  134.0 1.9 collective-permute-start.2
  136.6 15.9 %shard_map.73 = bf16[128,4096]{1,0:T(8,128)(2,1)} custom-call(s32[5]{0:T(128)} %pad_add_fusion.meta_ref, bf16[128,4096]{1,0:T(8,128)(2,1)} %bitcast.12, bf16[128,4096]{1,0:T(8,128)(2,1)} %bitcast.13, bf16[64,4096]{1,0:T(8,128)(2,1)} %copy-done.4, bf16[64,4096]{1,0:T(8,128)(2,1)} %collective-permute-done.1.k1b_ref, bf16[256,4096]{1,0:T(8,128)(2,1)} %reshape.22.k2_ref.k3_ref, ...), custom_call_target="tpu_custom_call" | custom-call | tf_op jit(solution)/shard_map/pallas_call | solution.py:100
  152.4 1.3 broadcast_select_fusion.1
  153.8 1.5 reshape.23
  155.3 9.6 %all-to-all-start.2 = ((bf16[64,2,4096]{2,1,0:T(2,128)(2,1)}), bf16[64,2,4096]{2,1,0:T(2,128)(2,1)S(1)}, u32[]{:S(2)}, u32[]{:S(2)}) async-start(bf16[64,2,4096]{2,1,0:T(2,128)(2,1)} %reshape.23), calls=%async_computation.2 | async-start | bytes 2097152 | tf_op jit(solution)/shard_map/all_to_all | solution.py:29
  166.8 24.7 %all-to-all-done.2 = bf16[64,2,4096]{2,1,0:T(2,128)(2,1)S(1)} async-done(((bf16[64,2,4096]{2,1,0:T(2,128)(2,1)}), bf16[64,2,4096]{2,1,0:T(2,128)(2,1)S(1)}, u32[]{:S(2)}, u32[]{:S(2)}) %all-to-all-start.2) | async-done | bytes 1048608 | tf_op jit(solution)/shard_map/all_to_all | solution.py:29
  191.5 4.3 %collective-permute-start.3 = (bf16[1,2,4096]{2,1,0:T(2,128)(2,1)S(1)}, bf16[1,2,4096]{2,1,0:T(2,128)(2,1)S(1)}, u32[]{:S(2)}, u32[]{:S(2)}) collective-permute-start(bf16[1,2,4096]{2,1,0:T(2,128)(2,1)S(1)} %constant_dynamic-slice_fusion), channel_id=1, source_target_pairs={{0,64},{64,128},{128,192},{192,256},{256,320},{320,384},{384,448},... | collective-permute-start | bytes 49160 | tf_op jit(solution)/shard_map/ppermute | solution.py:22
  195.8 1.4 collective-permute-done.3
  197.2 4.3 %collective-permute-start.4 = (bf16[128,4096]{1,0:T(8,128)(2,1)S(1)}, bf16[128,4096]{1,0:T(8,128)(2,1)}, u32[]{:S(2)}, u32[]{:S(2)}) collective-permute-start(bf16[128,4096]{1,0:T(8,128)(2,1)S(1)} %copy-done.2), channel_id=1, source_target_pairs={{0,64},{64,128},{128,192},{192,256},{256,320},{320,384},{384,448},... | collective-permute-start | bytes 3145736 | tf_op jit(solution)/shard_map/ppermute | solution.py:158
  201.5 2.0 broadcast_in_dim.20
  203.5 8.1 %all-to-all-start.3 = ((bf16[64,2,4096]{2,1,0:T(2,128)(2,1)}), bf16[64,2,4096]{2,1,0:T(2,128)(2,1)S(1)}, u32[]{:S(2)}, u32[]{:S(2)}) async-start(bf16[64,2,4096]{2,1,0:T(2,128)(2,1)} %broadcast_in_dim.20), calls=%async_computation.3 | async-start | bytes 2097152 | tf_op jit(solution)/shard_map/all_to_all | solution.py:36
  211.6 5.2 %collective-permute-start.5 = (bf16[128,4096]{1,0:T(8,128)(2,1)S(1)}, bf16[128,4096]{1,0:T(8,128)(2,1)}, u32[]{:S(2)}, u32[]{:S(2)}) collective-permute-start(bf16[128,4096]{1,0:T(8,128)(2,1)S(1)} %copy-done.2), channel_id=1, source_target_pairs={{0,65},{1,66},{2,67},{3,68},{4,69},{5,70},{6,71},{7,72},{8,73},{9,... | collective-permute-start | bytes 3145736 | tf_op jit(solution)/shard_map/ppermute | solution.py:164
  216.8 10.8 %collective-permute-done.4 = bf16[128,4096]{1,0:T(8,128)(2,1)} collective-permute-done((bf16[128,4096]{1,0:T(8,128)(2,1)S(1)}, bf16[128,4096]{1,0:T(8,128)(2,1)}, u32[]{:S(2)}, u32[]{:S(2)}) %collective-permute-start.4) | collective-permute-done | bytes 1048608 | tf_op jit(solution)/shard_map/ppermute | solution.py:158
  227.6 2.3 broadcast_select_fusion.4.q_ref.k0_ref
  230.0 22.0 %collective-permute-done.5 = bf16[128,4096]{1,0:T(8,128)(2,1)} collective-permute-done((bf16[128,4096]{1,0:T(8,128)(2,1)S(1)}, bf16[128,4096]{1,0:T(8,128)(2,1)}, u32[]{:S(2)}, u32[]{:S(2)}) %collective-permute-start.5) | collective-permute-done | bytes 1048608 | tf_op jit(solution)/shard_map/ppermute | solution.py:164
  252.0 2.3 broadcast_select_fusion.k1a_ref.k1b_ref
  254.3 1.2 reshape.24.k3_ref
  255.5 15.9 %shard_map.74 = bf16[128,4096]{1,0:T(8,128)(2,1)} custom-call(s32[5]{0:T(128)} %pad_add_fusion.meta_ref, bf16[128,4096]{1,0:T(8,128)(2,1)} %broadcast_select_fusion.4.q_ref.k0_ref, bf16[128,4096]{1,0:T(8,128)(2,1)} %broadcast_select_fusion.4.q_ref.k0_ref, bf16[128,4096]{1,0:T(8,128)(2,1)} %broadcast_select_fusion.k1a_ref.k1b_ref, ...), custom_call_target="tpu_custom_call" | custom-call | tf_op jit(solution)/shard_map/pallas_call | solution.py:100
  (19 shorter events, 2.2 us)
Async XLA Ops:
  3.9 11.3 %copy-start = (bf16[1,128,4096]{2,1,0:T(8,128)(2,1)S(1)}, bf16[1,128,4096]{2,1,0:T(8,128)(2,1)}, u32[]{:S(2)}) copy-start(bf16[1,128,4096]{2,1,0:T(8,128)(2,1)} %param.8) | copy-start | bytes 3145732
  3.9 11.3 %copy-start.1 = (bf16[128,4096]{1,0:T(8,128)(2,1)S(1)}, bf16[128,4096]{1,0:T(8,128)(2,1)}, u32[]{:S(2)}) copy-start(bf16[128,4096]{1,0:T(8,128)(2,1)} %param.9) | copy-start | bytes 3145732
  3.9 11.3 %copy-start.3 = (bf16[1,128,4096]{2,1,0:T(8,128)(2,1)S(1)}, bf16[1,128,4096]{2,1,0:T(8,128)(2,1)}, u32[]{:S(2)}) copy-start(bf16[1,128,4096]{2,1,0:T(8,128)(2,1)} %param.7) | copy-start | bytes 3145732
  3.9 60.5 %all-to-all-start = ((bf16[64,4,4096]{2,1,0:T(4,128)(2,1)}), bf16[64,4,4096]{2,1,0:T(4,128)(2,1)}, u32[]{:S(2)}, u32[]{:S(2)}) async-start(bf16[64,4,4096]{2,1,0:T(4,128)(2,1)} %reshape.21), calls=%async_computation | async-start | bytes 4194304 | tf_op jit(solution)/shard_map/all_to_all | solution.py:29
  16.3 2.9 %copy-start.5 = (s32[64,4]{0,1:T(4,128)S(1)}, s32[64,4]{0,1:T(4,128)}, u32[]{:S(2)}) copy-start(s32[64,4]{0,1:T(4,128)} %param.10) | copy-start | bytes 3076
  17.2 52.1 %collective-permute-start = (bf16[64,4096]{1,0:T(8,128)(2,1)S(1)}, bf16[64,4096]{1,0:T(8,128)(2,1)S(1)}, u32[]{:S(2)}, u32[]{:S(2)}) collective-permute-start(bf16[64,4096]{1,0:T(8,128)(2,1)S(1)} %get-tuple-element.28), channel_id=1, source_target_pairs={{0,1},{1,2},{2,3},{3,4},{4,5},{5,6},{6,7},{7,8},{8,9},{9,10},{10,1... | collective-permute-start | bytes 1572872 | tf_op jit(solution)/shard_map/ppermute | solution.py:22
  69.3 2.4 copy-start.4
  71.6 57.2 %all-to-all-start.1 = ((bf16[64,4,4096]{2,1,0:T(4,128)(2,1)}), bf16[64,4,4096]{2,1,0:T(4,128)(2,1)S(1)}, u32[]{:S(2)}, u32[]{:S(2)}) async-start(bf16[64,4,4096]{2,1,0:T(4,128)(2,1)} %broadcast_in_dim.18), calls=%async_computation.1 | async-start | bytes 4194304 | tf_op jit(solution)/shard_map/all_to_all | solution.py:36
  79.6 54.4 %collective-permute-start.1 = (bf16[64,4096]{1,0:T(8,128)(2,1)}, bf16[64,4096]{1,0:T(8,128)(2,1)}, u32[]{:S(2)}, u32[]{:S(2)}) collective-permute-start(bf16[64,4096]{1,0:T(8,128)(2,1)} %get-tuple-element.27), channel_id=1, source_target_pairs={{0,1},{1,2},{2,3},{3,4},{4,5},{5,6},{6,7},{7,8},{8,9},{9,10},{10,1... | collective-permute-start | bytes 1572872 | tf_op jit(solution)/shard_map/ppermute | solution.py:22
  134.0 19.8 %collective-permute-start.2 = (bf16[128,4096]{1,0:T(8,128)(2,1)}, bf16[128,4096]{1,0:T(8,128)(2,1)}, u32[]{:S(2)}, u32[]{:S(2)}) collective-permute-start(bf16[128,4096]{1,0:T(8,128)(2,1)} %get-tuple-element.20), channel_id=1, source_target_pairs={{0,1},{1,2},{2,3},{3,4},{4,5},{5,6},{6,7},{7,8},{8,9},{9,10},{10,1... | collective-permute-start | bytes 3145736 | tf_op jit(solution)/shard_map/ppermute | solution.py:22
  153.8 43.5 %copy-start.2 = (bf16[128,4096]{1,0:T(8,128)(2,1)S(1)}, bf16[128,4096]{1,0:T(8,128)(2,1)}, u32[]{:S(2)}) copy-start(bf16[128,4096]{1,0:T(8,128)(2,1)} %shard_map.73) | copy-start | bytes 3145732
  155.3 36.2 %all-to-all-start.2 = ((bf16[64,2,4096]{2,1,0:T(2,128)(2,1)}), bf16[64,2,4096]{2,1,0:T(2,128)(2,1)S(1)}, u32[]{:S(2)}, u32[]{:S(2)}) async-start(bf16[64,2,4096]{2,1,0:T(2,128)(2,1)} %reshape.23), calls=%async_computation.2 | async-start | bytes 2097152 | tf_op jit(solution)/shard_map/all_to_all | solution.py:29
  191.5 5.7 %collective-permute-start.3 = (bf16[1,2,4096]{2,1,0:T(2,128)(2,1)S(1)}, bf16[1,2,4096]{2,1,0:T(2,128)(2,1)S(1)}, u32[]{:S(2)}, u32[]{:S(2)}) collective-permute-start(bf16[1,2,4096]{2,1,0:T(2,128)(2,1)S(1)} %constant_dynamic-slice_fusion), channel_id=1, source_target_pairs={{0,64},{64,128},{128,192},{192,256},{256,320},{320,384},{384,448},... | collective-permute-start | bytes 49160 | tf_op jit(solution)/shard_map/ppermute | solution.py:22
  197.2 30.4 %collective-permute-start.4 = (bf16[128,4096]{1,0:T(8,128)(2,1)S(1)}, bf16[128,4096]{1,0:T(8,128)(2,1)}, u32[]{:S(2)}, u32[]{:S(2)}) collective-permute-start(bf16[128,4096]{1,0:T(8,128)(2,1)S(1)} %copy-done.2), channel_id=1, source_target_pairs={{0,64},{64,128},{128,192},{192,256},{256,320},{320,384},{384,448},... | collective-permute-start | bytes 3145736 | tf_op jit(solution)/shard_map/ppermute | solution.py:158
  203.5 50.8 %all-to-all-start.3 = ((bf16[64,2,4096]{2,1,0:T(2,128)(2,1)}), bf16[64,2,4096]{2,1,0:T(2,128)(2,1)S(1)}, u32[]{:S(2)}, u32[]{:S(2)}) async-start(bf16[64,2,4096]{2,1,0:T(2,128)(2,1)} %broadcast_in_dim.20), calls=%async_computation.3 | async-start | bytes 2097152 | tf_op jit(solution)/shard_map/all_to_all | solution.py:36
  211.6 40.4 %collective-permute-start.5 = (bf16[128,4096]{1,0:T(8,128)(2,1)S(1)}, bf16[128,4096]{1,0:T(8,128)(2,1)}, u32[]{:S(2)}, u32[]{:S(2)}) collective-permute-start(bf16[128,4096]{1,0:T(8,128)(2,1)S(1)} %copy-done.2), channel_id=1, source_target_pairs={{0,65},{1,66},{2,67},{3,68},{4,69},{5,70},{6,71},{7,72},{8,73},{9,... | collective-permute-start | bytes 3145736 | tf_op jit(solution)/shard_map/ppermute | solution.py:164

commit v10 on v7

--- a/solution.py
+++ b/solution.py
@@ -22,10 +22,10 @@
     return lax.ppermute(value, axis, pairs)
 
 
-def scatter_piece(payload, axis, root):
+def scatter_piece(payloads, axis, root):
     count = lax.axis_size(axis)
-    rows = payload.shape[0]
-    pieces = payload.reshape(count, rows // count, payload.shape[1])
+    rows = sum(payload.shape[0] for payload in payloads) // count
+    pieces = jnp.concatenate([payload.reshape(-1, rows, payload.shape[1]) for payload in payloads])
     received = lax.all_to_all(pieces, axis, 0, 0, tiled=True)
     return lax.dynamic_index_in_dim(received, root, 0, keepdims=True)
 
@@ -120,7 +120,7 @@
     first_earlier = earlier_span[0]
     first_current = span_inputs[0]
     root = full_entries[LOCAL] % group_size
-    piece_one = scatter_piece(jnp.concatenate([first_earlier, first_current]), "ctx", root)
+    piece_one = scatter_piece([first_earlier, first_current], "ctx", root)
     behind = jnp.where(last, first_earlier, first_current)
     front = shifted(behind[: BLOCK // 2], "ctx", 1)
     piece_one, front = lax.optimization_barrier((piece_one, front))
@@ -145,7 +145,7 @@
     later_root = full_entries[LOCAL + NR] % group_size
     source = jnp.where(section_pos == sections - 1, next_inputs, first_result)
     source, previous_early = lax.optimization_barrier((source, previous_early))
-    piece = shifted(scatter_piece(source, "ctx", later_root), "section", 1)
+    piece = shifted(scatter_piece([source], "ctx", later_root), "section", 1)
     outgoing, piece = lax.optimization_barrier((first_result, piece))
     straight = [(s, s + 1) for s in range(sections - 1)]
     received = lax.ppermute(outgoing, "section", straight)

time: 272 us -> 272 us (level)
  no operation moved by 1% of the time
where the time goes in v10:
time: 272 us; the launch traced here: 271 us
  waiting for transfers between devices  156 us (57%)
  starting transfers between devices  56.6 us (21%)
  Pallas kernels  31.1 us (11%)
  local copies, waits for them, and re-layouts  13.5 us (5%)
  other arithmetic  10.4 us (4%)
  between operations  3.75 us (1%)
    all_to_all x2, waiting for transfers between devices, scatter_piece(): received = lax.all_to_all(pieces, axis, 0, 0, tiled=True)  67.6 us
    all_to_all x2, waiting for transfers between devices, gather_pieces(): lax.all_to_all(jnp.broadcast_to(piece, shape), axis, 0, 0, tiled=True)  47.1 us
    pallas_call x2, Pallas kernels, attend_pallas(): pl.pallas_call(attend_kernel, grid_spec=grid_spec, out_shape=jax.ShapeDty...  31.1 us
    ppermute x1, waiting for transfers between devices, local(): received_previous = lax.ppermute(outgoing, ('section', 'ctx'), diagonal)  22 us
    all_to_all x2, starting transfers between devices, scatter_piece(): received = lax.all_to_all(pieces, axis, 0, 0, tiled=True)  20.7 us
    all_to_all x2, starting transfers between devices, gather_pieces(): lax.all_to_all(jnp.broadcast_to(piece, shape), axis, 0, 0, tiled=True)  16 us
    ppermute x1, waiting for transfers between devices, local(): received = lax.ppermute(outgoing, 'section', straight)  10.6 us
    ppermute x4, starting transfers between devices, shifted(): return lax.ppermute(value, axis, pairs)  10.2 us
  transfers between devices with their start and end apart: 10, of which 8 were waited for; matrix products, arithmetic and copies ran while one was open for 5% of the time, Pallas kernels for 6%

profile of v10, /device:TPU:70, one launch (start us, length us, event | category | flops | bytes accessed | tf_op | source)
XLA Modules:
  0.0 271.4 jit_solution(13819536584809980689)
XLA Ops:
  0.0 1.5 reshape_squeeze.6
  2.0 2.7 pad_maximum_fusion
  4.7 11.1 %all-to-all-start = ((bf16[64,4,4096]{2,1,0:T(4,128)(2,1)}), bf16[64,4,4096]{2,1,0:T(4,128)(2,1)}, u32[]{:S(2)}, u32[]{:S(2)}) async-start(bf16[64,4,4096]{2,1,0:T(4,128)(2,1)} %pad_maximum_fusion), calls=%async_computation | async-start | bytes 4194304 | tf_op jit(solution)/shard_map/all_to_all | solution.py:29
  15.8 1.1 broadcast_select_fusion.2
  17.0 0.9 fusion
  17.8 2.0 collective-permute-start
  22.2 42.8 %all-to-all-done = bf16[64,4,4096]{2,1,0:T(4,128)(2,1)} async-done(((bf16[64,4,4096]{2,1,0:T(4,128)(2,1)}), bf16[64,4,4096]{2,1,0:T(4,128)(2,1)}, u32[]{:S(2)}, u32[]{:S(2)}) %all-to-all-start) | async-done | bytes 2097184 | tf_op jit(solution)/shard_map/all_to_all | solution.py:29
  65.8 4.2 %collective-permute-done.k1a_ref = bf16[64,4096]{1,0:T(8,128)(2,1)S(1)} collective-permute-done((bf16[64,4096]{1,0:T(8,128)(2,1)S(1)}, bf16[64,4096]{1,0:T(8,128)(2,1)S(1)}, u32[]{:S(2)}, u32[]{:S(2)}) %collective-permute-start) | collective-permute-done | bytes 524320 | tf_op jit(solution)/shard_map/ppermute | solution.py:22
  69.9 2.4 broadcast_in_dim.18
  72.3 7.9 %all-to-all-start.1 = ((bf16[64,4,4096]{2,1,0:T(4,128)(2,1)}), bf16[64,4,4096]{2,1,0:T(4,128)(2,1)S(1)}, u32[]{:S(2)}, u32[]{:S(2)}) async-start(bf16[64,4,4096]{2,1,0:T(4,128)(2,1)} %broadcast_in_dim.18), calls=%async_computation.1 | async-start | bytes 4194304 | tf_op jit(solution)/shard_map/all_to_all | solution.py:36
  80.2 2.0 collective-permute-start.1
  82.5 47.0 %all-to-all-done.1 = bf16[64,4,4096]{2,1,0:T(4,128)(2,1)S(1)} async-done(((bf16[64,4,4096]{2,1,0:T(4,128)(2,1)}), bf16[64,4,4096]{2,1,0:T(4,128)(2,1)S(1)}, u32[]{:S(2)}, u32[]{:S(2)}) %all-to-all-start.1) | async-done | bytes 2097184 | tf_op jit(solution)/shard_map/all_to_all | solution.py:36
  129.5 2.1 reshape.18.k2_ref.k3_ref
  131.6 3.1 %collective-permute-done.1.k1b_ref = bf16[64,4096]{1,0:T(8,128)(2,1)} collective-permute-done((bf16[64,4096]{1,0:T(8,128)(2,1)}, bf16[64,4096]{1,0:T(8,128)(2,1)}, u32[]{:S(2)}, u32[]{:S(2)}) %collective-permute-start.1) | collective-permute-done | bytes 524320 | tf_op jit(solution)/shard_map/ppermute | solution.py:22
  134.7 1.9 collective-permute-start.2
  137.2 15.5 %shard_map.73 = bf16[128,4096]{1,0:T(8,128)(2,1)} custom-call(s32[5]{0:T(128)} %pad_add_fusion.meta_ref, bf16[128,4096]{1,0:T(8,128)(2,1)} %bitcast.11, bf16[128,4096]{1,0:T(8,128)(2,1)} %bitcast.12, bf16[64,4096]{1,0:T(8,128)(2,1)} %copy-done.4, bf16[64,4096]{1,0:T(8,128)(2,1)} %collective-permute-done.1.k1b_ref, bf16[256,4096]{1,0:T(8,128)(2,1)} %reshape.18.k2_ref.k3_ref, ...), custom_call_target="tpu_custom_call" | custom-call | tf_op jit(solution)/shard_map/pallas_call | solution.py:93
  152.7 1.3 broadcast_select_fusion.1
  154.1 1.5 reshape.19
  155.6 9.6 %all-to-all-start.2 = ((bf16[64,2,4096]{2,1,0:T(2,128)(2,1)}), bf16[64,2,4096]{2,1,0:T(2,128)(2,1)S(1)}, u32[]{:S(2)}, u32[]{:S(2)}) async-start(bf16[64,2,4096]{2,1,0:T(2,128)(2,1)} %reshape.19), calls=%async_computation.2 | async-start | bytes 2097152 | tf_op jit(solution)/shard_map/all_to_all | solution.py:29
  167.1 24.7 %all-to-all-done.2 = bf16[64,2,4096]{2,1,0:T(2,128)(2,1)S(1)} async-done(((bf16[64,2,4096]{2,1,0:T(2,128)(2,1)}), bf16[64,2,4096]{2,1,0:T(2,128)(2,1)S(1)}, u32[]{:S(2)}, u32[]{:S(2)}) %all-to-all-start.2) | async-done | bytes 1048608 | tf_op jit(solution)/shard_map/all_to_all | solution.py:29
  191.8 4.3 %collective-permute-start.3 = (bf16[1,2,4096]{2,1,0:T(2,128)(2,1)S(1)}, bf16[1,2,4096]{2,1,0:T(2,128)(2,1)S(1)}, u32[]{:S(2)}, u32[]{:S(2)}) collective-permute-start(bf16[1,2,4096]{2,1,0:T(2,128)(2,1)S(1)} %constant_dynamic-slice_fusion), channel_id=1, source_target_pairs={{0,64},{64,128},{128,192},{192,256},{256,320},{320,384},{384,448},... | collective-permute-start | bytes 49160 | tf_op jit(solution)/shard_map/ppermute | solution.py:22
  196.1 1.4 collective-permute-done.3
  197.5 4.3 %collective-permute-start.4 = (bf16[128,4096]{1,0:T(8,128)(2,1)S(1)}, bf16[128,4096]{1,0:T(8,128)(2,1)}, u32[]{:S(2)}, u32[]{:S(2)}) collective-permute-start(bf16[128,4096]{1,0:T(8,128)(2,1)S(1)} %copy-done.2), channel_id=1, source_target_pairs={{0,64},{64,128},{128,192},{192,256},{256,320},{320,384},{384,448},... | collective-permute-start | bytes 3145736 | tf_op jit(solution)/shard_map/ppermute | solution.py:151
  201.8 2.0 broadcast_in_dim.20
  203.8 8.1 %all-to-all-start.3 = ((bf16[64,2,4096]{2,1,0:T(2,128)(2,1)}), bf16[64,2,4096]{2,1,0:T(2,128)(2,1)S(1)}, u32[]{:S(2)}, u32[]{:S(2)}) async-start(bf16[64,2,4096]{2,1,0:T(2,128)(2,1)} %broadcast_in_dim.20), calls=%async_computation.3 | async-start | bytes 2097152 | tf_op jit(solution)/shard_map/all_to_all | solution.py:36
  211.9 5.4 %collective-permute-start.5 = (bf16[128,4096]{1,0:T(8,128)(2,1)S(1)}, bf16[128,4096]{1,0:T(8,128)(2,1)}, u32[]{:S(2)}, u32[]{:S(2)}) collective-permute-start(bf16[128,4096]{1,0:T(8,128)(2,1)S(1)} %copy-done.2), channel_id=1, source_target_pairs={{0,65},{1,66},{2,67},{3,68},{4,69},{5,70},{6,71},{7,72},{8,73},{9,... | collective-permute-start | bytes 3145736 | tf_op jit(solution)/shard_map/ppermute | solution.py:157
  217.3 10.6 %collective-permute-done.4 = bf16[128,4096]{1,0:T(8,128)(2,1)} collective-permute-done((bf16[128,4096]{1,0:T(8,128)(2,1)S(1)}, bf16[128,4096]{1,0:T(8,128)(2,1)}, u32[]{:S(2)}, u32[]{:S(2)}) %collective-permute-start.4) | collective-permute-done | bytes 1048608 | tf_op jit(solution)/shard_map/ppermute | solution.py:151
  228.0 2.3 broadcast_select_fusion.3.q_ref.k0_ref
  230.3 22.0 %collective-permute-done.5 = bf16[128,4096]{1,0:T(8,128)(2,1)} collective-permute-done((bf16[128,4096]{1,0:T(8,128)(2,1)S(1)}, bf16[128,4096]{1,0:T(8,128)(2,1)}, u32[]{:S(2)}, u32[]{:S(2)}) %collective-permute-start.5) | collective-permute-done | bytes 1048608 | tf_op jit(solution)/shard_map/ppermute | solution.py:157
  252.3 2.3 broadcast_select_fusion.k1a_ref.k1b_ref
  254.6 1.2 reshape.20.k3_ref
  255.8 15.6 %shard_map.74 = bf16[128,4096]{1,0:T(8,128)(2,1)} custom-call(s32[5]{0:T(128)} %pad_add_fusion.meta_ref, bf16[128,4096]{1,0:T(8,128)(2,1)} %broadcast_select_fusion.3.q_ref.k0_ref, bf16[128,4096]{1,0:T(8,128)(2,1)} %broadcast_select_fusion.3.q_ref.k0_ref, bf16[128,4096]{1,0:T(8,128)(2,1)} %broadcast_select_fusion.k1a_ref.k1b_ref, ...), custom_call_target="tpu_custom_call" | custom-call | tf_op jit(solution)/shard_map/pallas_call | solution.py:93
  (20 shorter events, 2.7 us)
Async XLA Ops:
  0.0 1.6 copy-start
  4.7 11.1 %copy-start.1 = (bf16[128,4096]{1,0:T(8,128)(2,1)S(1)}, bf16[128,4096]{1,0:T(8,128)(2,1)}, u32[]{:S(2)}) copy-start(bf16[128,4096]{1,0:T(8,128)(2,1)} %param.9) | copy-start | bytes 3145732
  4.7 11.2 %copy-start.3 = (bf16[1,128,4096]{2,1,0:T(8,128)(2,1)S(1)}, bf16[1,128,4096]{2,1,0:T(8,128)(2,1)}, u32[]{:S(2)}) copy-start(bf16[1,128,4096]{2,1,0:T(8,128)(2,1)} %param.7) | copy-start | bytes 3145732
  4.7 60.3 %all-to-all-start = ((bf16[64,4,4096]{2,1,0:T(4,128)(2,1)}), bf16[64,4,4096]{2,1,0:T(4,128)(2,1)}, u32[]{:S(2)}, u32[]{:S(2)}) async-start(bf16[64,4,4096]{2,1,0:T(4,128)(2,1)} %pad_maximum_fusion), calls=%async_computation | async-start | bytes 4194304 | tf_op jit(solution)/shard_map/all_to_all | solution.py:29
  17.0 2.9 %copy-start.5 = (s32[64,4]{0,1:T(4,128)S(1)}, s32[64,4]{0,1:T(4,128)}, u32[]{:S(2)}) copy-start(s32[64,4]{0,1:T(4,128)} %param.10) | copy-start | bytes 3076
  17.8 52.1 %collective-permute-start = (bf16[64,4096]{1,0:T(8,128)(2,1)S(1)}, bf16[64,4096]{1,0:T(8,128)(2,1)S(1)}, u32[]{:S(2)}, u32[]{:S(2)}) collective-permute-start(bf16[64,4096]{1,0:T(8,128)(2,1)S(1)} %get-tuple-element.28), channel_id=1, source_target_pairs={{0,1},{1,2},{2,3},{3,4},{4,5},{5,6},{6,7},{7,8},{8,9},{9,10},{10,1... | collective-permute-start | bytes 1572872 | tf_op jit(solution)/shard_map/ppermute | solution.py:22
  69.9 2.4 copy-start.4
  72.3 57.2 %all-to-all-start.1 = ((bf16[64,4,4096]{2,1,0:T(4,128)(2,1)}), bf16[64,4,4096]{2,1,0:T(4,128)(2,1)S(1)}, u32[]{:S(2)}, u32[]{:S(2)}) async-start(bf16[64,4,4096]{2,1,0:T(4,128)(2,1)} %broadcast_in_dim.18), calls=%async_computation.1 | async-start | bytes 4194304 | tf_op jit(solution)/shard_map/all_to_all | solution.py:36
  80.2 54.4 %collective-permute-start.1 = (bf16[64,4096]{1,0:T(8,128)(2,1)}, bf16[64,4096]{1,0:T(8,128)(2,1)}, u32[]{:S(2)}, u32[]{:S(2)}) collective-permute-start(bf16[64,4096]{1,0:T(8,128)(2,1)} %get-tuple-element.27), channel_id=1, source_target_pairs={{0,1},{1,2},{2,3},{3,4},{4,5},{5,6},{6,7},{7,8},{8,9},{9,10},{10,1... | collective-permute-start | bytes 1572872 | tf_op jit(solution)/shard_map/ppermute | solution.py:22
  134.7 19.4 %collective-permute-start.2 = (bf16[128,4096]{1,0:T(8,128)(2,1)}, bf16[128,4096]{1,0:T(8,128)(2,1)}, u32[]{:S(2)}, u32[]{:S(2)}) collective-permute-start(bf16[128,4096]{1,0:T(8,128)(2,1)} %get-tuple-element.20), channel_id=1, source_target_pairs={{0,1},{1,2},{2,3},{3,4},{4,5},{5,6},{6,7},{7,8},{8,9},{9,10},{10,1... | collective-permute-start | bytes 3145736 | tf_op jit(solution)/shard_map/ppermute | solution.py:22
  154.1 43.5 %copy-start.2 = (bf16[128,4096]{1,0:T(8,128)(2,1)S(1)}, bf16[128,4096]{1,0:T(8,128)(2,1)}, u32[]{:S(2)}) copy-start(bf16[128,4096]{1,0:T(8,128)(2,1)} %shard_map.73) | copy-start | bytes 3145732
  155.6 36.2 %all-to-all-start.2 = ((bf16[64,2,4096]{2,1,0:T(2,128)(2,1)}), bf16[64,2,4096]{2,1,0:T(2,128)(2,1)S(1)}, u32[]{:S(2)}, u32[]{:S(2)}) async-start(bf16[64,2,4096]{2,1,0:T(2,128)(2,1)} %reshape.19), calls=%async_computation.2 | async-start | bytes 2097152 | tf_op jit(solution)/shard_map/all_to_all | solution.py:29
  191.8 5.7 %collective-permute-start.3 = (bf16[1,2,4096]{2,1,0:T(2,128)(2,1)S(1)}, bf16[1,2,4096]{2,1,0:T(2,128)(2,1)S(1)}, u32[]{:S(2)}, u32[]{:S(2)}) collective-permute-start(bf16[1,2,4096]{2,1,0:T(2,128)(2,1)S(1)} %constant_dynamic-slice_fusion), channel_id=1, source_target_pairs={{0,64},{64,128},{128,192},{192,256},{256,320},{320,384},{384,448},... | collective-permute-start | bytes 49160 | tf_op jit(solution)/shard_map/ppermute | solution.py:22
  197.5 30.4 %collective-permute-start.4 = (bf16[128,4096]{1,0:T(8,128)(2,1)S(1)}, bf16[128,4096]{1,0:T(8,128)(2,1)}, u32[]{:S(2)}, u32[]{:S(2)}) collective-permute-start(bf16[128,4096]{1,0:T(8,128)(2,1)S(1)} %copy-done.2), channel_id=1, source_target_pairs={{0,64},{64,128},{128,192},{192,256},{256,320},{320,384},{384,448},... | collective-permute-start | bytes 3145736 | tf_op jit(solution)/shard_map/ppermute | solution.py:151
  203.8 50.8 %all-to-all-start.3 = ((bf16[64,2,4096]{2,1,0:T(2,128)(2,1)}), bf16[64,2,4096]{2,1,0:T(2,128)(2,1)S(1)}, u32[]{:S(2)}, u32[]{:S(2)}) async-start(bf16[64,2,4096]{2,1,0:T(2,128)(2,1)} %broadcast_in_dim.20), calls=%async_computation.3 | async-start | bytes 2097152 | tf_op jit(solution)/shard_map/all_to_all | solution.py:36
  211.9 40.4 %collective-permute-start.5 = (bf16[128,4096]{1,0:T(8,128)(2,1)S(1)}, bf16[128,4096]{1,0:T(8,128)(2,1)}, u32[]{:S(2)}, u32[]{:S(2)}) collective-permute-start(bf16[128,4096]{1,0:T(8,128)(2,1)S(1)} %copy-done.2), channel_id=1, source_target_pairs={{0,65},{1,66},{2,67},{3,68},{4,69},{5,70},{6,71},{7,72},{8,73},{9,... | collective-permute-start | bytes 3145736 | tf_op jit(solution)/shard_map/ppermute | solution.py:157

commit v11 on v9

--- a/solution.py
+++ b/solution.py
@@ -13,7 +13,7 @@
 NR = 1
 WIDTH = 4096
 NSEL = 4
-GROUP = 16
+GROUP = 8
 
 
 def shifted(value, axis, steps):

time: 272 us -> 272 us (level)
  no operation moved by 1% of the time
where the time goes in v11:
time: 272 us; the launch traced here: 271 us
  waiting for transfers between devices  156 us (57%)
  starting transfers between devices  56.8 us (21%)
  Pallas kernels  31.6 us (12%)
  local copies, waits for them, and re-layouts  13.8 us (5%)
  other arithmetic  9.42 us (3%)
  between operations  3.74 us (1%)
    all_to_all x2, waiting for transfers between devices, scatter_piece(): received = lax.all_to_all(pieces, axis, 0, 0, tiled=True)  67.5 us
    all_to_all x2, waiting for transfers between devices, gather_pieces(): lax.all_to_all(jnp.broadcast_to(piece, shape), axis, 0, 0, tiled=True)  47.1 us
    pallas_call x2, Pallas kernels, attend_pallas(): pl.pallas_call(attend_kernel, grid_spec=grid_spec, out_shape=jax.ShapeDty...  31.6 us
    ppermute x1, waiting for transfers between devices, local(): received_previous = lax.ppermute(outgoing, ('section', 'ctx'), diagonal)  22 us
    all_to_all x2, starting transfers between devices, scatter_piece(): received = lax.all_to_all(pieces, axis, 0, 0, tiled=True)  20.9 us
    all_to_all x2, starting transfers between devices, gather_pieces(): lax.all_to_all(jnp.broadcast_to(piece, shape), axis, 0, 0, tiled=True)  16 us
    ppermute x1, waiting for transfers between devices, local(): received = lax.ppermute(outgoing, 'section', straight)  10.6 us
    ppermute x4, starting transfers between devices, shifted(): return lax.ppermute(value, axis, pairs)  10.2 us
  transfers between devices with their start and end apart: 10, of which 8 were waited for; matrix products, arithmetic and copies ran while one was open for 5% of the time, Pallas kernels for 6%

profile of v11, /device:TPU:70, one launch (start us, length us, event | category | flops | bytes accessed | tf_op | source)
XLA Modules:
  0.0 271.3 jit_solution(14783978263503609472)
XLA Ops:
  0.0 1.7 pad_maximum_fusion
  1.7 2.2 reshape.21
  3.9 11.3 %all-to-all-start = ((bf16[64,4,4096]{2,1,0:T(4,128)(2,1)}), bf16[64,4,4096]{2,1,0:T(4,128)(2,1)}, u32[]{:S(2)}, u32[]{:S(2)}) async-start(bf16[64,4,4096]{2,1,0:T(4,128)(2,1)} %reshape.21), calls=%async_computation | async-start | bytes 4194304 | tf_op jit(solution)/shard_map/all_to_all | solution.py:29
  15.2 1.1 broadcast_select_fusion.2
  16.3 0.9 fusion
  17.2 2.0 collective-permute-start
  21.5 42.8 %all-to-all-done = bf16[64,4,4096]{2,1,0:T(4,128)(2,1)} async-done(((bf16[64,4,4096]{2,1,0:T(4,128)(2,1)}), bf16[64,4,4096]{2,1,0:T(4,128)(2,1)}, u32[]{:S(2)}, u32[]{:S(2)}) %all-to-all-start) | async-done | bytes 2097184 | tf_op jit(solution)/shard_map/all_to_all | solution.py:29
  65.1 4.2 %collective-permute-done.k1a_ref = bf16[64,4096]{1,0:T(8,128)(2,1)S(1)} collective-permute-done((bf16[64,4096]{1,0:T(8,128)(2,1)S(1)}, bf16[64,4096]{1,0:T(8,128)(2,1)S(1)}, u32[]{:S(2)}, u32[]{:S(2)}) %collective-permute-start) | collective-permute-done | bytes 524320 | tf_op jit(solution)/shard_map/ppermute | solution.py:22
  69.3 2.4 broadcast_in_dim.18
  71.6 7.9 %all-to-all-start.1 = ((bf16[64,4,4096]{2,1,0:T(4,128)(2,1)}), bf16[64,4,4096]{2,1,0:T(4,128)(2,1)S(1)}, u32[]{:S(2)}, u32[]{:S(2)}) async-start(bf16[64,4,4096]{2,1,0:T(4,128)(2,1)} %broadcast_in_dim.18), calls=%async_computation.1 | async-start | bytes 4194304 | tf_op jit(solution)/shard_map/all_to_all | solution.py:36
  79.6 2.0 collective-permute-start.1
  81.8 47.0 %all-to-all-done.1 = bf16[64,4,4096]{2,1,0:T(4,128)(2,1)S(1)} async-done(((bf16[64,4,4096]{2,1,0:T(4,128)(2,1)}), bf16[64,4,4096]{2,1,0:T(4,128)(2,1)S(1)}, u32[]{:S(2)}, u32[]{:S(2)}) %all-to-all-start.1) | async-done | bytes 2097184 | tf_op jit(solution)/shard_map/all_to_all | solution.py:36
  128.9 2.1 reshape.22.k2_ref.k3_ref
  130.9 3.1 %collective-permute-done.1.k1b_ref = bf16[64,4096]{1,0:T(8,128)(2,1)} collective-permute-done((bf16[64,4096]{1,0:T(8,128)(2,1)}, bf16[64,4096]{1,0:T(8,128)(2,1)}, u32[]{:S(2)}, u32[]{:S(2)}) %collective-permute-start.1) | collective-permute-done | bytes 524320 | tf_op jit(solution)/shard_map/ppermute | solution.py:22
  134.0 1.9 collective-permute-start.2
  136.6 15.8 %shard_map.73 = bf16[128,4096]{1,0:T(8,128)(2,1)} custom-call(s32[5]{0:T(128)} %pad_add_fusion.meta_ref, bf16[128,4096]{1,0:T(8,128)(2,1)} %bitcast.12, bf16[128,4096]{1,0:T(8,128)(2,1)} %bitcast.13, bf16[64,4096]{1,0:T(8,128)(2,1)} %copy-done.4, bf16[64,4096]{1,0:T(8,128)(2,1)} %collective-permute-done.1.k1b_ref, bf16[256,4096]{1,0:T(8,128)(2,1)} %reshape.22.k2_ref.k3_ref, ...), custom_call_target="tpu_custom_call" | custom-call | tf_op jit(solution)/shard_map/pallas_call | solution.py:100
  152.4 1.3 broadcast_select_fusion.1
  153.7 1.5 reshape.23
  155.2 9.6 %all-to-all-start.2 = ((bf16[64,2,4096]{2,1,0:T(2,128)(2,1)}), bf16[64,2,4096]{2,1,0:T(2,128)(2,1)S(1)}, u32[]{:S(2)}, u32[]{:S(2)}) async-start(bf16[64,2,4096]{2,1,0:T(2,128)(2,1)} %reshape.23), calls=%async_computation.2 | async-start | bytes 2097152 | tf_op jit(solution)/shard_map/all_to_all | solution.py:29
  166.7 24.7 %all-to-all-done.2 = bf16[64,2,4096]{2,1,0:T(2,128)(2,1)S(1)} async-done(((bf16[64,2,4096]{2,1,0:T(2,128)(2,1)}), bf16[64,2,4096]{2,1,0:T(2,128)(2,1)S(1)}, u32[]{:S(2)}, u32[]{:S(2)}) %all-to-all-start.2) | async-done | bytes 1048608 | tf_op jit(solution)/shard_map/all_to_all | solution.py:29
  191.5 4.3 %collective-permute-start.3 = (bf16[1,2,4096]{2,1,0:T(2,128)(2,1)S(1)}, bf16[1,2,4096]{2,1,0:T(2,128)(2,1)S(1)}, u32[]{:S(2)}, u32[]{:S(2)}) collective-permute-start(bf16[1,2,4096]{2,1,0:T(2,128)(2,1)S(1)} %constant_dynamic-slice_fusion), channel_id=1, source_target_pairs={{0,64},{64,128},{128,192},{192,256},{256,320},{320,384},{384,448},... | collective-permute-start | bytes 49160 | tf_op jit(solution)/shard_map/ppermute | solution.py:22
  195.8 1.4 collective-permute-done.3
  197.2 4.2 %collective-permute-start.4 = (bf16[128,4096]{1,0:T(8,128)(2,1)S(1)}, bf16[128,4096]{1,0:T(8,128)(2,1)}, u32[]{:S(2)}, u32[]{:S(2)}) collective-permute-start(bf16[128,4096]{1,0:T(8,128)(2,1)S(1)} %copy-done.2), channel_id=1, source_target_pairs={{0,64},{64,128},{128,192},{192,256},{256,320},{320,384},{384,448},... | collective-permute-start | bytes 3145736 | tf_op jit(solution)/shard_map/ppermute | solution.py:158
  201.4 2.0 broadcast_in_dim.20
  203.4 8.1 %all-to-all-start.3 = ((bf16[64,2,4096]{2,1,0:T(2,128)(2,1)}), bf16[64,2,4096]{2,1,0:T(2,128)(2,1)S(1)}, u32[]{:S(2)}, u32[]{:S(2)}) async-start(bf16[64,2,4096]{2,1,0:T(2,128)(2,1)} %broadcast_in_dim.20), calls=%async_computation.3 | async-start | bytes 2097152 | tf_op jit(solution)/shard_map/all_to_all | solution.py:36
  211.5 5.4 %collective-permute-start.5 = (bf16[128,4096]{1,0:T(8,128)(2,1)S(1)}, bf16[128,4096]{1,0:T(8,128)(2,1)}, u32[]{:S(2)}, u32[]{:S(2)}) collective-permute-start(bf16[128,4096]{1,0:T(8,128)(2,1)S(1)} %copy-done.2), channel_id=1, source_target_pairs={{0,65},{1,66},{2,67},{3,68},{4,69},{5,70},{6,71},{7,72},{8,73},{9,... | collective-permute-start | bytes 3145736 | tf_op jit(solution)/shard_map/ppermute | solution.py:164
  217.0 10.6 %collective-permute-done.4 = bf16[128,4096]{1,0:T(8,128)(2,1)} collective-permute-done((bf16[128,4096]{1,0:T(8,128)(2,1)S(1)}, bf16[128,4096]{1,0:T(8,128)(2,1)}, u32[]{:S(2)}, u32[]{:S(2)}) %collective-permute-start.4) | collective-permute-done | bytes 1048608 | tf_op jit(solution)/shard_map/ppermute | solution.py:158
  227.6 2.3 broadcast_select_fusion.4.q_ref.k0_ref
  229.9 22.0 %collective-permute-done.5 = bf16[128,4096]{1,0:T(8,128)(2,1)} collective-permute-done((bf16[128,4096]{1,0:T(8,128)(2,1)S(1)}, bf16[128,4096]{1,0:T(8,128)(2,1)}, u32[]{:S(2)}, u32[]{:S(2)}) %collective-permute-start.5) | collective-permute-done | bytes 1048608 | tf_op jit(solution)/shard_map/ppermute | solution.py:164
  251.9 2.3 broadcast_select_fusion.k1a_ref.k1b_ref
  254.3 1.2 reshape.24.k3_ref
  255.5 15.8 %shard_map.74 = bf16[128,4096]{1,0:T(8,128)(2,1)} custom-call(s32[5]{0:T(128)} %pad_add_fusion.meta_ref, bf16[128,4096]{1,0:T(8,128)(2,1)} %broadcast_select_fusion.4.q_ref.k0_ref, bf16[128,4096]{1,0:T(8,128)(2,1)} %broadcast_select_fusion.4.q_ref.k0_ref, bf16[128,4096]{1,0:T(8,128)(2,1)} %broadcast_select_fusion.k1a_ref.k1b_ref, ...), custom_call_target="tpu_custom_call" | custom-call | tf_op jit(solution)/shard_map/pallas_call | solution.py:100
  (19 shorter events, 2.2 us)
Async XLA Ops:
  3.9 11.3 %copy-start = (bf16[1,128,4096]{2,1,0:T(8,128)(2,1)S(1)}, bf16[1,128,4096]{2,1,0:T(8,128)(2,1)}, u32[]{:S(2)}) copy-start(bf16[1,128,4096]{2,1,0:T(8,128)(2,1)} %param.8) | copy-start | bytes 3145732
  3.9 11.3 %copy-start.1 = (bf16[128,4096]{1,0:T(8,128)(2,1)S(1)}, bf16[128,4096]{1,0:T(8,128)(2,1)}, u32[]{:S(2)}) copy-start(bf16[128,4096]{1,0:T(8,128)(2,1)} %param.9) | copy-start | bytes 3145732
  3.9 11.3 %copy-start.3 = (bf16[1,128,4096]{2,1,0:T(8,128)(2,1)S(1)}, bf16[1,128,4096]{2,1,0:T(8,128)(2,1)}, u32[]{:S(2)}) copy-start(bf16[1,128,4096]{2,1,0:T(8,128)(2,1)} %param.7) | copy-start | bytes 3145732
  3.9 60.5 %all-to-all-start = ((bf16[64,4,4096]{2,1,0:T(4,128)(2,1)}), bf16[64,4,4096]{2,1,0:T(4,128)(2,1)}, u32[]{:S(2)}, u32[]{:S(2)}) async-start(bf16[64,4,4096]{2,1,0:T(4,128)(2,1)} %reshape.21), calls=%async_computation | async-start | bytes 4194304 | tf_op jit(solution)/shard_map/all_to_all | solution.py:29
  16.3 2.9 %copy-start.5 = (s32[64,4]{0,1:T(4,128)S(1)}, s32[64,4]{0,1:T(4,128)}, u32[]{:S(2)}) copy-start(s32[64,4]{0,1:T(4,128)} %param.10) | copy-start | bytes 3076
  17.2 52.1 %collective-permute-start = (bf16[64,4096]{1,0:T(8,128)(2,1)S(1)}, bf16[64,4096]{1,0:T(8,128)(2,1)S(1)}, u32[]{:S(2)}, u32[]{:S(2)}) collective-permute-start(bf16[64,4096]{1,0:T(8,128)(2,1)S(1)} %get-tuple-element.28), channel_id=1, source_target_pairs={{0,1},{1,2},{2,3},{3,4},{4,5},{5,6},{6,7},{7,8},{8,9},{9,10},{10,1... | collective-permute-start | bytes 1572872 | tf_op jit(solution)/shard_map/ppermute | solution.py:22
  69.3 2.4 copy-start.4
  71.6 57.2 %all-to-all-start.1 = ((bf16[64,4,4096]{2,1,0:T(4,128)(2,1)}), bf16[64,4,4096]{2,1,0:T(4,128)(2,1)S(1)}, u32[]{:S(2)}, u32[]{:S(2)}) async-start(bf16[64,4,4096]{2,1,0:T(4,128)(2,1)} %broadcast_in_dim.18), calls=%async_computation.1 | async-start | bytes 4194304 | tf_op jit(solution)/shard_map/all_to_all | solution.py:36
  79.6 54.4 %collective-permute-start.1 = (bf16[64,4096]{1,0:T(8,128)(2,1)}, bf16[64,4096]{1,0:T(8,128)(2,1)}, u32[]{:S(2)}, u32[]{:S(2)}) collective-permute-start(bf16[64,4096]{1,0:T(8,128)(2,1)} %get-tuple-element.27), channel_id=1, source_target_pairs={{0,1},{1,2},{2,3},{3,4},{4,5},{5,6},{6,7},{7,8},{8,9},{9,10},{10,1... | collective-permute-start | bytes 1572872 | tf_op jit(solution)/shard_map/ppermute | solution.py:22
  134.0 19.7 %collective-permute-start.2 = (bf16[128,4096]{1,0:T(8,128)(2,1)}, bf16[128,4096]{1,0:T(8,128)(2,1)}, u32[]{:S(2)}, u32[]{:S(2)}) collective-permute-start(bf16[128,4096]{1,0:T(8,128)(2,1)} %get-tuple-element.20), channel_id=1, source_target_pairs={{0,1},{1,2},{2,3},{3,4},{4,5},{5,6},{6,7},{7,8},{8,9},{9,10},{10,1... | collective-permute-start | bytes 3145736 | tf_op jit(solution)/shard_map/ppermute | solution.py:22
  153.7 43.5 %copy-start.2 = (bf16[128,4096]{1,0:T(8,128)(2,1)S(1)}, bf16[128,4096]{1,0:T(8,128)(2,1)}, u32[]{:S(2)}) copy-start(bf16[128,4096]{1,0:T(8,128)(2,1)} %shard_map.73) | copy-start | bytes 3145732
  155.2 36.3 %all-to-all-start.2 = ((bf16[64,2,4096]{2,1,0:T(2,128)(2,1)}), bf16[64,2,4096]{2,1,0:T(2,128)(2,1)S(1)}, u32[]{:S(2)}, u32[]{:S(2)}) async-start(bf16[64,2,4096]{2,1,0:T(2,128)(2,1)} %reshape.23), calls=%async_computation.2 | async-start | bytes 2097152 | tf_op jit(solution)/shard_map/all_to_all | solution.py:29
  191.5 5.7 %collective-permute-start.3 = (bf16[1,2,4096]{2,1,0:T(2,128)(2,1)S(1)}, bf16[1,2,4096]{2,1,0:T(2,128)(2,1)S(1)}, u32[]{:S(2)}, u32[]{:S(2)}) collective-permute-start(bf16[1,2,4096]{2,1,0:T(2,128)(2,1)S(1)} %constant_dynamic-slice_fusion), channel_id=1, source_target_pairs={{0,64},{64,128},{128,192},{192,256},{256,320},{320,384},{384,448},... | collective-permute-start | bytes 49160 | tf_op jit(solution)/shard_map/ppermute | solution.py:22
  197.2 30.4 %collective-permute-start.4 = (bf16[128,4096]{1,0:T(8,128)(2,1)S(1)}, bf16[128,4096]{1,0:T(8,128)(2,1)}, u32[]{:S(2)}, u32[]{:S(2)}) collective-permute-start(bf16[128,4096]{1,0:T(8,128)(2,1)S(1)} %copy-done.2), channel_id=1, source_target_pairs={{0,64},{64,128},{128,192},{192,256},{256,320},{320,384},{384,448},... | collective-permute-start | bytes 3145736 | tf_op jit(solution)/shard_map/ppermute | solution.py:158
  203.4 50.8 %all-to-all-start.3 = ((bf16[64,2,4096]{2,1,0:T(2,128)(2,1)}), bf16[64,2,4096]{2,1,0:T(2,128)(2,1)S(1)}, u32[]{:S(2)}, u32[]{:S(2)}) async-start(bf16[64,2,4096]{2,1,0:T(2,128)(2,1)} %broadcast_in_dim.20), calls=%async_computation.3 | async-start | bytes 2097152 | tf_op jit(solution)/shard_map/all_to_all | solution.py:36
  211.5 40.4 %collective-permute-start.5 = (bf16[128,4096]{1,0:T(8,128)(2,1)S(1)}, bf16[128,4096]{1,0:T(8,128)(2,1)}, u32[]{:S(2)}, u32[]{:S(2)}) collective-permute-start(bf16[128,4096]{1,0:T(8,128)(2,1)S(1)} %copy-done.2), channel_id=1, source_target_pairs={{0,65},{1,66},{2,67},{3,68},{4,69},{5,70},{6,71},{7,72},{8,73},{9,... | collective-permute-start | bytes 3145736 | tf_op jit(solution)/shard_map/ppermute | solution.py:164
